TPU v7x, 32 devices: a whole 2x2x4 slice. The times are simulated.
32 devices in a mesh: grp: 4 (over y, core), shard: 8 (over z, x).
Axes of the slice: x: 2, y: 2, z: 4, core: 2. Of those that a mesh axis runs over, the one named last changes fastest.
Arguments:
- query_rows: bfloat16 [16, 6144], P('grp'), may hold values from -10 to 10
- key_cache: bfloat16 [16, 2048, 1024], P('grp', 'shard'), may hold values from -10 to 10
- value_cache: bfloat16 [16, 2048, 1024], P('grp', 'shard'), may hold values from -6 to 6
- lengths: int32 [16], P('grp'), may hold values from 2 to 2048
- attn_gain: float32 [6144], replicated, may hold values from 0.5 to 1.5
- router: bfloat16 [6144, 4], replicated, may hold values from -0.078125 to 0.078125
- expert_ids: int32 [16, 2], replicated, may hold values from 0 to 3, all different within a row; in each aligned block of 4 rows (0 to 3, 4 to 7, ...) at most 2 rows name the same one
- w_gate: bfloat16 [4, 6144, 8192], P('grp', None, 'shard'), may hold values from -0.078125 to 0.078125
- w_up: bfloat16 [4, 6144, 8192], P('grp', None, 'shard'), may hold values from -0.078125 to 0.078125
- w_down: bfloat16 [4, 8192, 6144], P('grp', 'shard'), may hold values from -0.0625 to 0.0625
Outputs:
- normed: bfloat16 [16, 6144], P('grp')
- expert_out: bfloat16 [16, 6144], P('grp', 'shard')
Inputs may be any that keep to these rules, and one draw needn't show every extreme that they name: `expert_ids`: the two ids of a row differ. Among the 4 rows of one index of grp (aligned blocks), no expert is named by more than 2 rows, a bound that some block reaches.
All inputs are finite; a program needn't handle non-finite values.
Results may differ from a plain program's by a relative error of at most 0.0095.
Values may be sent and summed in bfloat16 or wider, within the bound.
No kernel may reach another device: no remote copies, remote signals or barrier semaphores. Data moves between devices by JAX's collectives and lax.ppermute only.
A program may use at most 128 MiB of HBM per device.

v0:
```python
import math

import jax
import jax.numpy as jnp
from jax import lax
from jax.sharding import PartitionSpec as P

HEADS = 48
KV_HEADS = 8
HEAD_DIM = 128


NEG_FILL = -1e30


def combined_all(value, axis, join):
    pieces = jax.tree.map(lambda part: lax.all_gather(part, axis), value)
    head = jax.tree.map(lambda part: part[0], pieces)
    tail = jax.tree.map(lambda part: part[1:], pieces)
    total, _ = lax.scan(lambda total, share: (join(total, share), None), head, tail)
    return total


def merge_parts(earlier, second):
    joint_max = jnp.maximum(earlier[0], second[0])
    left_scale = jnp.exp(earlier[0] - joint_max)
    right_scale = jnp.exp(second[0] - joint_max)
    joint_sum = earlier[1] * left_scale + second[1] * right_scale
    joint_mix = earlier[2] * left_scale[..., None] + second[2] * right_scale[..., None]
    return (joint_max, joint_sum, joint_mix)


def shards(
    query_rows, key_cache, value_cache, lengths, attn_gain, router, expert_ids, w_gate, w_up, w_down
):
    rows_here = query_rows.shape[0]
    span = key_cache.shape[1]
    kv_share = HEADS // KV_HEADS
    shard_id = lax.axis_index("shard")
    query_heads = query_rows.reshape(rows_here, KV_HEADS, kv_share, HEAD_DIM)
    key_heads = key_cache.reshape(rows_here, span, KV_HEADS, HEAD_DIM)
    value_heads = value_cache.reshape(rows_here, span, KV_HEADS, HEAD_DIM)
    scores = jnp.einsum(
        "rgjd,rtgd->rgjt", query_heads, key_heads, preferred_element_type=jnp.float32
    ) / math.sqrt(HEAD_DIM)
    position = shard_id * span + jnp.arange(span, dtype=jnp.int32)
    live_mask = (position[None, :] < lengths[:, None])[:, None, None, :]
    scores = jnp.where(live_mask, scores, NEG_FILL)
    block_max = jnp.max(scores, axis=-1)
    block_probs = jnp.where(live_mask, jnp.exp(scores - block_max[..., None]), 0.0).astype(
        jnp.bfloat16
    )
    block_sum = jnp.sum(block_probs.astype(jnp.float32), axis=-1)
    block_mix = jnp.einsum(
        "rgjt,rtgd->rgjd", block_probs, value_heads, preferred_element_type=jnp.float32
    )
    whole_max, whole_sum, whole_mix = combined_all(
        (block_max, block_sum, block_mix), "shard", merge_parts
    )
    attended = (whole_mix / whole_sum[..., None]).reshape(rows_here, -1)
    mean_square = jnp.mean(attended * attended, axis=-1, keepdims=True)
    normed = (attended * lax.rsqrt(mean_square + 1e-05) * attn_gain).astype(jnp.bfloat16)
    experts = router.shape[1]
    capacity = rows_here // 2
    width = normed.shape[1]
    logits = jnp.dot(normed, router, preferred_element_type=jnp.float32)
    own_ids = lax.dynamic_slice_in_dim(expert_ids, lax.axis_index("grp") * rows_here, rows_here, 0)
    expert_range = jnp.arange(experts, dtype=jnp.int32)
    expert_hit = own_ids[:, :, None] == expert_range[None, None, :]
    chosen = jnp.sum(jnp.where(expert_hit, logits[:, None, :], 0.0), axis=-1)
    first_weight = jax.nn.sigmoid(chosen[:, 0] - chosen[:, 1])
    route_weight = jnp.stack([first_weight, 1.0 - first_weight], axis=1)
    row_range = jnp.arange(rows_here, dtype=jnp.int32)
    strictly_lower = (row_range[:, None] > row_range[None, :]).astype(jnp.float32)
    counts = jnp.sum(expert_hit, axis=1).astype(jnp.float32)
    before = jnp.dot(
        strictly_lower, counts, precision=lax.Precision.HIGHEST, preferred_element_type=jnp.float32
    )
    slot_index = jnp.sum(jnp.where(expert_hit, before[:, None, :], 0.0), axis=-1)
    slot_base = jnp.sum(
        jnp.where(expert_hit, (expert_range * capacity).astype(jnp.float32)[None, None, :], 0.0),
        axis=-1,
    )
    destination = slot_base + slot_index
    slot_columns = jnp.arange(experts * capacity, dtype=jnp.int32).astype(jnp.float32)
    placed = (destination[:, :, None] == slot_columns[None, None, :]).astype(jnp.float32)
    send_matrix = jnp.sum(placed, axis=1)
    combine_matrix = jnp.sum(placed * route_weight[:, :, None], axis=1)
    gate_local = w_gate[0]
    up_local = w_up[0]
    down_local = w_down[0]
    outgoing = jnp.einsum(
        "rc,rd->cd", send_matrix.astype(jnp.bfloat16), normed, preferred_element_type=jnp.float32
    )
    outgoing = outgoing.astype(jnp.bfloat16).reshape(experts, capacity, width)
    arrived = lax.all_to_all(outgoing, "grp", split_axis=0, concat_axis=0, tiled=True)
    gate_proj = jnp.einsum("gcd,df->gcf", arrived, gate_local, preferred_element_type=jnp.float32)
    up_proj = jnp.einsum("gcd,df->gcf", arrived, up_local, preferred_element_type=jnp.float32)
    hidden = (jax.nn.silu(gate_proj) * up_proj).astype(jnp.bfloat16)
    partial_value = jnp.einsum(
        "gcf,fd->gcd", hidden, down_local, preferred_element_type=jnp.float32
    )
    summed = lax.psum(partial_value, "shard")
    returned = lax.all_to_all(summed, "grp", split_axis=0, concat_axis=0, tiled=True)
    full_rows = jnp.dot(
        combine_matrix,
        returned.reshape(experts * capacity, width),
        precision=lax.Precision.HIGHEST,
        preferred_element_type=jnp.float32,
    )
    out_width = width // lax.axis_size("shard")
    result = lax.dynamic_slice_in_dim(full_rows, shard_id * out_width, out_width, 1)
    return (normed, result.astype(jnp.bfloat16))


def solution(mesh):
    in_specs = (
        P("grp", None),
        P("grp", "shard", None),
        P("grp", "shard", None),
        P("grp"),
        P(),
        P(),
        P(),
        P("grp", None, "shard"),
        P("grp", None, "shard"),
        P("grp", "shard", None),
    )
    out_specs = (P("grp", None), P("grp", "shard"))
    return jax.shard_map(shards, mesh=mesh, in_specs=in_specs, out_specs=out_specs, check_vma=False)
```

profile of v0, /device:TPU:0, one launch (start us, length us, event | category | flops | bytes accessed | tf_op | source)
XLA Modules:
  0.0 222.4 jit_solution(8904298598831475986)
XLA Ops:
  7.3 1.0 reshape.80
  8.3 0.9 broadcast_compare_fusion
  9.2 0.7 fusion.36
  9.9 32.4 %all-gather = f32[32,8,6]{2,1,0:T(8,128)S(1)} all-gather(f32[4,8,6]{2,1,0:T(8,128)S(1)} %get-tuple-element.90), channel_id=2, replica_groups=mesh['grp'=4,'shard'=8] {'shard'}, dimensions={0}, use_global_device_ids=true | all-gather | bytes 6912 | tf_op jit(solution)/shard_map/all_gather | solution.py:17
  42.3 0.2 convert_reduce_fusion
  42.5 30.5 %all-gather.1 = f32[32,8,6]{2,1,0:T(8,128)S(1)} all-gather(f32[4,8,6]{2,1,0:T(8,128)S(1)} %convert_reduce_fusion), channel_id=3, replica_groups=mesh['grp'=4,'shard'=8] {'shard'}, dimensions={0}, use_global_device_ids=true | all-gather | bytes 6912 | tf_op jit(solution)/shard_map/all_gather | solution.py:17
  73.1 0.4 fusion.10
  73.5 31.6 %all-gather.2 = f32[32,8,6,128]{3,1,2,0:T(8,128)S(1)} all-gather(f32[4,8,6,128]{3,1,2,0:T(8,128)S(1)} %copy.53), channel_id=4, replica_groups=mesh['grp'=4,'shard'=8] {'shard'}, dimensions={0}, use_global_device_ids=true | all-gather | bytes 884736 | tf_op jit(solution)/shard_map/all_gather | solution.py:17
  105.4 0.1 fusion.31
  105.6 0.2 copy.59
  105.8 0.1 copy.57
  105.9 0.2 copy.60
  106.3 3.0 %while.14 = (s32[]{:T(128)}, f32[4,8,6]{1,0,2:T(4,128)S(1)}, f32[4,8,6]{1,0,2:T(4,128)S(1)}, f32[4,8,6,128]{3,2,1,0:T(8,128)S(1)}, f32[7,4,8,6]{2,1,3,0:T(4,128)...) while((s32[]{:T(128)}, f32[4,8,6]{1,0,2:T(4,128)S(1)}, ...), condition=%wide.region_3.4_spmd, body=%wide.region_2.3_spmd.sunk | while | flops 74882 | bytes 502373 | solution.py:20
  106.3 0.1 copy.97
  106.4 0.1 copy.98
  106.5 0.2 fusion.53
  106.7 0.1 copy.97
  106.8 0.1 copy.98
  107.0 0.2 fusion.53
  107.2 0.1 copy.97
  107.3 0.1 copy.98
  107.4 0.2 fusion.53
  107.6 0.1 copy.97
  107.7 0.1 copy.98
  107.8 0.2 fusion.53
  108.0 0.1 copy.97
  108.1 0.1 copy.98
  108.2 0.2 fusion.53
  108.4 0.1 copy.97
  108.6 0.2 fusion.53
  108.9 0.1 copy.97
  109.1 0.2 fusion.53
  109.2 0.1 copy.62
  109.3 0.2 multiply_reduce_fusion
  109.7 0.2 fusion.37
  109.9 0.2 select_reduce_fusion.1
  110.2 0.2 convolution_convert_fusion
  110.5 6.9 %all_to_all.10 = bf16[4,2,6144]{2,1,0:T(2,128)(2,1)S(1)} all-to-all(bf16[4,2,6144]{2,1,0:T(2,128)(2,1)S(1)} %reshape.84), channel_id=1, replica_groups=mesh['grp'=4,'shard'=8] {'grp'}, dimensions={0} | all-to-all | bytes 196608 | tf_op jit(solution)/shard_map/all_to_all | solution.py:96
  117.4 6.8 %fusion.8 = f32[4,2,1024]{2,1,0:T(2,128)S(1)} fusion(bf16[4,2,6144]{2,1,0:T(2,128)(2,1)S(1)} %all_to_all.10, bf16[1,6144,1024]{2,1,0:T(8,128)(2,1)} %param.19), kind=kOutput, calls=%fused_computation.14 | convolution fusion | flops 100663296 | bytes 12713984 | tf_op jit(solution)/shard_map/gcd,df->gcf/dot_general | solution.py:97
  124.2 6.7 %fusion.25 = bf16[4,2,1024]{2,1,0:T(2,128)(2,1)S(1)} fusion(bf16[4,2,6144]{2,1,0:T(2,128)(2,1)S(1)} %all_to_all.10, bf16[1,6144,1024]{2,1,0:T(8,128)(2,1)} %param.20, f32[4,2,1024]{2,1,0:T(2,128)S(1)} %fusion.8), kind=kOutput, calls=%fused_computation.26 | convolution fusion | flops 100712448 | bytes 12730368 | tf_op jit(solution)/shard_map/gcd,df->gcf/dot_general | solution.py:98
  130.9 2.5 %fusion.4 = f32[4,2,6144]{2,0,1:T(4,128)} fusion(bf16[1,1024,6144]{2,1,0:T(8,128)(2,1)S(1)} %bitcast.70, bf16[4,2,1024]{2,1,0:T(2,128)(2,1)S(1)} %fusion.25), kind=kOutput, calls=%fused_computation.10 | convolution fusion | flops 100663296 | bytes 12795904 | tf_op jit(solution)/shard_map/gcf,fd->gcd/dot_general | solution.py:100
  133.5 70.6 %all-reduce.2.cloned.1.call-done = f32[4,2,6144]{2,0,1:T(4,128)} async-done(((f32[4,2,6144]{2,0,1:T(4,128)}), f32[4,2,6144]{2,0,1:T(4,128)}) %all-reduce.2.cloned.1.call-update) | async-done | bytes 196624 | tf_op jit(solution)/shard_map/psum | solution.py:103
  204.1 1.8 copy.64
  205.8 3.4 %all-to-all-start.1 = ((f32[4,2,6144]{2,1,0:T(2,128)}), f32[4,2,6144]{2,1,0:T(2,128)S(1)}, u32[]{:S(2)}, u32[]{:S(2)}) async-start(f32[4,2,6144]{2,1,0:T(2,128)} %copy.64), calls=%async_computation.1 | async-start | bytes 393216 | tf_op jit(solution)/shard_map/all_to_all | solution.py:104
  209.2 5.3 %all-to-all-done.1 = f32[4,2,6144]{2,1,0:T(2,128)S(1)} async-done(((f32[4,2,6144]{2,1,0:T(2,128)}), f32[4,2,6144]{2,1,0:T(2,128)S(1)}, u32[]{:S(2)}, u32[]{:S(2)}) %all-to-all-start.1) | async-done | bytes 196640 | tf_op jit(solution)/shard_map/all_to_all | solution.py:104
  214.5 0.1 reshape.85
  214.6 0.3 fusion.38
  214.9 0.6 dynamic-slice_convert_fusion
  (59 shorter events, 1.4 us)
Async XLA Ops:
  7.2 2.0 copy-start
  7.2 196.9 %all-reduce.2.cloned.1.call-start = ((), (), s32[]{:S(2)}) async-start(), calls=%async_computation.2 | async-start | bytes 393216 | tf_op jit(solution)/shard_map/psum | solution.py:103
  8.3 64.8 %copy-start.1 = (bf16[4,256,1024]{2,1,0:T(8,128)(2,1)S(1)}, bf16[4,256,1024]{2,1,0:T(8,128)(2,1)}, u32[]{:S(2)}) copy-start(bf16[4,256,1024]{2,1,0:T(8,128)(2,1)} %param.14) | copy-start | bytes 6291460
  73.0 32.2 %copy-start.4 = (s32[16,2]{0,1:T(2,128)S(1)}, s32[16,2]{0,1:T(2,128)}, u32[]{:S(2)}) copy-start(s32[16,2]{0,1:T(2,128)} %param.18) | copy-start | bytes 388
  106.3 3.4 %copy-start.3 = (f32[6144]{0:T(1024)S(1)}, f32[6144]{0:T(1024)}, u32[]{:S(2)}) copy-start(f32[6144]{0:T(1024)} %param.16) | copy-start | bytes 73732
  106.3 3.5 %copy-start.5 = (bf16[6144,4]{0,1:T(4,128)(2,1)S(1)}, bf16[6144,4]{0,1:T(4,128)(2,1)}, u32[]{:S(2)}) copy-start(bf16[6144,4]{0,1:T(4,128)(2,1)} %param.17) | copy-start | bytes 147460
  109.7 14.4 %copy-start.2 = (bf16[4,6144]{1,0:T(4,128)(2,1)}, bf16[4,6144]{1,0:T(4,128)(2,1)S(1)}, u32[]{:S(2)}) copy-start(bf16[4,6144]{1,0:T(4,128)(2,1)S(1)} %multiply_convert_fusion) | copy-start | bytes 147460
  117.4 13.5 %slice-start = ((s8[12582912]{0:T(1024)(128)(4,1)}), s8[4194304]{0:T(1024)(128)(4,1)S(1)}, s32[]{:S(2)}) async-start(s8[12582912]{0:T(1024)(128)(4,1)} %bitcast.69), calls=%async_computation.3 | async-start | bytes 8388608
  117.4 13.5 %slice-start.1 = ((s8[12582912]{0:T(1024)(128)(4,1)}), s8[4194304]{0:T(1024)(128)(4,1)S(1)}, s32[]{:S(2)}) async-start(s8[12582912]{0:T(1024)(128)(4,1)} %bitcast.69), calls=%async_computation.4 | async-start | bytes 8388608
  124.2 6.7 %slice-start.2 = ((s8[12582912]{0:T(1024)(128)(4,1)}), s8[4194304]{0:T(1024)(128)(4,1)S(1)}, s32[]{:S(2)}) async-start(s8[12582912]{0:T(1024)(128)(4,1)} %bitcast.69), calls=%async_computation.5 | async-start | bytes 8388608
  205.8 8.7 %all-to-all-start.1 = ((f32[4,2,6144]{2,1,0:T(2,128)}), f32[4,2,6144]{2,1,0:T(2,128)S(1)}, u32[]{:S(2)}, u32[]{:S(2)}) async-start(f32[4,2,6144]{2,1,0:T(2,128)} %copy.64), calls=%async_computation.1 | async-start | bytes 393216 | tf_op jit(solution)/shard_map/all_to_all | solution.py:104
Sparse Core Ops, SparseCore 0:
  133.6 70.4 all-reduce.1
where the time goes:
time: 223 us; the launch traced here: 222 us
  blocking collectives  101 us (45%)
  waiting for transfers between devices  75.9 us (34%)
  matrix products  17.9 us (8%)
  between operations  14.3 us (6%)
  local copies, waits for them, and re-layouts  6.13 us (3%)
  starting transfers between devices  3.4 us (2%)
  other arithmetic  3.13 us (1%)
    all_gather x3, blocking collectives, combined_all(): pieces = jax.tree.map(lambda part: lax.all_gather(part, axis), value)  94.5 us
    psum x1, waiting for transfers between devices, shards(): summed = lax.psum(partial_value, 'shard')  70.6 us
    all_to_all x1, blocking collectives, shards(): lax.all_to_all(outgoing, 'grp', split_axis=0, concat_axis=0, tiled=True)  6.89 us
    dot_general x1, matrix products, shards(): jnp.einsum('gcd,df->gcf', arrived, gate_local, preferred_element_type=jnp...  6.76 us
    dot_general x1, matrix products, shards(): jnp.einsum('gcd,df->gcf', arrived, up_local, preferred_element_type=jnp.f...  6.69 us
    all_to_all x1, waiting for transfers between devices, shards(): lax.all_to_all(summed, 'grp', split_axis=0, concat_axis=0, tiled=True)  5.29 us
  transfers between devices with their start and end apart: 2, of which 2 were waited for; matrix products, arithmetic and copies ran while one was open for 0% of the time, Pallas kernels for 0%

commit v1 on v0

v1 whole, which is shorter than its diff:
```python
import math

import jax
import jax.numpy as jnp
from jax import lax
from jax.sharding import PartitionSpec as P

HEADS = 48
KV_HEADS = 8
HEAD_DIM = 128
BLOCK = 256


NEG_FILL = -1e30


def shards(
    query_rows, key_cache, value_cache, lengths, attn_gain, router, expert_ids, w_gate, w_up, w_down
):
    rows_here = query_rows.shape[0]
    span = key_cache.shape[1]
    kv_share = HEADS // KV_HEADS
    n_grp = lax.axis_size("grp")
    n_shard = lax.axis_size("shard")
    grp_id = lax.axis_index("grp")
    shard_id = lax.axis_index("shard")
    n_blocks = span // BLOCK

    query_heads = query_rows.reshape(rows_here, KV_HEADS, kv_share, HEAD_DIM)
    key_heads = key_cache.reshape(rows_here, span, KV_HEADS, HEAD_DIM)
    value_heads = value_cache.reshape(rows_here, n_blocks, BLOCK, KV_HEADS, HEAD_DIM)
    scores = jnp.einsum(
        "rgjd,rtgd->rgjt", query_heads, key_heads, preferred_element_type=jnp.float32
    ) / math.sqrt(HEAD_DIM)
    position = shard_id * span + jnp.arange(span, dtype=jnp.int32)
    live_mask = (position[None, :] < lengths[:, None])[:, None, None, :]
    scores = jnp.where(live_mask, scores, NEG_FILL)
    scores = scores.reshape(rows_here, KV_HEADS, kv_share, n_blocks, BLOCK)
    live_blocks = live_mask.reshape(rows_here, 1, 1, n_blocks, BLOCK)
    block_max = jnp.max(scores, axis=-1)
    block_probs = jnp.where(live_blocks, jnp.exp(scores - block_max[..., None]), 0.0).astype(
        jnp.bfloat16
    )
    block_sum = jnp.sum(block_probs.astype(jnp.float32), axis=-1)
    block_mix = jnp.einsum(
        "rgjbt,rbtgd->rgjbd", block_probs, value_heads, preferred_element_type=jnp.float32
    )
    dev_max = jnp.max(block_max, axis=-1)
    dev_factor = jnp.exp(block_max - dev_max[..., None])
    dev_sum = jnp.sum(block_sum * dev_factor, axis=-1).reshape(rows_here, HEADS)
    dev_mix = jnp.sum(block_mix * dev_factor[..., None], axis=-2).reshape(rows_here, HEADS, HEAD_DIM)
    dev_max = dev_max.reshape(rows_here, HEADS)

    per_chunk = HEADS // n_shard
    mix_out = dev_mix.reshape(rows_here, n_shard, per_chunk, HEAD_DIM)
    side = jnp.concatenate(
        [dev_max.reshape(rows_here, n_shard, per_chunk), dev_sum.reshape(rows_here, n_shard, per_chunk)],
        axis=-1,
    )
    side = jnp.pad(side, ((0, 0), (0, 0), (0, HEAD_DIM - 2 * per_chunk)))
    packed = jnp.concatenate([mix_out, side[:, :, None, :]], axis=2)
    packed = jnp.transpose(packed, (1, 0, 2, 3))
    stats = lax.all_to_all(packed, "shard", 0, 0, tiled=True)
    got_mix = stats[:, :, :per_chunk, :]
    got_max = stats[:, :, per_chunk, :per_chunk]
    got_sum = stats[:, :, per_chunk, per_chunk : 2 * per_chunk]
    top = jnp.max(got_max, axis=0)
    factor = jnp.exp(got_max - top[None])
    whole_sum = jnp.sum(got_sum * factor, axis=0)
    whole_mix = jnp.sum(got_mix * factor[..., None], axis=0)
    chunk = (whole_mix / whole_sum[..., None]).reshape(rows_here, per_chunk * HEAD_DIM)

    n_dev = n_grp * n_shard
    spread = jnp.broadcast_to(chunk[None], (n_dev,) + chunk.shape)
    gathered = lax.all_to_all(spread, ("grp", "shard"), 0, 0, tiled=True)
    gathered = gathered.reshape(n_grp, n_shard, rows_here, per_chunk * HEAD_DIM)
    attended = jnp.transpose(gathered, (0, 2, 1, 3)).reshape(n_grp * rows_here, -1)

    mean_square = jnp.mean(attended * attended, axis=-1, keepdims=True)
    normed_all = (attended * lax.rsqrt(mean_square + 1e-05) * attn_gain).astype(jnp.bfloat16)
    normed = lax.dynamic_slice_in_dim(normed_all, grp_id * rows_here, rows_here, 0)

    logits = jnp.dot(normed_all, router, preferred_element_type=jnp.float32)
    experts = router.shape[1]
    expert_range = jnp.arange(experts, dtype=jnp.int32)
    expert_hit = expert_ids[:, :, None] == expert_range[None, None, :]
    chosen = jnp.sum(jnp.where(expert_hit, logits[:, None, :], 0.0), axis=-1)
    first_weight = jax.nn.sigmoid(chosen[:, 0] - chosen[:, 1])
    route_weight = jnp.stack([first_weight, 1.0 - first_weight], axis=1)

    local_experts = w_gate.shape[0]
    width = normed_all.shape[1]
    total = jnp.zeros((n_grp * rows_here, width), jnp.float32)
    for local in range(local_experts):
        expert_index = grp_id * local_experts + local
        coefficient = jnp.sum(jnp.where(expert_ids == expert_index, route_weight, 0.0), axis=-1)
        gate_proj = jnp.dot(normed_all, w_gate[local], preferred_element_type=jnp.float32)
        up_proj = jnp.dot(normed_all, w_up[local], preferred_element_type=jnp.float32)
        hidden = (jax.nn.silu(gate_proj) * up_proj).astype(jnp.bfloat16)
        expert_y = jnp.dot(hidden, w_down[local], preferred_element_type=jnp.float32)
        total = total + coefficient[:, None] * expert_y

    out_width = width // n_shard
    blocks = total.reshape(n_grp, rows_here, n_shard, out_width)
    blocks = jnp.transpose(blocks, (0, 2, 1, 3)).reshape(n_dev, rows_here, out_width)
    arrived = lax.all_to_all(blocks, ("grp", "shard"), 0, 0, tiled=True)
    result = jnp.sum(arrived, axis=0)
    return (normed, result.astype(jnp.bfloat16))


def solution(mesh):
    in_specs = (
        P("grp", None),
        P("grp", "shard", None),
        P("grp", "shard", None),
        P("grp"),
        P(),
        P(),
        P(),
        P("grp", None, "shard"),
        P("grp", None, "shard"),
        P("grp", "shard", None),
    )
    out_specs = (P("grp", None), P("grp", "shard"))
    return jax.shard_map(shards, mesh=mesh, in_specs=in_specs, out_specs=out_specs, check_vma=False)
```

time: 223 us -> 73.6 us (0.33)
  blocking collectives: 101 us -> 14.3 us
  waiting for transfers between devices: 75.9 us -> 26.4 us
  between operations: 14.3 us -> 0.84 us
    all_gather x3 -> x0, blocking collectives: 94.5 us -> none  [combined_all(): pieces = jax.tree.map(lambda part: lax.all_gather(part, axis), value)]
    psum x1 -> x0, waiting for transfers between devices: 70.6 us -> none  [shards(): summed = lax.psum(partial_value, 'shard')]
    all_to_all x1 -> x2, waiting for transfers between devices: 5.29 us -> 26.4 us  [the longest x1 13.5 us: shards(): gathered = lax.all_to_all(spread, ('grp', 'shard'), 0, 0, tiled=True)]
    all_to_all x1, blocking collectives: 6.89 us -> 14.3 us  [shards(): stats = lax.all_to_all(packed, 'shard', 0, 0, tiled=True)]
    all_to_all x1 -> x2, starting transfers between devices: 3.36 us -> 5.19 us  [the longest x1 2.59 us: shards(): gathered = lax.all_to_all(spread, ('grp', 'shard'), 0, 0, tiled=True)]
    dot_general x8 -> x4, matrix products: 17.2 us -> 18.5 us  [the longest x1 11.5 us: shards(): jnp.dot(hidden, w_down[local], preferred_element_type=jnp.float32)]
  transfers between devices with their start and end apart: 2 -> 2, of which waited for: 2 -> 2; matrix products, arithmetic and copies ran while one was open for 0% -> 1% of each run, Pallas kernels for 0% -> 0%
where the time goes in v1:
time: 73.6 us; the launch traced here: 73.2 us
  waiting for transfers between devices  26.4 us (36%)
  matrix products  19.2 us (26%)
  blocking collectives  14.3 us (19%)
  starting transfers between devices  5.19 us (7%)
  local copies, waits for them, and re-layouts  4.61 us (6%)
  other arithmetic  2.72 us (4%)
  between operations  0.84 us (1%)
    all_to_all x1, blocking collectives, shards(): stats = lax.all_to_all(packed, 'shard', 0, 0, tiled=True)  14.3 us
    all_to_all x1, waiting for transfers between devices, shards(): gathered = lax.all_to_all(spread, ('grp', 'shard'), 0, 0, tiled=True)  13.5 us
    all_to_all x1, waiting for transfers between devices, shards(): arrived = lax.all_to_all(blocks, ('grp', 'shard'), 0, 0, tiled=True)  12.9 us
    dot_general x1, matrix products, shards(): jnp.dot(hidden, w_down[local], preferred_element_type=jnp.float32)  11.5 us
    dot_general x1, matrix products, shards(): jnp.dot(normed_all, w_gate[local], preferred_element_type=jnp.float32)  6.32 us
    all_to_all x1, starting transfers between devices, shards(): gathered = lax.all_to_all(spread, ('grp', 'shard'), 0, 0, tiled=True)  2.59 us
    all_to_all x1, starting transfers between devices, shards(): arrived = lax.all_to_all(blocks, ('grp', 'shard'), 0, 0, tiled=True)  2.59 us
  transfers between devices with their start and end apart: 2, of which 2 were waited for; matrix products, arithmetic and copies ran while one was open for 1% of the time, Pallas kernels for 0%

profile of v1, /device:TPU:0, one launch (start us, length us, event | category | flops | bytes accessed | tf_op | source)
XLA Modules:
  0.0 73.2 jit_solution(12586287830241184702)
XLA Ops:
  0.6 0.0 copy-start
  0.7 1.0 %reshape.175 = bf16[4,8,6,128]{3,2,1,0:T(8,128)(2,1)S(1)} reshape(bf16[4,6144]{1,0:T(4,128)(2,1)} %param.10) | data formatting | bytes 98304 | tf_op jit(solution)/shard_map/reshape | solution.py:29
  1.7 0.0 copy-start.1
  1.7 0.9 %broadcast_compare_fusion = pred[4,256]{1,0:T(4,128)(4,1)S(1)} fusion(s32[256]{0:T(256)S(1)} %iota_add_fusion, s32[4]{0:T(128)} %param.13), kind=kLoop, calls=%fused_computation.49 | loop fusion | flops 1024 | bytes 2064 | tf_op jit(solution)/shard_map/lt | solution.py:36
  2.6 0.0 copy-done
  2.6 0.7 fusion.53
  3.3 0.2 convert_reduce_fusion
  3.5 0.1 select_maximum_fusion
  3.6 0.0 copy-done.1
  3.6 0.0 copy-start.2
  3.6 0.4 fusion.27
  4.1 0.1 copy.75
  4.2 14.3 %all_to_all.15 = f32[8,4,7,128]{3,1,2,0:T(4,128)S(1)} all-to-all(f32[8,4,7,128]{3,1,2,0:T(4,128)S(1)} %copy.75), channel_id=1, replica_groups=mesh['grp'=4,'shard'=8] {'shard'}, dimensions={0} | all-to-all | bytes 229376 | tf_op jit(solution)/shard_map/all_to_all | solution.py:63
  18.5 0.1 fusion.46
  18.6 0.1 copy.78
  18.7 0.1 copy.77
  18.8 0.1 fusion.38
  18.9 0.1 divide_bitcast_fusion
  19.0 0.8 %broadcast_in_dim.65 = f32[32,4,768]{2,1,0:T(4,128)} broadcast(f32[4,768]{1,0:T(4,128)S(1)} %divide_bitcast_fusion), dimensions={1,2} | broadcast | bytes 405504 | tf_op jit(solution)/shard_map/broadcast_in_dim | solution.py:74
  19.8 2.6 %all-to-all-start.1 = ((f32[32,4,768]{2,1,0:T(4,128)}), f32[32,4,768]{2,1,0:T(4,128)S(1)}, u32[]{:S(2)}, u32[]{:S(2)}) async-start(f32[32,4,768]{2,1,0:T(4,128)} %broadcast_in_dim.65), calls=%async_computation.1 | async-start | bytes 786432 | tf_op jit(solution)/shard_map/all_to_all | solution.py:75
  22.4 0.0 copy-done.2
  22.4 13.5 %all-to-all-done.1 = f32[32,4,768]{2,1,0:T(4,128)S(1)} async-done(((f32[32,4,768]{2,1,0:T(4,128)}), f32[32,4,768]{2,1,0:T(4,128)S(1)}, u32[]{:S(2)}, u32[]{:S(2)}) %all-to-all-start.1) | async-done | bytes 393248 | tf_op jit(solution)/shard_map/all_to_all | solution.py:75
  36.0 0.2 multiply_reduce_fusion
  36.1 0.1 copy.81
  36.2 0.1 rsqrt.13
  36.3 0.0 copy-start.4
  36.3 0.1 copy.118
  36.4 0.0 copy-start.3
  36.5 0.1 copy.88
  36.6 0.1 multiply_convert_fusion
  36.8 0.1 multiply_convert_fusion.1
  36.9 0.2 copy-done.4
  37.1 0.2 fusion.54
  37.3 0.0 copy-done.3
  37.3 6.3 %fusion.4 = f32[16,1024]{1,0:T(8,128)S(1)} fusion(bf16[16,6144]{1,0:T(8,128)(2,1)S(1)} %bitcast.102, bf16[1,6144,1024]{2,1,0:T(8,128)(2,1)} %param.17), kind=kOutput, calls=%fused_computation.4 | convolution fusion | flops 201326592 | bytes 12845056 | tf_op jit(solution)/shard_map/dot_general | solution.py:97
  43.7 11.5 %fusion.6 = f32[16,6144]{1,0:T(8,128)S(1)} fusion(bf16[1,1024,6144]{2,1,0:T(8,128)(2,1)} %param.19, bf16[16,6144]{1,0:T(8,128)(2,1)S(1)} %bitcast.103, bf16[1,6144,1024]{2,1,0:T(8,128)(2,1)} %param.18, f32[16]{0:T(128)S(1)} %fusion.48, f32[16,1024]{1,0:T(8,128)S(1)} %fusion.4), kind=kOutput, calls=%fused_computation.6 | convolution fusion | flops 402849792 | bytes 25821248 | tf_op jit(solution)/shard_map/dot_general | solution.py:100
  55.2 0.1 copy.90
  55.4 1.0 %copy.84 = f32[32,4,768]{2,1,0:T(4,128)} copy(f32[32,4,768]{2,0,1:T(8,128)S(1)} %bitcast.106) | data formatting | bytes 786432 | tf_op jit(solution)/shard_map/reshape | solution.py:105
  56.4 2.6 %all-to-all-start.2 = ((f32[32,4,768]{2,1,0:T(4,128)}), f32[32,4,768]{2,1,0:T(4,128)S(1)}, u32[]{:S(2)}, u32[]{:S(2)}) async-start(f32[32,4,768]{2,1,0:T(4,128)} %copy.84), calls=%async_computation.2 | async-start | bytes 786432 | tf_op jit(solution)/shard_map/all_to_all | solution.py:106
  59.0 0.7 constant_dynamic-slice_fusion
  59.7 12.9 %all-to-all-done.2 = f32[32,4,768]{2,1,0:T(4,128)S(1)} async-done(((f32[32,4,768]{2,1,0:T(4,128)}), f32[32,4,768]{2,1,0:T(4,128)S(1)}, u32[]{:S(2)}, u32[]{:S(2)}) %all-to-all-start.2) | async-done | bytes 393248 | tf_op jit(solution)/shard_map/all_to_all | solution.py:106
  72.5 0.7 reduce_sum.80
  (13 shorter events, 0.3 us)
Async XLA Ops:
  0.6 1.9 %copy-start = (bf16[4,256,1024]{2,1,0:T(8,128)(2,1)S(1)}, bf16[4,256,1024]{2,1,0:T(8,128)(2,1)}, u32[]{:S(2)}) copy-start(bf16[4,256,1024]{2,1,0:T(8,128)(2,1)} %param.11) | copy-start | bytes 6291460
  1.7 1.9 %copy-start.1 = (bf16[4,256,1024]{2,1,0:T(8,128)(2,1)S(1)}, bf16[4,256,1024]{2,1,0:T(8,128)(2,1)}, u32[]{:S(2)}) copy-start(bf16[4,256,1024]{2,1,0:T(8,128)(2,1)} %param.12) | copy-start | bytes 6291460
  3.6 18.8 %copy-start.2 = (f32[6144]{0:T(1024)S(1)}, f32[6144]{0:T(1024)}, u32[]{:S(2)}) copy-start(f32[6144]{0:T(1024)} %param.14) | copy-start | bytes 73732
  19.8 16.1 %all-to-all-start.1 = ((f32[32,4,768]{2,1,0:T(4,128)}), f32[32,4,768]{2,1,0:T(4,128)S(1)}, u32[]{:S(2)}, u32[]{:S(2)}) async-start(f32[32,4,768]{2,1,0:T(4,128)} %broadcast_in_dim.65), calls=%async_computation.1 | async-start | bytes 786432 | tf_op jit(solution)/shard_map/all_to_all | solution.py:75
  36.3 0.8 %copy-start.4 = (bf16[6144,4]{0,1:T(4,128)(2,1)S(1)}, bf16[6144,4]{0,1:T(4,128)(2,1)}, u32[]{:S(2)}) copy-start(bf16[6144,4]{0,1:T(4,128)(2,1)} %param.15) | copy-start | bytes 147460
  36.4 0.9 %copy-start.3 = (s32[16,2]{0,1:T(2,128)S(1)}, s32[16,2]{0,1:T(2,128)}, u32[]{:S(2)}) copy-start(s32[16,2]{0,1:T(2,128)} %param.16) | copy-start | bytes 388
  56.4 16.1 %all-to-all-start.2 = ((f32[32,4,768]{2,1,0:T(4,128)}), f32[32,4,768]{2,1,0:T(4,128)S(1)}, u32[]{:S(2)}, u32[]{:S(2)}) async-start(f32[32,4,768]{2,1,0:T(4,128)} %copy.84), calls=%async_computation.2 | async-start | bytes 786432 | tf_op jit(solution)/shard_map/all_to_all | solution.py:106

commit v2 on v1

--- a/solution.py
+++ b/solution.py
@@ -71,8 +71,8 @@
     chunk = (whole_mix / whole_sum[..., None]).reshape(rows_here, per_chunk * HEAD_DIM)
 
     n_dev = n_grp * n_shard
-    spread = jnp.broadcast_to(chunk[None], (n_dev,) + chunk.shape)
-    gathered = lax.all_to_all(spread, ("grp", "shard"), 0, 0, tiled=True)
+    spread = jnp.broadcast_to(chunk.astype(jnp.bfloat16)[None], (n_dev,) + chunk.shape)
+    gathered = lax.all_to_all(spread, ("grp", "shard"), 0, 0, tiled=True).astype(jnp.float32)
     gathered = gathered.reshape(n_grp, n_shard, rows_here, per_chunk * HEAD_DIM)
     attended = jnp.transpose(gathered, (0, 2, 1, 3)).reshape(n_grp * rows_here, -1)
 

time: 73.6 us -> 68.5 us (0.931)
  waiting for transfers between devices: 26.4 us -> 21.4 us
    all_to_all x1, waiting for transfers between devices: 13.5 us -> 8.5 us  [shards(): lax.all_to_all(spread, ('grp', 'shard'), 0, 0, tiled=True)]
where the time goes in v2:
time: 68.5 us; the launch traced here: 68.2 us
  waiting for transfers between devices  21.4 us (31%)
  matrix products  19.2 us (28%)
  blocking collectives  14.3 us (21%)
  starting transfers between devices  5.53 us (8%)
  local copies, waits for them, and re-layouts  4.26 us (6%)
  other arithmetic  2.69 us (4%)
  between operations  0.86 us (1%)
    all_to_all x1, blocking collectives, shards(): stats = lax.all_to_all(packed, 'shard', 0, 0, tiled=True)  14.3 us
    all_to_all x1, waiting for transfers between devices, shards(): arrived = lax.all_to_all(blocks, ('grp', 'shard'), 0, 0, tiled=True)  12.9 us
    dot_general x1, matrix products, shards(): jnp.dot(hidden, w_down[local], preferred_element_type=jnp.float32)  11.5 us
    all_to_all x1, waiting for transfers between devices, shards(): lax.all_to_all(spread, ('grp', 'shard'), 0, 0, tiled=True)  8.5 us
    dot_general x1, matrix products, shards(): jnp.dot(normed_all, w_gate[local], preferred_element_type=jnp.float32)  6.32 us
    all_to_all x1, starting transfers between devices, shards(): arrived = lax.all_to_all(blocks, ('grp', 'shard'), 0, 0, tiled=True)  2.95 us
    all_to_all x1, starting transfers between devices, shards(): lax.all_to_all(spread, ('grp', 'shard'), 0, 0, tiled=True)  2.58 us
  transfers between devices with their start and end apart: 2, of which 2 were waited for; matrix products, arithmetic and copies ran while one was open for 1% of the time, Pallas kernels for 0%

profile of v2, /device:TPU:0, one launch (start us, length us, event | category | flops | bytes accessed | tf_op | source)
XLA Modules:
  0.0 68.2 jit_solution(6895623396108691515)
XLA Ops:
  0.6 0.0 copy-start
  0.6 1.0 %reshape.179 = bf16[4,8,6,128]{3,2,1,0:T(8,128)(2,1)S(1)} reshape(bf16[4,6144]{1,0:T(4,128)(2,1)} %param.10) | data formatting | bytes 98304 | tf_op jit(solution)/shard_map/reshape | solution.py:29
  1.7 0.0 copy-start.1
  1.7 0.9 %broadcast_compare_fusion = pred[4,256]{1,0:T(4,128)(4,1)S(1)} fusion(s32[256]{0:T(256)S(1)} %iota_add_fusion, s32[4]{0:T(128)} %param.13), kind=kLoop, calls=%fused_computation.50 | loop fusion | flops 1024 | bytes 2064 | tf_op jit(solution)/shard_map/lt | solution.py:36
  2.6 0.0 copy-done
  2.6 0.7 %fusion.54 = (f32[4,8,6]{2,1,0:T(8,128)S(1)}, f32[4,8,6,256]{3,2,1,0:T(8,128)S(1)}) fusion(bf16[4,8,6,128]{3,2,1,0:T(8,128)(2,1)S(1)} %reshape.179, pred[4,256]{1,0:T(4,128)(4,1)S(1)} %broadcast_compare_fusion, bf16[4,256,1024]{2,1,0:T(8,128)(2,1)S(1)} %copy-done), kind=kOutput, calls=%fused_computation.60 | convolution fusion | flops 12730176 | bytes 2344704 | tf_op jit(solution)/shard_map/rgjd,rtgd->rgjt/dot_general | solution.py:32
  3.3 0.2 convert_reduce_fusion
  3.5 0.1 select_maximum_fusion
  3.6 0.0 copy-start.2
  3.6 0.0 copy-done.1
  3.6 0.4 fusion.27
  4.1 0.1 copy.75
  4.2 14.3 %all_to_all.15 = f32[8,4,7,128]{3,1,2,0:T(4,128)S(1)} all-to-all(f32[8,4,7,128]{3,1,2,0:T(4,128)S(1)} %copy.75), channel_id=1, replica_groups=mesh['grp'=4,'shard'=8] {'shard'}, dimensions={0} | all-to-all | bytes 229376 | tf_op jit(solution)/shard_map/all_to_all | solution.py:63
  18.5 0.1 fusion.46
  18.6 0.1 copy.77
  18.7 0.1 copy.78
  18.8 0.1 fusion.38
  18.9 0.1 fusion.48
  19.0 0.7 %broadcast_in_dim.66 = bf16[32,4,768]{2,1,0:T(4,128)(2,1)} broadcast(bf16[4,768]{1,0:T(4,128)(2,1)S(1)} %fusion.48), dimensions={1,2} | broadcast | bytes 202752 | tf_op jit(solution)/shard_map/broadcast_in_dim | solution.py:74
  19.8 2.6 %all-to-all-start.1 = ((bf16[32,4,768]{2,1,0:T(4,128)(2,1)}), bf16[32,4,768]{2,1,0:T(4,128)(2,1)S(1)}, u32[]{:S(2)}, u32[]{:S(2)}) async-start(bf16[32,4,768]{2,1,0:T(4,128)(2,1)} %broadcast_in_dim.66), calls=%async_computation.1 | async-start | bytes 393216 | tf_op jit(solution)/shard_map/all_to_all | solution.py:75
  22.3 0.0 copy-done.2
  22.4 0.0 copy-start.4
  22.4 0.0 copy-start.3
  22.4 8.5 %all-to-all-done.1 = bf16[32,4,768]{2,1,0:T(4,128)(2,1)S(1)} async-done(((bf16[32,4,768]{2,1,0:T(4,128)(2,1)}), bf16[32,4,768]{2,1,0:T(4,128)(2,1)S(1)}, u32[]{:S(2)}, u32[]{:S(2)}) %all-to-all-start.1) | async-done | bytes 196640 | tf_op jit(solution)/shard_map/all_to_all | solution.py:75
  31.0 0.1 copy.88
  31.1 0.1 multiply_reduce_fusion
  31.2 0.1 copy.81
  31.3 0.1 rsqrt.13
  31.4 0.1 multiply_convert_fusion
  31.6 0.1 multiply_convert_fusion.1
  31.7 0.0 copy-done.4
  31.7 0.2 fusion.55
  31.9 0.0 copy-done.3
  32.0 6.3 %fusion.4 = f32[16,1024]{1,0:T(8,128)S(1)} fusion(bf16[16,6144]{1,0:T(8,128)(2,1)S(1)} %bitcast.104, bf16[1,6144,1024]{2,1,0:T(8,128)(2,1)} %param.17), kind=kOutput, calls=%fused_computation.4 | convolution fusion | flops 201326592 | bytes 12845056 | tf_op jit(solution)/shard_map/dot_general | solution.py:97
  38.3 11.5 %fusion.6 = f32[16,6144]{1,0:T(8,128)S(1)} fusion(bf16[1,1024,6144]{2,1,0:T(8,128)(2,1)} %param.19, bf16[16,6144]{1,0:T(8,128)(2,1)S(1)} %bitcast.105, bf16[1,6144,1024]{2,1,0:T(8,128)(2,1)} %param.18, f32[16]{0:T(128)S(1)} %fusion.49, f32[16,1024]{1,0:T(8,128)S(1)} %fusion.4), kind=kOutput, calls=%fused_computation.6 | convolution fusion | flops 402849792 | bytes 25821248 | tf_op jit(solution)/shard_map/dot_general | solution.py:100
  49.9 0.1 copy.90
  50.0 1.0 %copy.84 = f32[32,4,768]{2,1,0:T(4,128)} copy(f32[32,4,768]{2,0,1:T(8,128)S(1)} %bitcast.108) | data formatting | bytes 786432 | tf_op jit(solution)/shard_map/reshape | solution.py:105
  51.0 2.9 %all-to-all-start.2 = ((f32[32,4,768]{2,1,0:T(4,128)}), f32[32,4,768]{2,1,0:T(4,128)S(1)}, u32[]{:S(2)}, u32[]{:S(2)}) async-start(f32[32,4,768]{2,1,0:T(4,128)} %copy.84), calls=%async_computation.2 | async-start | bytes 786432 | tf_op jit(solution)/shard_map/all_to_all | solution.py:106
  54.0 0.7 constant_dynamic-slice_fusion
  54.6 12.9 %all-to-all-done.2 = f32[32,4,768]{2,1,0:T(4,128)S(1)} async-done(((f32[32,4,768]{2,1,0:T(4,128)}), f32[32,4,768]{2,1,0:T(4,128)S(1)}, u32[]{:S(2)}, u32[]{:S(2)}) %all-to-all-start.2) | async-done | bytes 393248 | tf_op jit(solution)/shard_map/all_to_all | solution.py:106
  67.5 0.7 reduce_sum.80
  (14 shorter events, 0.3 us)
Async XLA Ops:
  0.6 1.9 %copy-start = (bf16[4,256,1024]{2,1,0:T(8,128)(2,1)S(1)}, bf16[4,256,1024]{2,1,0:T(8,128)(2,1)}, u32[]{:S(2)}) copy-start(bf16[4,256,1024]{2,1,0:T(8,128)(2,1)} %param.11) | copy-start | bytes 6291460
  1.7 1.9 %copy-start.1 = (bf16[4,256,1024]{2,1,0:T(8,128)(2,1)S(1)}, bf16[4,256,1024]{2,1,0:T(8,128)(2,1)}, u32[]{:S(2)}) copy-start(bf16[4,256,1024]{2,1,0:T(8,128)(2,1)} %param.12) | copy-start | bytes 6291460
  3.6 18.7 %copy-start.2 = (f32[6144]{0:T(1024)S(1)}, f32[6144]{0:T(1024)}, u32[]{:S(2)}) copy-start(f32[6144]{0:T(1024)} %param.14) | copy-start | bytes 73732
  19.8 11.1 %all-to-all-start.1 = ((bf16[32,4,768]{2,1,0:T(4,128)(2,1)}), bf16[32,4,768]{2,1,0:T(4,128)(2,1)S(1)}, u32[]{:S(2)}, u32[]{:S(2)}) async-start(bf16[32,4,768]{2,1,0:T(4,128)(2,1)} %broadcast_in_dim.66), calls=%async_computation.1 | async-start | bytes 393216 | tf_op jit(solution)/shard_map/all_to_all | solution.py:75
  22.4 9.4 %copy-start.4 = (bf16[6144,4]{0,1:T(4,128)(2,1)S(1)}, bf16[6144,4]{0,1:T(4,128)(2,1)}, u32[]{:S(2)}) copy-start(bf16[6144,4]{0,1:T(4,128)(2,1)} %param.15) | copy-start | bytes 147460
  22.4 9.5 %copy-start.3 = (s32[16,2]{0,1:T(2,128)S(1)}, s32[16,2]{0,1:T(2,128)}, u32[]{:S(2)}) copy-start(s32[16,2]{0,1:T(2,128)} %param.16) | copy-start | bytes 388
  51.0 16.5 %all-to-all-start.2 = ((f32[32,4,768]{2,1,0:T(4,128)}), f32[32,4,768]{2,1,0:T(4,128)S(1)}, u32[]{:S(2)}, u32[]{:S(2)}) async-start(f32[32,4,768]{2,1,0:T(4,128)} %copy.84), calls=%async_computation.2 | async-start | bytes 786432 | tf_op jit(solution)/shard_map/all_to_all | solution.py:106

commit v3 on v2

--- a/solution.py
+++ b/solution.py
@@ -12,6 +12,20 @@
 
 
 NEG_FILL = -1e30
+CAP = 2
+
+
+def slots_of(expert_ids, expert_index, rows_here, n_groups):
+    ids = expert_ids.reshape(n_groups, rows_here, expert_ids.shape[1])
+    hit = jnp.any(ids == expert_index, axis=-1)
+    rank = jnp.cumsum(hit.astype(jnp.int32), axis=1) - 1
+    local = jnp.arange(rows_here, dtype=jnp.int32)
+    rows, live = [], []
+    for slot in range(CAP):
+        match = hit & (rank == slot)
+        rows.append(jnp.sum(jnp.where(match, local[None, :], 0), axis=1))
+        live.append(jnp.any(match, axis=1))
+    return jnp.stack(rows, axis=1), jnp.stack(live, axis=1)
 
 
 def shards(
@@ -89,6 +103,7 @@
     route_weight = jnp.stack([first_weight, 1.0 - first_weight], axis=1)
 
     local_experts = w_gate.shape[0]
+    assert local_experts == 1
     width = normed_all.shape[1]
     total = jnp.zeros((n_grp * rows_here, width), jnp.float32)
     for local in range(local_experts):
@@ -101,10 +116,21 @@
         total = total + coefficient[:, None] * expert_y
 
     out_width = width // n_shard
-    blocks = total.reshape(n_grp, rows_here, n_shard, out_width)
-    blocks = jnp.transpose(blocks, (0, 2, 1, 3)).reshape(n_dev, rows_here, out_width)
+    picked_rows, picked_live = slots_of(expert_ids, grp_id * local_experts, rows_here, n_grp)
+    grouped = total.reshape(n_grp, rows_here, width)
+    picked = jnp.take_along_axis(grouped, picked_rows[:, :, None], axis=1)
+    picked = jnp.where(picked_live[:, :, None], picked, 0.0)
+    blocks = picked.reshape(n_grp, CAP, n_shard, out_width)
+    blocks = jnp.transpose(blocks, (0, 2, 1, 3)).reshape(n_dev, CAP, out_width)
     arrived = lax.all_to_all(blocks, ("grp", "shard"), 0, 0, tiled=True)
-    result = jnp.sum(arrived, axis=0)
+    per_expert = jnp.sum(arrived.reshape(n_grp, n_shard, CAP, out_width), axis=1)
+    own_ids = lax.dynamic_slice_in_dim(expert_ids, grp_id * rows_here, rows_here, 0)
+    result = jnp.zeros((rows_here, out_width), jnp.float32)
+    for source in range(n_grp):
+        home_rows, home_live = slots_of(own_ids, source * local_experts, rows_here, 1)
+        for slot in range(CAP):
+            hit = (jnp.arange(rows_here) == home_rows[0, slot]) & home_live[0, slot]
+            result = result + jnp.where(hit[:, None], per_expert[source, slot][None, :], 0.0)
     return (normed, result.astype(jnp.bfloat16))
 
 

time: 68.5 us -> 71.5 us (1.044)
  other arithmetic: 2.69 us -> 17.3 us
  blocking collectives: 14.3 us -> 0 us
  starting transfers between devices: 5.53 us -> 16.3 us
  waiting for transfers between devices: 21.4 us -> 11.3 us
  local copies, waits for them, and re-layouts: 4.26 us -> 5.91 us
    all_to_all x1 -> x0, blocking collectives: 14.3 us -> none  [shards(): stats = lax.all_to_all(packed, 'shard', 0, 0, tiled=True)]
    and x0 -> x9, other arithmetic: none -> 10.2 us  [the longest x8 10.1 us: shards(): hit = (jnp.arange(rows_here) == home_rows[0, slot]) & home_live[0, slot]]
    all_to_all x0 -> x1, starting transfers between devices: none -> 7.25 us  [shards(): stats = lax.all_to_all(packed, 'shard', 0, 0, tiled=True)]
    all_to_all x1, waiting for transfers between devices: 8.5 us -> 3.41 us  [shards(): lax.all_to_all(spread, ('grp', 'shard'), 0, 0, tiled=True)]
    all_to_all x1, waiting for transfers between devices: 12.9 us -> 7.89 us  [shards(): arrived = lax.all_to_all(blocks, ('grp', 'shard'), 0, 0, tiled=True)]
    all_to_all x1, starting transfers between devices: 2.58 us -> 6.03 us  [shards(): lax.all_to_all(spread, ('grp', 'shard'), 0, 0, tiled=True)]
    reduce_or x0 -> x5, other arithmetic: none -> 1.72 us  [the longest x3 1.6 us: slots_of(): live.append(jnp.any(match, axis=1))]
    reduce_sum x1 -> x4, other arithmetic: 0.67 us -> 1.71 us  [the longest x3 1.66 us: slots_of(): rows.append(jnp.sum(jnp.where(match, local[None, :], 0), axis=1))]
  transfers between devices with their start and end apart: 2 -> 3, of which waited for: 2 -> 2; matrix products, arithmetic and copies ran while one was open for 1% -> 22% of each run, Pallas kernels for 0% -> 0%
where the time goes in v3:
time: 71.5 us; the launch traced here: 71 us
  matrix products  19.2 us (27%)
  other arithmetic  17.3 us (24%)
  starting transfers between devices  16.3 us (23%)
  waiting for transfers between devices  11.3 us (16%)
  local copies, waits for them, and re-layouts  5.91 us (8%)
  between operations  0.96 us (1%)
    dot_general x1, matrix products, shards(): jnp.dot(hidden, w_down[local], preferred_element_type=jnp.float32)  11.5 us
    and x8, other arithmetic, shards(): hit = (jnp.arange(rows_here) == home_rows[0, slot]) & home_live[0, slot]  10.1 us
    all_to_all x1, waiting for transfers between devices, shards(): arrived = lax.all_to_all(blocks, ('grp', 'shard'), 0, 0, tiled=True)  7.89 us
    all_to_all x1, starting transfers between devices, shards(): stats = lax.all_to_all(packed, 'shard', 0, 0, tiled=True)  7.25 us
    dot_general x1, matrix products, shards(): jnp.dot(normed_all, w_gate[local], preferred_element_type=jnp.float32)  6.3 us
    all_to_all x1, starting transfers between devices, shards(): lax.all_to_all(spread, ('grp', 'shard'), 0, 0, tiled=True)  6.03 us
    all_to_all x1, waiting for transfers between devices, shards(): lax.all_to_all(spread, ('grp', 'shard'), 0, 0, tiled=True)  3.41 us
    all_to_all x1, starting transfers between devices, shards(): arrived = lax.all_to_all(blocks, ('grp', 'shard'), 0, 0, tiled=True)  3.05 us
  transfers between devices with their start and end apart: 3, of which 2 were waited for; matrix products, arithmetic and copies ran while one was open for 22% of the time, Pallas kernels for 0%

profile of v3, /device:TPU:0, one launch (start us, length us, event | category | flops | bytes accessed | tf_op | source)
XLA Modules:
  0.0 71.0 jit_solution(3881589903452942743)
XLA Ops:
  0.7 1.0 %reshape.607 = bf16[4,8,6,128]{3,2,1,0:T(8,128)(2,1)S(1)} reshape(bf16[4,6144]{1,0:T(4,128)(2,1)} %param.10) | data formatting | bytes 98304 | tf_op jit(solution)/shard_map/reshape | solution.py:43
  1.7 0.9 %broadcast_compare_fusion = pred[4,256]{1,0:T(4,128)(4,1)S(1)} fusion(s32[256]{0:T(256)S(1)} %iota_add_fusion, s32[4]{0:T(128)} %param.13), kind=kLoop, calls=%fused_computation.75 | loop fusion | flops 1024 | bytes 2064 | tf_op jit(solution)/shard_map/lt | solution.py:50
  2.6 0.7 %fusion.78 = (f32[4,8,6]{2,1,0:T(8,128)S(1)}, f32[4,8,6,256]{3,2,1,0:T(8,128)S(1)}) fusion(bf16[4,8,6,128]{3,2,1,0:T(8,128)(2,1)S(1)} %reshape.607, pred[4,256]{1,0:T(4,128)(4,1)S(1)} %broadcast_compare_fusion, bf16[4,256,1024]{2,1,0:T(8,128)(2,1)S(1)} %copy-done), kind=kOutput, calls=%fused_computation.137 | convolution fusion | flops 12730176 | bytes 2344704 | tf_op jit(solution)/shard_map/rgjd,rtgd->rgjt/dot_general | solution.py:46
  3.3 0.2 convert_reduce_fusion
  3.6 0.4 fusion.27
  4.1 0.7 %copy.86 = f32[8,4,7,128]{3,1,2,0:T(4,128)} copy(f32[8,4,7,128]{3,2,0,1:T(8,128)S(1)} %maximum_bitcast_fusion) | data formatting | bytes 229376 | tf_op jit(solution)/shard_map/transpose | solution.py:76
  4.8 7.3 %all-to-all-start = ((f32[8,4,7,128]{3,1,2,0:T(4,128)}), f32[8,4,7,128]{3,1,2,0:T(4,128)S(1)}, u32[]{:S(2)}, u32[]{:S(2)}) async-start(f32[8,4,7,128]{3,1,2,0:T(4,128)} %copy.86), calls=%async_computation | async-start | bytes 229376 | tf_op jit(solution)/shard_map/all_to_all | solution.py:77
  12.1 0.1 compare_reduce_fusion.3
  12.2 0.2 reduce-window.26
  12.4 0.2 reduce-window.27
  12.6 0.8 %select_reduce_fusion.4 = (s32[]{:T(128)}, s32[]{:T(128)}, s32[]{:T(128)}, s32[]{:T(128)}) fusion(pred[4]{0:T(512)(128)(4,1)S(1)} %get-tuple-element.17, s32[4,1]{0,1:T(1,128)S(1)} %reduce-window.27, pred[4]{0:T(512)(128)(4,1)S(1)} %get-tuple-element.16, s32[4,1]{0,1:T(1,128)S(1)} %reduce-window.26), kind=kLoop, calls=%fused_computation.111 | loop fusion | flops 68 | bytes 56 | tf_op jit(solution)/shard_map/reduce_sum | solution.py:26
  13.3 0.7 %fusion.70 = (pred[]{:T(512)}, pred[]{:T(512)}, pred[]{:T(512)}, pred[]{:T(512)}) fusion(pred[4]{0:T(512)(128)(4,1)S(1)} %get-tuple-element.16, s32[4,1]{0,1:T(1,128)S(1)} %reduce-window.26, pred[4]{0:T(512)(128)(4,1)S(1)} %get-tuple-element.17, s32[4,1]{0,1:T(1,128)S(1)} %reduce-window.27), kind=kLoop, calls=%fused_computation.130 | loop fusion | flops 52 | bytes 44 | tf_op jit(solution)/shard_map/reduce_or | solution.py:27
  14.1 0.2 reduce-window.24
  14.3 0.2 reduce-window.25
  14.4 0.7 fusion.66
  15.2 0.8 %select_reduce_fusion.8 = (s32[]{:T(128)}, s32[]{:T(128)}, s32[]{:T(128)}, s32[]{:T(128)}) fusion(pred[4]{0:T(512)(128)(4,1)S(1)} %get-tuple-element.15, s32[4,1]{0,1:T(1,128)S(1)} %reduce-window.25, pred[4]{0:T(512)(128)(4,1)S(1)} %get-tuple-element.14, s32[4,1]{0,1:T(1,128)S(1)} %reduce-window.24), kind=kLoop, calls=%fused_computation.115 | loop fusion | flops 68 | bytes 56 | tf_op jit(solution)/shard_map/reduce_sum | solution.py:26
  16.0 0.2 reduce_window_sum.24
  16.2 0.2 fusion.75
  16.3 0.2 select_reduce_fusion.1
  16.5 1.4 %compare_and_fusion = pred[4]{0:T(512)(128)(4,1)S(1)} fusion(pred[]{:T(512)} %get-tuple-element.50, s32[]{:T(128)} %get-tuple-element.27), kind=kLoop, calls=%fused_computation.85 | loop fusion | flops 8 | bytes 9 | tf_op jit(solution)/shard_map/and | solution.py:132
  17.9 1.2 %compare_and_fusion.1 = pred[4]{0:T(512)(128)(4,1)S(1)} fusion(pred[]{:T(512)} %get-tuple-element.51, s32[]{:T(128)} %get-tuple-element.26), kind=kLoop, calls=%fused_computation.86 | loop fusion | flops 8 | bytes 9 | tf_op jit(solution)/shard_map/and | solution.py:132
  19.1 1.3 %compare_and_fusion.10 = pred[4]{0:T(512)(128)(4,1)S(1)} fusion(pred[]{:T(512)} %get-tuple-element.12, s32[]{:T(128)} %get-tuple-element.47), kind=kLoop, calls=%fused_computation.98 | loop fusion | flops 8 | bytes 9 | tf_op jit(solution)/shard_map/and | solution.py:132
  20.4 1.3 %compare_and_fusion.2 = pred[4]{0:T(512)(128)(4,1)S(1)} fusion(pred[]{:T(512)} %get-tuple-element.25, s32[]{:T(128)} %get-tuple-element.44), kind=kLoop, calls=%fused_computation.88 | loop fusion | flops 8 | bytes 9 | tf_op jit(solution)/shard_map/and | solution.py:132
  21.9 0.1 copy.88
  22.1 0.1 fusion.40
  22.4 0.7 %broadcast_in_dim.244 = bf16[32,4,768]{2,1,0:T(4,128)(2,1)} broadcast(bf16[4,768]{1,0:T(4,128)(2,1)S(1)} %fusion.50), dimensions={1,2} | broadcast | bytes 202752 | tf_op jit(solution)/shard_map/broadcast_in_dim | solution.py:88
  23.1 6.0 %all-to-all-start.1 = ((bf16[32,4,768]{2,1,0:T(4,128)(2,1)}), bf16[32,4,768]{2,1,0:T(4,128)(2,1)S(1)}, u32[]{:S(2)}, u32[]{:S(2)}) async-start(bf16[32,4,768]{2,1,0:T(4,128)(2,1)} %broadcast_in_dim.244), calls=%async_computation.1 | async-start | bytes 393216 | tf_op jit(solution)/shard_map/all_to_all | solution.py:89
  29.1 1.3 %compare_and_fusion.3 = pred[4]{0:T(512)(128)(4,1)S(1)} fusion(pred[]{:T(512)} %get-tuple-element.24, s32[]{:T(128)} %get-tuple-element.45), kind=kLoop, calls=%fused_computation.89 | loop fusion | flops 8 | bytes 9 | tf_op jit(solution)/shard_map/and | solution.py:132
  30.4 0.1 copy.94
  30.6 1.2 %compare_and_fusion.4 = pred[4]{0:T(512)(128)(4,1)S(1)} fusion(pred[]{:T(512)} %get-tuple-element.48, s32[]{:T(128)} %get-tuple-element.19), kind=kLoop, calls=%fused_computation.91 | loop fusion | flops 8 | bytes 9 | tf_op jit(solution)/shard_map/and | solution.py:132
  31.8 1.2 %compare_and_fusion.5 = pred[4]{0:T(512)(128)(4,1)S(1)} fusion(pred[]{:T(512)} %get-tuple-element.49, s32[]{:T(128)} %get-tuple-element.18), kind=kLoop, calls=%fused_computation.92 | loop fusion | flops 8 | bytes 9 | tf_op jit(solution)/shard_map/and | solution.py:132
  33.0 1.3 %compare_and_fusion.6 = pred[4]{0:T(512)(128)(4,1)S(1)} fusion(pred[]{:T(512)} %get-tuple-element.13, s32[]{:T(128)} %get-tuple-element.46), kind=kLoop, calls=%fused_computation.94 | loop fusion | flops 8 | bytes 9 | tf_op jit(solution)/shard_map/and | solution.py:132
  34.3 3.4 %all-to-all-done.1 = bf16[32,4,768]{2,1,0:T(4,128)(2,1)S(1)} async-done(((bf16[32,4,768]{2,1,0:T(4,128)(2,1)}), bf16[32,4,768]{2,1,0:T(4,128)(2,1)S(1)}, u32[]{:S(2)}, u32[]{:S(2)}) %all-to-all-start.1) | async-done | bytes 196640 | tf_op jit(solution)/shard_map/all_to_all | solution.py:89
  37.7 0.1 copy.110
  37.9 0.1 multiply_reduce_fusion
  38.0 0.1 copy.92
  38.2 0.1 multiply_convert_fusion.1
  38.3 0.2 fusion.79
  38.5 0.1 multiply_convert_fusion
  38.8 6.3 %fusion.4 = f32[16,1024]{1,0:T(8,128)S(1)} fusion(bf16[16,6144]{1,0:T(8,128)(2,1)S(1)} %bitcast.201, bf16[1,6144,1024]{2,1,0:T(8,128)(2,1)} %param.17), kind=kOutput, calls=%fused_computation.5 | convolution fusion | flops 201326592 | bytes 12845056 | tf_op jit(solution)/shard_map/dot_general | solution.py:112
  45.1 11.5 %fusion.6 = f32[16,6144]{1,0:T(8,128)S(1)} fusion(bf16[1,1024,6144]{2,1,0:T(8,128)(2,1)} %param.19, bf16[16,6144]{1,0:T(8,128)(2,1)S(1)} %bitcast.202, bf16[1,6144,1024]{2,1,0:T(8,128)(2,1)} %param.18, f32[16]{0:T(128)S(1)} %fusion.62, f32[16,1024]{1,0:T(8,128)S(1)} %fusion.4), kind=kOutput, calls=%fused_computation.7 | convolution fusion | flops 402849792 | bytes 25821248 | tf_op jit(solution)/shard_map/dot_general | solution.py:115
  56.6 0.1 reshape.612
  56.7 0.8 %gather_fusion = f32[8,6144]{1,0:T(8,128)S(1)} fusion(f32[4,4,6144]{2,1,0:T(4,128)S(1)} %reshape.612, s32[8]{0:T(128)S(1)} %reshape.620), kind=kCustom, calls=%fused_computation | custom fusion | bytes 393280 | tf_op jit(solution)/shard_map/jit(take_along_axis)/gather | solution.py:121
  57.8 0.8 %copy.96 = f32[32,2,768]{2,1,0:T(2,128)} copy(f32[32,2,768]{2,0,1:T(8,128)S(1)} %fusion.39) | data formatting | bytes 393216 | tf_op jit(solution)/shard_map/reshape | solution.py:124
  58.6 3.0 %all-to-all-start.2 = ((f32[32,2,768]{2,1,0:T(2,128)}), f32[32,2,768]{2,1,0:T(2,128)S(1)}, u32[]{:S(2)}, u32[]{:S(2)}) async-start(f32[32,2,768]{2,1,0:T(2,128)} %copy.96), calls=%async_computation.2 | async-start | bytes 393216 | tf_op jit(solution)/shard_map/all_to_all | solution.py:125
  61.6 0.7 constant_dynamic-slice_fusion.1
  62.3 7.9 %all-to-all-done.2 = f32[32,2,768]{2,1,0:T(2,128)S(1)} async-done(((f32[32,2,768]{2,1,0:T(2,128)}), f32[32,2,768]{2,1,0:T(2,128)S(1)}, u32[]{:S(2)}, u32[]{:S(2)}) %all-to-all-start.2) | async-done | bytes 196640 | tf_op jit(solution)/shard_map/all_to_all | solution.py:125
  70.3 0.7 add_convert_fusion
  (44 shorter events, 1.2 us)
Async XLA Ops:
  0.6 1.9 %copy-start = (bf16[4,256,1024]{2,1,0:T(8,128)(2,1)S(1)}, bf16[4,256,1024]{2,1,0:T(8,128)(2,1)}, u32[]{:S(2)}) copy-start(bf16[4,256,1024]{2,1,0:T(8,128)(2,1)} %param.11) | copy-start | bytes 6291460
  1.7 1.9 %copy-start.1 = (bf16[4,256,1024]{2,1,0:T(8,128)(2,1)S(1)}, bf16[4,256,1024]{2,1,0:T(8,128)(2,1)}, u32[]{:S(2)}) copy-start(bf16[4,256,1024]{2,1,0:T(8,128)(2,1)} %param.12) | copy-start | bytes 6291460
  3.3 8.8 %copy-start.3 = (s32[16,2]{0,1:T(2,128)S(1)}, s32[16,2]{0,1:T(2,128)}, u32[]{:S(2)}) copy-start(s32[16,2]{0,1:T(2,128)} %param.16) | copy-start | bytes 388
  3.6 26.8 %copy-start.2 = (f32[6144]{0:T(1024)S(1)}, f32[6144]{0:T(1024)}, u32[]{:S(2)}) copy-start(f32[6144]{0:T(1024)} %param.14) | copy-start | bytes 73732
  4.8 17.0 %all-to-all-start = ((f32[8,4,7,128]{3,1,2,0:T(4,128)}), f32[8,4,7,128]{3,1,2,0:T(4,128)S(1)}, u32[]{:S(2)}, u32[]{:S(2)}) async-start(f32[8,4,7,128]{3,1,2,0:T(4,128)} %copy.86), calls=%async_computation | async-start | bytes 229376 | tf_op jit(solution)/shard_map/all_to_all | solution.py:77
  12.1 26.3 %copy-start.4 = (bf16[6144,4]{0,1:T(4,128)(2,1)S(1)}, bf16[6144,4]{0,1:T(4,128)(2,1)}, u32[]{:S(2)}) copy-start(bf16[6144,4]{0,1:T(4,128)(2,1)} %param.15) | copy-start | bytes 147460
  23.1 14.6 %all-to-all-start.1 = ((bf16[32,4,768]{2,1,0:T(4,128)(2,1)}), bf16[32,4,768]{2,1,0:T(4,128)(2,1)S(1)}, u32[]{:S(2)}, u32[]{:S(2)}) async-start(bf16[32,4,768]{2,1,0:T(4,128)(2,1)} %broadcast_in_dim.244), calls=%async_computation.1 | async-start | bytes 393216 | tf_op jit(solution)/shard_map/all_to_all | solution.py:89
  58.6 11.6 %all-to-all-start.2 = ((f32[32,2,768]{2,1,0:T(2,128)}), f32[32,2,768]{2,1,0:T(2,128)S(1)}, u32[]{:S(2)}, u32[]{:S(2)}) async-start(f32[32,2,768]{2,1,0:T(2,128)} %copy.96), calls=%async_computation.2 | async-start | bytes 393216 | tf_op jit(solution)/shard_map/all_to_all | solution.py:125

commit v4 on v2

--- a/solution.py
+++ b/solution.py
@@ -12,6 +12,15 @@
 
 
 NEG_FILL = -1e30
+CAP = 2
+
+
+def slot_match(expert_ids, experts, rows_here, n_groups):
+    ids = expert_ids.reshape(n_groups, rows_here, expert_ids.shape[1])
+    hit = jnp.any(ids[None, :, :, :] == experts[:, None, None, None], axis=-1)
+    rank = jnp.cumsum(hit.astype(jnp.int32), axis=-1) - 1
+    slot = jnp.arange(CAP, dtype=jnp.int32)
+    return hit[:, :, None, :] & (rank[:, :, None, :] == slot[None, None, :, None])
 
 
 def shards(
@@ -89,6 +98,7 @@
     route_weight = jnp.stack([first_weight, 1.0 - first_weight], axis=1)
 
     local_experts = w_gate.shape[0]
+    assert local_experts == 1
     width = normed_all.shape[1]
     total = jnp.zeros((n_grp * rows_here, width), jnp.float32)
     for local in range(local_experts):
@@ -101,10 +111,17 @@
         total = total + coefficient[:, None] * expert_y
 
     out_width = width // n_shard
-    blocks = total.reshape(n_grp, rows_here, n_shard, out_width)
-    blocks = jnp.transpose(blocks, (0, 2, 1, 3)).reshape(n_dev, rows_here, out_width)
+    sending = slot_match(expert_ids, (grp_id * local_experts)[None], rows_here, n_grp)[0]
+    grouped = total.reshape(n_grp, 1, rows_here, width)
+    picked = jnp.sum(jnp.where(sending[..., None], grouped, 0.0), axis=2)
+    blocks = picked.reshape(n_grp, CAP, n_shard, out_width)
+    blocks = jnp.transpose(blocks, (0, 2, 1, 3)).reshape(n_dev, CAP, out_width)
     arrived = lax.all_to_all(blocks, ("grp", "shard"), 0, 0, tiled=True)
-    result = jnp.sum(arrived, axis=0)
+    per_expert = jnp.sum(arrived.reshape(n_grp, n_shard, CAP, out_width), axis=1)
+    own_ids = lax.dynamic_slice_in_dim(expert_ids, grp_id * rows_here, rows_here, 0)
+    homes = slot_match(own_ids, jnp.arange(n_grp, dtype=jnp.int32) * local_experts, rows_here, 1)[:, 0]
+    spread_back = jnp.where(homes[..., None], per_expert[:, :, None, :], 0.0)
+    result = jnp.sum(spread_back, axis=(0, 1))
     return (normed, result.astype(jnp.bfloat16))
 
 

time: 68.5 us -> 65.2 us (0.952)
  blocking collectives: 14.3 us -> 0 us
  starting transfers between devices: 5.53 us -> 12.9 us
  waiting for transfers between devices: 21.4 us -> 23 us
  other arithmetic: 2.69 us -> 3.83 us
  local copies, waits for them, and re-layouts: 4.26 us -> 5.02 us
    all_to_all x1 -> x0, blocking collectives: 14.3 us -> none  [shards(): stats = lax.all_to_all(packed, 'shard', 0, 0, tiled=True)]
    all_to_all x0 -> x1, starting transfers between devices: none -> 7.38 us  [shards(): stats = lax.all_to_all(packed, 'shard', 0, 0, tiled=True)]
    all_to_all x0 -> x1, waiting for transfers between devices: none -> 6.61 us  [shards(): stats = lax.all_to_all(packed, 'shard', 0, 0, tiled=True)]
    all_to_all x1, waiting for transfers between devices: 12.9 us -> 7.89 us  [shards(): arrived = lax.all_to_all(blocks, ('grp', 'shard'), 0, 0, tiled=True)]
  transfers between devices with their start and end apart: 2 -> 3, of which waited for: 2 -> 3; matrix products, arithmetic and copies ran while one was open for 1% -> 2% of each run, Pallas kernels for 0% -> 0%
where the time goes in v4:
time: 65.2 us; the launch traced here: 64.8 us
  waiting for transfers between devices  23 us (35%)
  matrix products  19.2 us (29%)
  starting transfers between devices  12.9 us (20%)
  local copies, waits for them, and re-layouts  5.02 us (8%)
  other arithmetic  3.83 us (6%)
  between operations  0.87 us (1%)
    dot_general x1, matrix products, shards(): jnp.dot(hidden, w_down[local], preferred_element_type=jnp.float32)  11.5 us
    all_to_all x1, waiting for transfers between devices, shards(): lax.all_to_all(spread, ('grp', 'shard'), 0, 0, tiled=True)  8.52 us
    all_to_all x1, waiting for transfers between devices, shards(): arrived = lax.all_to_all(blocks, ('grp', 'shard'), 0, 0, tiled=True)  7.89 us
    all_to_all x1, starting transfers between devices, shards(): stats = lax.all_to_all(packed, 'shard', 0, 0, tiled=True)  7.38 us
    all_to_all x1, waiting for transfers between devices, shards(): stats = lax.all_to_all(packed, 'shard', 0, 0, tiled=True)  6.61 us
    dot_general x1, matrix products, shards(): jnp.dot(normed_all, w_gate[local], preferred_element_type=jnp.float32)  6.3 us
    all_to_all x1, starting transfers between devices, shards(): arrived = lax.all_to_all(blocks, ('grp', 'shard'), 0, 0, tiled=True)  2.95 us
    all_to_all x1, starting transfers between devices, shards(): lax.all_to_all(spread, ('grp', 'shard'), 0, 0, tiled=True)  2.58 us
  transfers between devices with their start and end apart: 3, of which 3 were waited for; matrix products, arithmetic and copies ran while one was open for 2% of the time, Pallas kernels for 0%

profile of v4, /device:TPU:0, one launch (start us, length us, event | category | flops | bytes accessed | tf_op | source)
XLA Modules:
  0.0 64.8 jit_solution(1972132333917243913)
XLA Ops:
  0.6 0.0 copy-start
  0.7 1.0 %reshape.263 = bf16[4,8,6,128]{3,2,1,0:T(8,128)(2,1)S(1)} reshape(bf16[4,6144]{1,0:T(4,128)(2,1)} %param.10) | data formatting | bytes 98304 | tf_op jit(solution)/shard_map/reshape | solution.py:38
  1.7 0.0 copy-start.1
  1.7 0.9 %broadcast_compare_fusion = pred[4,256]{1,0:T(4,128)(4,1)S(1)} fusion(s32[256]{0:T(256)S(1)} %iota_add_fusion, s32[4]{0:T(128)} %param.13), kind=kLoop, calls=%fused_computation.57 | loop fusion | flops 1024 | bytes 2064 | tf_op jit(solution)/shard_map/lt | solution.py:45
  2.6 0.0 copy-done
  2.6 0.7 %fusion.56 = (f32[4,8,6]{2,1,0:T(8,128)S(1)}, f32[4,8,6,256]{3,2,1,0:T(8,128)S(1)}) fusion(bf16[4,8,6,128]{3,2,1,0:T(8,128)(2,1)S(1)} %reshape.263, pred[4,256]{1,0:T(4,128)(4,1)S(1)} %broadcast_compare_fusion, bf16[4,256,1024]{2,1,0:T(8,128)(2,1)S(1)} %copy-done), kind=kOutput, calls=%fused_computation.72 | convolution fusion | flops 12730176 | bytes 2344704 | tf_op jit(solution)/shard_map/rgjd,rtgd->rgjt/dot_general | solution.py:41
  3.3 0.0 copy-start.2
  3.3 0.0 copy-start.3
  3.3 0.2 convert_reduce_fusion
  3.5 0.1 select_maximum_fusion
  3.6 0.0 copy-done.1
  3.6 0.4 fusion.27
  4.1 0.7 %copy.82 = f32[8,4,7,128]{3,1,2,0:T(4,128)} copy(f32[8,4,7,128]{3,2,0,1:T(8,128)S(1)} %maximum_bitcast_fusion) | data formatting | bytes 229376 | tf_op jit(solution)/shard_map/transpose | solution.py:71
  4.8 7.4 %all-to-all-start = ((f32[8,4,7,128]{3,1,2,0:T(4,128)}), f32[8,4,7,128]{3,1,2,0:T(4,128)S(1)}, u32[]{:S(2)}, u32[]{:S(2)}) async-start(f32[8,4,7,128]{3,1,2,0:T(4,128)} %copy.82), calls=%async_computation | async-start | bytes 229376 | tf_op jit(solution)/shard_map/all_to_all | solution.py:72
  12.2 0.0 copy-done.2
  12.2 0.0 copy-done.3
  12.3 0.1 and.34
  12.4 0.2 reduce_window_sum.23
  12.5 0.1 constant_dynamic-slice_fusion
  12.6 0.2 reduce_window_sum.22
  12.8 6.6 %all-to-all-done = f32[8,4,7,128]{3,1,2,0:T(4,128)S(1)} async-done(((f32[8,4,7,128]{3,1,2,0:T(4,128)}), f32[8,4,7,128]{3,1,2,0:T(4,128)S(1)}, u32[]{:S(2)}, u32[]{:S(2)}) %all-to-all-start) | async-done | bytes 114720 | tf_op jit(solution)/shard_map/all_to_all | solution.py:72
  19.5 0.1 fusion.46
  19.6 0.1 copy.84
  19.7 0.1 copy.85
  19.8 0.1 fusion.38
  19.9 0.1 fusion.48
  20.0 0.7 %broadcast_in_dim.116 = bf16[32,4,768]{2,1,0:T(4,128)(2,1)} broadcast(bf16[4,768]{1,0:T(4,128)(2,1)S(1)} %fusion.48), dimensions={1,2} | broadcast | bytes 202752 | tf_op jit(solution)/shard_map/broadcast_in_dim | solution.py:83
  20.7 2.6 %all-to-all-start.1 = ((bf16[32,4,768]{2,1,0:T(4,128)(2,1)}), bf16[32,4,768]{2,1,0:T(4,128)(2,1)S(1)}, u32[]{:S(2)}, u32[]{:S(2)}) async-start(bf16[32,4,768]{2,1,0:T(4,128)(2,1)} %broadcast_in_dim.116), calls=%async_computation.1 | async-start | bytes 393216 | tf_op jit(solution)/shard_map/all_to_all | solution.py:84
  23.3 8.5 %all-to-all-done.1 = bf16[32,4,768]{2,1,0:T(4,128)(2,1)S(1)} async-done(((bf16[32,4,768]{2,1,0:T(4,128)(2,1)}), bf16[32,4,768]{2,1,0:T(4,128)(2,1)S(1)}, u32[]{:S(2)}, u32[]{:S(2)}) %all-to-all-start.1) | async-done | bytes 196640 | tf_op jit(solution)/shard_map/all_to_all | solution.py:84
  31.9 0.1 copy.98
  32.1 0.1 multiply_reduce_fusion
  32.2 0.1 copy.88
  32.3 0.1 rsqrt.13
  32.4 0.1 multiply_convert_fusion.1
  32.5 0.0 copy-done.4
  32.5 0.2 fusion.57
  32.7 0.1 multiply_convert_fusion
  33.0 6.3 %fusion.4 = f32[16,1024]{1,0:T(8,128)S(1)} fusion(bf16[16,6144]{1,0:T(8,128)(2,1)S(1)} %bitcast.103, bf16[1,6144,1024]{2,1,0:T(8,128)(2,1)} %param.17), kind=kOutput, calls=%fused_computation.4 | convolution fusion | flops 201326592 | bytes 12845056 | tf_op jit(solution)/shard_map/dot_general | solution.py:107
  39.3 11.5 %fusion.6 = f32[16,6144]{1,0:T(8,128)S(1)} fusion(bf16[1,1024,6144]{2,1,0:T(8,128)(2,1)} %param.19, bf16[16,6144]{1,0:T(8,128)(2,1)S(1)} %bitcast.104, bf16[1,6144,1024]{2,1,0:T(8,128)(2,1)} %param.18, f32[16]{0:T(128)S(1)} %fusion.50, f32[16,1024]{1,0:T(8,128)S(1)} %fusion.4), kind=kOutput, calls=%fused_computation.6 | convolution fusion | flops 402849792 | bytes 25821248 | tf_op jit(solution)/shard_map/dot_general | solution.py:110
  50.8 0.1 broadcast_in_dim.122
  50.9 0.6 select_reduce_fusion
  51.6 0.2 reshape.268
  51.7 0.8 %copy.91 = f32[32,2,768]{2,1,0:T(2,128)} copy(f32[32,2,768]{2,0,1:T(8,128)S(1)} %bitcast.108) | data formatting | bytes 393216 | tf_op jit(solution)/shard_map/reshape | solution.py:118
  52.6 2.9 %all-to-all-start.2 = ((f32[32,2,768]{2,1,0:T(2,128)}), f32[32,2,768]{2,1,0:T(2,128)S(1)}, u32[]{:S(2)}, u32[]{:S(2)}) async-start(f32[32,2,768]{2,1,0:T(2,128)} %copy.91), calls=%async_computation.2 | async-start | bytes 393216 | tf_op jit(solution)/shard_map/all_to_all | solution.py:119
  55.5 0.7 %constant_dynamic-slice_fusion.1 = bf16[4,6144]{1,0:T(4,128)(2,1)} fusion(bf16[16,6144]{1,0:T(8,128)(2,1)S(1)} %multiply_convert_fusion.1, s32[]{:T(128)S(6)} %select_n.31), kind=kLoop, calls=%fused_computation.66 | loop fusion | bytes 98308 | tf_op jit(solution)/shard_map/dynamic_slice | solution.py:90
  56.2 7.9 %all-to-all-done.2 = f32[32,2,768]{2,1,0:T(2,128)S(1)} async-done(((f32[32,2,768]{2,1,0:T(2,128)}), f32[32,2,768]{2,1,0:T(2,128)S(1)}, u32[]{:S(2)}, u32[]{:S(2)}) %all-to-all-start.2) | async-done | bytes 196640 | tf_op jit(solution)/shard_map/all_to_all | solution.py:119
  64.1 0.1 bitcast_reduce_fusion
  64.1 0.7 %select_reduce_fusion.1 = bf16[4,768]{1,0:T(4,128)(2,1)} fusion(f32[4,2,768]{2,1,0:T(2,128)S(1)} %bitcast_reduce_fusion, pred[4,2,4]{2,1,0:T(4,128)(4,1)S(1)} %compare_and_fusion.1), kind=kLoop, calls=%fused_computation.32 | loop fusion | flops 46080 | bytes 30752 | tf_op jit(solution)/shard_map/reduce_sum | solution.py:124
  (23 shorter events, 0.4 us)
Async XLA Ops:
  0.6 1.9 %copy-start = (bf16[4,256,1024]{2,1,0:T(8,128)(2,1)S(1)}, bf16[4,256,1024]{2,1,0:T(8,128)(2,1)}, u32[]{:S(2)}) copy-start(bf16[4,256,1024]{2,1,0:T(8,128)(2,1)} %param.11) | copy-start | bytes 6291460
  1.7 1.9 %copy-start.1 = (bf16[4,256,1024]{2,1,0:T(8,128)(2,1)S(1)}, bf16[4,256,1024]{2,1,0:T(8,128)(2,1)}, u32[]{:S(2)}) copy-start(bf16[4,256,1024]{2,1,0:T(8,128)(2,1)} %param.12) | copy-start | bytes 6291460
  3.3 8.9 %copy-start.2 = (f32[6144]{0:T(1024)S(1)}, f32[6144]{0:T(1024)}, u32[]{:S(2)}) copy-start(f32[6144]{0:T(1024)} %param.14) | copy-start | bytes 73732
  3.3 8.9 %copy-start.3 = (s32[16,2]{0,1:T(2,128)S(1)}, s32[16,2]{0,1:T(2,128)}, u32[]{:S(2)}) copy-start(s32[16,2]{0,1:T(2,128)} %param.16) | copy-start | bytes 388
  4.8 27.7 %copy-start.4 = (bf16[6144,4]{0,1:T(4,128)(2,1)S(1)}, bf16[6144,4]{0,1:T(4,128)(2,1)}, u32[]{:S(2)}) copy-start(bf16[6144,4]{0,1:T(4,128)(2,1)} %param.15) | copy-start | bytes 147460
  4.8 14.6 %all-to-all-start = ((f32[8,4,7,128]{3,1,2,0:T(4,128)}), f32[8,4,7,128]{3,1,2,0:T(4,128)S(1)}, u32[]{:S(2)}, u32[]{:S(2)}) async-start(f32[8,4,7,128]{3,1,2,0:T(4,128)} %copy.82), calls=%async_computation | async-start | bytes 229376 | tf_op jit(solution)/shard_map/all_to_all | solution.py:72
  20.7 11.1 %all-to-all-start.1 = ((bf16[32,4,768]{2,1,0:T(4,128)(2,1)}), bf16[32,4,768]{2,1,0:T(4,128)(2,1)S(1)}, u32[]{:S(2)}, u32[]{:S(2)}) async-start(bf16[32,4,768]{2,1,0:T(4,128)(2,1)} %broadcast_in_dim.116), calls=%async_computation.1 | async-start | bytes 393216 | tf_op jit(solution)/shard_map/all_to_all | solution.py:84
  52.6 11.5 %all-to-all-start.2 = ((f32[32,2,768]{2,1,0:T(2,128)}), f32[32,2,768]{2,1,0:T(2,128)S(1)}, u32[]{:S(2)}, u32[]{:S(2)}) async-start(f32[32,2,768]{2,1,0:T(2,128)} %copy.91), calls=%async_computation.2 | async-start | bytes 393216 | tf_op jit(solution)/shard_map/all_to_all | solution.py:119

commit v5 on v4

--- a/solution.py
+++ b/solution.py
@@ -116,7 +116,8 @@
     picked = jnp.sum(jnp.where(sending[..., None], grouped, 0.0), axis=2)
     blocks = picked.reshape(n_grp, CAP, n_shard, out_width)
     blocks = jnp.transpose(blocks, (0, 2, 1, 3)).reshape(n_dev, CAP, out_width)
-    arrived = lax.all_to_all(blocks, ("grp", "shard"), 0, 0, tiled=True)
+    arrived = lax.all_to_all(blocks.astype(jnp.bfloat16), ("grp", "shard"), 0, 0, tiled=True)
+    arrived = arrived.astype(jnp.float32)
     per_expert = jnp.sum(arrived.reshape(n_grp, n_shard, CAP, out_width), axis=1)
     own_ids = lax.dynamic_slice_in_dim(expert_ids, grp_id * rows_here, rows_here, 0)
     homes = slot_match(own_ids, jnp.arange(n_grp, dtype=jnp.int32) * local_experts, rows_here, 1)[:, 0]

time: 65.2 us -> 64.1 us (0.983)
  waiting for transfers between devices: 23 us -> 22 us
    reshape x3 -> x0, local copies, waits for them, and re-layouts: 1 us -> none  [the longest x1 0.82 us: shards(): blocks = jnp.transpose(blocks, (0, 2, 1, 3)).reshape(n_dev, CAP, out_width)]
    all_to_all x1, waiting for transfers between devices: 7.89 us -> 6.9 us  [shards(): lax.all_to_all(blocks.astype(jnp.bfloat16), ('grp', 'shard'), 0, 0, tiled...]
    convert_element_type x0 -> x3, local copies, waits for them, and re-layouts: none -> 0.8 us  [shards(): blocks.astype(jnp.bfloat16)]
where the time goes in v5:
time: 64.1 us; the launch traced here: 63.7 us
  waiting for transfers between devices  22 us (34%)
  matrix products  19.2 us (30%)
  starting transfers between devices  12.9 us (20%)
  local copies, waits for them, and re-layouts  4.82 us (8%)
  other arithmetic  3.87 us (6%)
  between operations  0.87 us (1%)
    dot_general x1, matrix products, shards(): jnp.dot(hidden, w_down[local], preferred_element_type=jnp.float32)  11.5 us
    all_to_all x1, waiting for transfers between devices, shards(): lax.all_to_all(spread, ('grp', 'shard'), 0, 0, tiled=True)  8.52 us
    all_to_all x1, starting transfers between devices, shards(): stats = lax.all_to_all(packed, 'shard', 0, 0, tiled=True)  7.38 us
    all_to_all x1, waiting for transfers between devices, shards(): lax.all_to_all(blocks.astype(jnp.bfloat16), ('grp', 'shard'), 0, 0, tiled...  6.9 us
    all_to_all x1, waiting for transfers between devices, shards(): stats = lax.all_to_all(packed, 'shard', 0, 0, tiled=True)  6.61 us
    dot_general x1, matrix products, shards(): jnp.dot(normed_all, w_gate[local], preferred_element_type=jnp.float32)  6.3 us
    all_to_all x1, starting transfers between devices, shards(): lax.all_to_all(blocks.astype(jnp.bfloat16), ('grp', 'shard'), 0, 0, tiled...  2.95 us
    all_to_all x1, starting transfers between devices, shards(): lax.all_to_all(spread, ('grp', 'shard'), 0, 0, tiled=True)  2.58 us
  transfers between devices with their start and end apart: 3, of which 3 were waited for; matrix products, arithmetic and copies ran while one was open for 2% of the time, Pallas kernels for 0%

profile of v5, /device:TPU:0, one launch (start us, length us, event | category | flops | bytes accessed | tf_op | source)
XLA Modules:
  0.0 63.7 jit_solution(13962101609671001244)
XLA Ops:
  0.6 0.0 copy-start
  0.7 1.0 %reshape.264 = bf16[4,8,6,128]{3,2,1,0:T(8,128)(2,1)S(1)} reshape(bf16[4,6144]{1,0:T(4,128)(2,1)} %param.10) | data formatting | bytes 98304 | tf_op jit(solution)/shard_map/reshape | solution.py:38
  1.7 0.0 copy-start.1
  1.7 0.9 %broadcast_compare_fusion = pred[4,256]{1,0:T(4,128)(4,1)S(1)} fusion(s32[256]{0:T(256)S(1)} %iota_add_fusion, s32[4]{0:T(128)} %param.13), kind=kLoop, calls=%fused_computation.57 | loop fusion | flops 1024 | bytes 2064 | tf_op jit(solution)/shard_map/lt | solution.py:45
  2.6 0.0 copy-done
  2.6 0.7 %fusion.56 = (f32[4,8,6]{2,1,0:T(8,128)S(1)}, f32[4,8,6,256]{3,2,1,0:T(8,128)S(1)}) fusion(bf16[4,8,6,128]{3,2,1,0:T(8,128)(2,1)S(1)} %reshape.264, pred[4,256]{1,0:T(4,128)(4,1)S(1)} %broadcast_compare_fusion, bf16[4,256,1024]{2,1,0:T(8,128)(2,1)S(1)} %copy-done), kind=kOutput, calls=%fused_computation.72 | convolution fusion | flops 12730176 | bytes 2344704 | tf_op jit(solution)/shard_map/rgjd,rtgd->rgjt/dot_general | solution.py:41
  3.3 0.0 copy-start.2
  3.3 0.0 copy-start.3
  3.3 0.2 convert_reduce_fusion
  3.5 0.1 select_maximum_fusion
  3.6 0.0 copy-done.1
  3.6 0.4 fusion.27
  4.1 0.7 %copy.82 = f32[8,4,7,128]{3,1,2,0:T(4,128)} copy(f32[8,4,7,128]{3,2,0,1:T(8,128)S(1)} %maximum_bitcast_fusion) | data formatting | bytes 229376 | tf_op jit(solution)/shard_map/transpose | solution.py:71
  4.8 7.4 %all-to-all-start = ((f32[8,4,7,128]{3,1,2,0:T(4,128)}), f32[8,4,7,128]{3,1,2,0:T(4,128)S(1)}, u32[]{:S(2)}, u32[]{:S(2)}) async-start(f32[8,4,7,128]{3,1,2,0:T(4,128)} %copy.82), calls=%async_computation | async-start | bytes 229376 | tf_op jit(solution)/shard_map/all_to_all | solution.py:72
  12.2 0.0 copy-done.2
  12.2 0.0 copy-done.3
  12.3 0.1 and.34
  12.4 0.2 reduce_window_sum.23
  12.5 0.1 constant_dynamic-slice_fusion
  12.6 0.2 reduce_window_sum.22
  12.8 6.6 %all-to-all-done = f32[8,4,7,128]{3,1,2,0:T(4,128)S(1)} async-done(((f32[8,4,7,128]{3,1,2,0:T(4,128)}), f32[8,4,7,128]{3,1,2,0:T(4,128)S(1)}, u32[]{:S(2)}, u32[]{:S(2)}) %all-to-all-start) | async-done | bytes 114720 | tf_op jit(solution)/shard_map/all_to_all | solution.py:72
  19.5 0.1 fusion.46
  19.6 0.1 copy.84
  19.7 0.1 copy.85
  19.8 0.1 fusion.38
  19.9 0.1 fusion.48
  20.0 0.7 %broadcast_in_dim.116 = bf16[32,4,768]{2,1,0:T(4,128)(2,1)} broadcast(bf16[4,768]{1,0:T(4,128)(2,1)S(1)} %fusion.48), dimensions={1,2} | broadcast | bytes 202752 | tf_op jit(solution)/shard_map/broadcast_in_dim | solution.py:83
  20.7 2.6 %all-to-all-start.1 = ((bf16[32,4,768]{2,1,0:T(4,128)(2,1)}), bf16[32,4,768]{2,1,0:T(4,128)(2,1)S(1)}, u32[]{:S(2)}, u32[]{:S(2)}) async-start(bf16[32,4,768]{2,1,0:T(4,128)(2,1)} %broadcast_in_dim.116), calls=%async_computation.1 | async-start | bytes 393216 | tf_op jit(solution)/shard_map/all_to_all | solution.py:84
  23.3 8.5 %all-to-all-done.1 = bf16[32,4,768]{2,1,0:T(4,128)(2,1)S(1)} async-done(((bf16[32,4,768]{2,1,0:T(4,128)(2,1)}), bf16[32,4,768]{2,1,0:T(4,128)(2,1)S(1)}, u32[]{:S(2)}, u32[]{:S(2)}) %all-to-all-start.1) | async-done | bytes 196640 | tf_op jit(solution)/shard_map/all_to_all | solution.py:84
  31.9 0.1 copy.98
  32.1 0.1 multiply_reduce_fusion
  32.2 0.1 copy.88
  32.3 0.1 rsqrt.13
  32.4 0.1 multiply_convert_fusion.1
  32.5 0.0 copy-done.4
  32.5 0.2 fusion.57
  32.7 0.1 multiply_convert_fusion
  33.0 6.3 %fusion.4 = f32[16,1024]{1,0:T(8,128)S(1)} fusion(bf16[16,6144]{1,0:T(8,128)(2,1)S(1)} %bitcast.104, bf16[1,6144,1024]{2,1,0:T(8,128)(2,1)} %param.17), kind=kOutput, calls=%fused_computation.4 | convolution fusion | flops 201326592 | bytes 12845056 | tf_op jit(solution)/shard_map/dot_general | solution.py:107
  39.3 11.5 %fusion.6 = f32[16,6144]{1,0:T(8,128)S(1)} fusion(bf16[1,1024,6144]{2,1,0:T(8,128)(2,1)} %param.19, bf16[16,6144]{1,0:T(8,128)(2,1)S(1)} %bitcast.105, bf16[1,6144,1024]{2,1,0:T(8,128)(2,1)} %param.18, f32[16]{0:T(128)S(1)} %fusion.50, f32[16,1024]{1,0:T(8,128)S(1)} %fusion.4), kind=kOutput, calls=%fused_computation.6 | convolution fusion | flops 402849792 | bytes 25821248 | tf_op jit(solution)/shard_map/dot_general | solution.py:110
  50.8 0.1 broadcast_in_dim.122
  50.9 0.6 select_reduce_fusion
  51.6 0.1 convert_element_type.82
  51.7 0.7 %copy.91 = bf16[32,2,768]{2,1,0:T(2,128)(2,1)} copy(bf16[32,2,768]{2,0,1:T(8,128)(2,1)S(1)} %bitcast.109) | data formatting | bytes 196608 | tf_op jit(solution)/shard_map/convert_element_type | solution.py:119
  52.4 2.9 %all-to-all-start.2 = ((bf16[32,2,768]{2,1,0:T(2,128)(2,1)}), bf16[32,2,768]{2,1,0:T(2,128)(2,1)S(1)}, u32[]{:S(2)}, u32[]{:S(2)}) async-start(bf16[32,2,768]{2,1,0:T(2,128)(2,1)} %copy.91), calls=%async_computation.2 | async-start | bytes 196608 | tf_op jit(solution)/shard_map/all_to_all | solution.py:119
  55.3 0.7 %constant_dynamic-slice_fusion.1 = bf16[4,6144]{1,0:T(4,128)(2,1)} fusion(bf16[16,6144]{1,0:T(8,128)(2,1)S(1)} %multiply_convert_fusion.1, s32[]{:T(128)S(6)} %select_n.31), kind=kLoop, calls=%fused_computation.66 | loop fusion | bytes 98308 | tf_op jit(solution)/shard_map/dynamic_slice | solution.py:90
  56.0 6.9 %all-to-all-done.2 = bf16[32,2,768]{2,1,0:T(2,128)(2,1)S(1)} async-done(((bf16[32,2,768]{2,1,0:T(2,128)(2,1)}), bf16[32,2,768]{2,1,0:T(2,128)(2,1)S(1)}, u32[]{:S(2)}, u32[]{:S(2)}) %all-to-all-start.2) | async-done | bytes 98336 | tf_op jit(solution)/shard_map/all_to_all | solution.py:119
  62.9 0.1 convert_reduce_fusion.1
  63.0 0.7 %select_reduce_fusion.1 = bf16[4,768]{1,0:T(4,128)(2,1)} fusion(f32[4,2,768]{2,1,0:T(2,128)S(1)} %convert_reduce_fusion.1, pred[4,2,4]{2,1,0:T(4,128)(4,1)S(1)} %compare_and_fusion.1), kind=kLoop, calls=%fused_computation.32 | loop fusion | flops 46080 | bytes 30752 | tf_op jit(solution)/shard_map/reduce_sum | solution.py:125
  (23 shorter events, 0.4 us)
Async XLA Ops:
  0.6 1.9 %copy-start = (bf16[4,256,1024]{2,1,0:T(8,128)(2,1)S(1)}, bf16[4,256,1024]{2,1,0:T(8,128)(2,1)}, u32[]{:S(2)}) copy-start(bf16[4,256,1024]{2,1,0:T(8,128)(2,1)} %param.11) | copy-start | bytes 6291460
  1.7 1.9 %copy-start.1 = (bf16[4,256,1024]{2,1,0:T(8,128)(2,1)S(1)}, bf16[4,256,1024]{2,1,0:T(8,128)(2,1)}, u32[]{:S(2)}) copy-start(bf16[4,256,1024]{2,1,0:T(8,128)(2,1)} %param.12) | copy-start | bytes 6291460
  3.3 8.9 %copy-start.2 = (f32[6144]{0:T(1024)S(1)}, f32[6144]{0:T(1024)}, u32[]{:S(2)}) copy-start(f32[6144]{0:T(1024)} %param.14) | copy-start | bytes 73732
  3.3 8.9 %copy-start.3 = (s32[16,2]{0,1:T(2,128)S(1)}, s32[16,2]{0,1:T(2,128)}, u32[]{:S(2)}) copy-start(s32[16,2]{0,1:T(2,128)} %param.16) | copy-start | bytes 388
  4.8 27.7 %copy-start.4 = (bf16[6144,4]{0,1:T(4,128)(2,1)S(1)}, bf16[6144,4]{0,1:T(4,128)(2,1)}, u32[]{:S(2)}) copy-start(bf16[6144,4]{0,1:T(4,128)(2,1)} %param.15) | copy-start | bytes 147460
  4.8 14.6 %all-to-all-start = ((f32[8,4,7,128]{3,1,2,0:T(4,128)}), f32[8,4,7,128]{3,1,2,0:T(4,128)S(1)}, u32[]{:S(2)}, u32[]{:S(2)}) async-start(f32[8,4,7,128]{3,1,2,0:T(4,128)} %copy.82), calls=%async_computation | async-start | bytes 229376 | tf_op jit(solution)/shard_map/all_to_all | solution.py:72
  20.7 11.1 %all-to-all-start.1 = ((bf16[32,4,768]{2,1,0:T(4,128)(2,1)}), bf16[32,4,768]{2,1,0:T(4,128)(2,1)S(1)}, u32[]{:S(2)}, u32[]{:S(2)}) async-start(bf16[32,4,768]{2,1,0:T(4,128)(2,1)} %broadcast_in_dim.116), calls=%async_computation.1 | async-start | bytes 393216 | tf_op jit(solution)/shard_map/all_to_all | solution.py:84
  52.4 10.5 %all-to-all-start.2 = ((bf16[32,2,768]{2,1,0:T(2,128)(2,1)}), bf16[32,2,768]{2,1,0:T(2,128)(2,1)S(1)}, u32[]{:S(2)}, u32[]{:S(2)}) async-start(bf16[32,2,768]{2,1,0:T(2,128)(2,1)} %copy.91), calls=%async_computation.2 | async-start | bytes 196608 | tf_op jit(solution)/shard_map/all_to_all | solution.py:119

commit v6 on v5

--- a/solution.py
+++ b/solution.py
@@ -3,6 +3,8 @@
 import jax
 import jax.numpy as jnp
 from jax import lax
+from jax.experimental import pallas as pl
+from jax.experimental.pallas import tpu as pltpu
 from jax.sharding import PartitionSpec as P
 
 HEADS = 48
@@ -13,6 +15,48 @@
 
 NEG_FILL = -1e30
 CAP = 2
+
+
+FF_TILE = 256
+
+
+def expert_kernel(x_ref, gate_ref, up_ref, down_ref, coef_ref, out_ref, acc_ref):
+    step = pl.program_id(0)
+
+    @pl.when(step == 0)
+    def _():
+        acc_ref[...] = jnp.zeros_like(acc_ref)
+
+    rows = x_ref[...]
+    gate_proj = jnp.dot(rows, gate_ref[...], preferred_element_type=jnp.float32)
+    up_proj = jnp.dot(rows, up_ref[...], preferred_element_type=jnp.float32)
+    hidden = (jax.nn.silu(gate_proj) * up_proj).astype(jnp.bfloat16)
+    acc_ref[...] += jnp.dot(hidden, down_ref[...], preferred_element_type=jnp.float32)
+
+    @pl.when(step == pl.num_programs(0) - 1)
+    def _():
+        out_ref[...] = acc_ref[...] * coef_ref[...]
+
+
+def expert_ffn(rows, w_gate, w_up, w_down, local, coefficient):
+    n_rows, width = rows.shape
+    hidden_units = w_gate.shape[2]
+    tile = min(FF_TILE, hidden_units)
+    return pl.pallas_call(
+        expert_kernel,
+        grid=(hidden_units // tile,),
+        in_specs=[
+            pl.BlockSpec((n_rows, width), lambda f: (0, 0)),
+            pl.BlockSpec((None, width, tile), lambda f: (local, 0, f)),
+            pl.BlockSpec((None, width, tile), lambda f: (local, 0, f)),
+            pl.BlockSpec((None, tile, width), lambda f: (local, f, 0)),
+            pl.BlockSpec((n_rows, 1), lambda f: (0, 0)),
+        ],
+        out_specs=pl.BlockSpec((n_rows, width), lambda f: (0, 0)),
+        out_shape=jax.ShapeDtypeStruct((n_rows, width), jnp.float32),
+        scratch_shapes=[pltpu.VMEM((n_rows, width), jnp.float32)],
+        compiler_params=pltpu.CompilerParams(vmem_limit_bytes=48 * 1024 * 1024),
+    )(rows, w_gate, w_up, w_down, coefficient[:, None])
 
 
 def slot_match(expert_ids, experts, rows_here, n_groups):
@@ -100,15 +144,12 @@
     local_experts = w_gate.shape[0]
     assert local_experts == 1
     width = normed_all.shape[1]
-    total = jnp.zeros((n_grp * rows_here, width), jnp.float32)
+    total = None
     for local in range(local_experts):
         expert_index = grp_id * local_experts + local
         coefficient = jnp.sum(jnp.where(expert_ids == expert_index, route_weight, 0.0), axis=-1)
-        gate_proj = jnp.dot(normed_all, w_gate[local], preferred_element_type=jnp.float32)
-        up_proj = jnp.dot(normed_all, w_up[local], preferred_element_type=jnp.float32)
-        hidden = (jax.nn.silu(gate_proj) * up_proj).astype(jnp.bfloat16)
-        expert_y = jnp.dot(hidden, w_down[local], preferred_element_type=jnp.float32)
-        total = total + coefficient[:, None] * expert_y
+        contribution = expert_ffn(normed_all, w_gate, w_up, w_down, local, coefficient)
+        total = contribution if total is None else total + contribution
 
     out_width = width // n_shard
     sending = slot_match(expert_ids, (grp_id * local_experts)[None], rows_here, n_grp)[0]

time: 64.1 us -> 59.8 us (0.933)
  matrix products: 19.2 us -> 1.32 us
  Pallas kernels: 0 us -> 13.7 us
    dot_general x2 -> x0, matrix products: 17.8 us -> none  [the longest x1 11.5 us: shards(): jnp.dot(hidden, w_down[local], preferred_element_type=jnp.float32)]
    pallas_call x0 -> x1, Pallas kernels: none -> 13.7 us  [expert_ffn(): pl.pallas_call(expert_kernel, grid=(hidden_units // tile,), in_specs=[pl....]
where the time goes in v6:
time: 59.8 us; the launch traced here: 59.4 us
  waiting for transfers between devices  22.1 us (37%)
  Pallas kernels  13.7 us (23%)
  starting transfers between devices  12.9 us (22%)
  local copies, waits for them, and re-layouts  4.85 us (8%)
  other arithmetic  3.74 us (6%)
  matrix products  1.32 us (2%)
  between operations  0.85 us (1%)
    pallas_call x1, Pallas kernels, expert_ffn(): pl.pallas_call(expert_kernel, grid=(hidden_units // tile,), in_specs=[pl....  13.7 us
    all_to_all x1, waiting for transfers between devices, shards(): lax.all_to_all(spread, ('grp', 'shard'), 0, 0, tiled=True)  8.52 us
    all_to_all x1, starting transfers between devices, shards(): stats = lax.all_to_all(packed, 'shard', 0, 0, tiled=True)  7.38 us
    all_to_all x1, waiting for transfers between devices, shards(): lax.all_to_all(blocks.astype(jnp.bfloat16), ('grp', 'shard'), 0, 0, tiled...  6.9 us
    all_to_all x1, waiting for transfers between devices, shards(): stats = lax.all_to_all(packed, 'shard', 0, 0, tiled=True)  6.64 us
    all_to_all x1, starting transfers between devices, shards(): lax.all_to_all(blocks.astype(jnp.bfloat16), ('grp', 'shard'), 0, 0, tiled...  2.95 us
    all_to_all x1, starting transfers between devices, shards(): lax.all_to_all(spread, ('grp', 'shard'), 0, 0, tiled=True)  2.58 us
  transfers between devices with their start and end apart: 3, of which 3 were waited for; matrix products, arithmetic and copies ran while one was open for 2% of the time, Pallas kernels for 0%

profile of v6, /device:TPU:0, one launch (start us, length us, event | category | flops | bytes accessed | tf_op | source)
XLA Modules:
  0.0 59.4 jit_solution(61944565961987385)
XLA Ops:
  0.6 0.0 copy-start
  0.7 1.0 %reshape.243 = bf16[4,8,6,128]{3,2,1,0:T(8,128)(2,1)S(1)} reshape(bf16[4,6144]{1,0:T(4,128)(2,1)} %param.10) | data formatting | bytes 98304 | tf_op jit(solution)/shard_map/reshape | solution.py:82
  1.7 0.0 copy-start.1
  1.7 0.9 %broadcast_compare_fusion = pred[4,256]{1,0:T(4,128)(4,1)S(1)} fusion(s32[256]{0:T(256)S(1)} %iota_add_fusion, s32[4]{0:T(128)} %param.13), kind=kLoop, calls=%fused_computation.41 | loop fusion | flops 1024 | bytes 2064 | tf_op jit(solution)/shard_map/lt | solution.py:89
  2.6 0.0 copy-done
  2.6 0.7 %fusion.32 = (f32[4,8,6]{2,1,0:T(8,128)S(1)}, f32[4,8,6,256]{3,2,1,0:T(8,128)S(1)}) fusion(bf16[4,8,6,128]{3,2,1,0:T(8,128)(2,1)S(1)} %reshape.243, pred[4,256]{1,0:T(4,128)(4,1)S(1)} %broadcast_compare_fusion, bf16[4,256,1024]{2,1,0:T(8,128)(2,1)S(1)} %copy-done), kind=kOutput, calls=%fused_computation.55 | convolution fusion | flops 12730176 | bytes 2344704 | tf_op jit(solution)/shard_map/rgjd,rtgd->rgjt/dot_general | solution.py:85
  3.3 0.0 copy-start.3
  3.3 0.2 convert_reduce_fusion
  3.5 0.1 select_maximum_fusion
  3.6 0.0 copy-done.1
  3.6 0.4 fusion.18
  4.0 0.0 copy-start.2
  4.1 0.7 %copy.75 = f32[8,4,7,128]{3,1,2,0:T(4,128)} copy(f32[8,4,7,128]{3,2,0,1:T(8,128)S(1)} %maximum_bitcast_fusion) | data formatting | bytes 229376 | tf_op jit(solution)/shard_map/transpose | solution.py:115
  4.8 0.0 copy-start.4
  4.8 7.4 %all-to-all-start = ((f32[8,4,7,128]{3,1,2,0:T(4,128)}), f32[8,4,7,128]{3,1,2,0:T(4,128)S(1)}, u32[]{:S(2)}, u32[]{:S(2)}) async-start(f32[8,4,7,128]{3,1,2,0:T(4,128)} %copy.75), calls=%async_computation | async-start | bytes 229376 | tf_op jit(solution)/shard_map/all_to_all | solution.py:116
  12.2 0.0 copy-done.3
  12.2 0.1 and.34
  12.3 0.1 constant_dynamic-slice_fusion
  12.4 0.2 reduce_window_sum.22
  12.6 0.2 reduce_window_sum.23
  12.8 6.6 %all-to-all-done = f32[8,4,7,128]{3,1,2,0:T(4,128)S(1)} async-done(((f32[8,4,7,128]{3,1,2,0:T(4,128)}), f32[8,4,7,128]{3,1,2,0:T(4,128)S(1)}, u32[]{:S(2)}, u32[]{:S(2)}) %all-to-all-start) | async-done | bytes 114720 | tf_op jit(solution)/shard_map/all_to_all | solution.py:116
  19.5 0.1 fusion.23
  19.5 0.1 copy.78
  19.6 0.1 copy.77
  19.8 0.1 fusion.21
  19.9 0.1 fusion.25
  20.0 0.7 %broadcast_in_dim.118 = bf16[32,4,768]{2,1,0:T(4,128)(2,1)} broadcast(bf16[4,768]{1,0:T(4,128)(2,1)S(1)} %fusion.25), dimensions={1,2} | broadcast | bytes 202752 | tf_op jit(solution)/shard_map/broadcast_in_dim | solution.py:127
  20.7 2.6 %all-to-all-start.1 = ((bf16[32,4,768]{2,1,0:T(4,128)(2,1)}), bf16[32,4,768]{2,1,0:T(4,128)(2,1)S(1)}, u32[]{:S(2)}, u32[]{:S(2)}) async-start(bf16[32,4,768]{2,1,0:T(4,128)(2,1)} %broadcast_in_dim.118), calls=%async_computation.1 | async-start | bytes 393216 | tf_op jit(solution)/shard_map/all_to_all | solution.py:128
  23.3 8.5 %all-to-all-done.1 = bf16[32,4,768]{2,1,0:T(4,128)(2,1)S(1)} async-done(((bf16[32,4,768]{2,1,0:T(4,128)(2,1)}), bf16[32,4,768]{2,1,0:T(4,128)(2,1)S(1)}, u32[]{:S(2)}, u32[]{:S(2)}) %all-to-all-start.1) | async-done | bytes 196640 | tf_op jit(solution)/shard_map/all_to_all | solution.py:128
  31.9 0.1 multiply_reduce_fusion
  32.0 0.1 copy.81
  32.1 0.1 rsqrt.12
  32.3 0.1 copy.91
  32.4 0.0 copy-done.2
  32.4 0.1 multiply_convert_fusion.x_ref
  32.5 0.0 copy-done.4
  32.5 0.2 fusion.33
  32.8 0.1 copy.82.coef_ref
  32.9 13.7 %shard_map.113 = f32[16,6144]{1,0:T(8,128)S(1)} custom-call(bf16[16,6144]{1,0:T(8,128)(2,1)S(1)} %multiply_convert_fusion.x_ref, bf16[1,6144,1024]{2,1,0:T(8,128)(2,1)} %gate_ref.1, bf16[1,6144,1024]{2,1,0:T(8,128)(2,1)} %up_ref.1, bf16[1,1024,6144]{2,1,0:T(8,128)(2,1)} %down_ref.1, f32[16,1]{1,0:T(8,128)S(1)} %copy.82.coef_ref), custom_call_target="tpu_custom_call" | custom-call | tf_op jit(solution)/shard_map/pallas_call | solution.py:45
  46.5 0.1 broadcast_in_dim.125
  46.7 0.6 %select_reduce_fusion = bf16[4,2,6144]{2,1,0:T(2,128)(2,1)S(1)} fusion(f32[4,4,6144]{2,1,0:T(4,128)S(1)} %broadcast_in_dim.125, pred[4,2,4]{2,1,0:T(4,128)(4,1)S(1)} %compare_and_fusion), kind=kLoop, calls=%fused_computation.11 | loop fusion | flops 344064 | bytes 491552 | tf_op jit(solution)/shard_map/reduce_sum | solution.py:157
  47.3 0.1 convert_element_type.70
  47.4 0.7 %copy.84 = bf16[32,2,768]{2,1,0:T(2,128)(2,1)} copy(bf16[32,2,768]{2,0,1:T(8,128)(2,1)S(1)} %bitcast.83) | data formatting | bytes 196608 | tf_op jit(solution)/shard_map/convert_element_type | solution.py:160
  48.1 2.9 %all-to-all-start.2 = ((bf16[32,2,768]{2,1,0:T(2,128)(2,1)}), bf16[32,2,768]{2,1,0:T(2,128)(2,1)S(1)}, u32[]{:S(2)}, u32[]{:S(2)}) async-start(bf16[32,2,768]{2,1,0:T(2,128)(2,1)} %copy.84), calls=%async_computation.2 | async-start | bytes 196608 | tf_op jit(solution)/shard_map/all_to_all | solution.py:160
  51.1 0.7 %constant_dynamic-slice_fusion.1 = bf16[4,6144]{1,0:T(4,128)(2,1)} fusion(bf16[16,6144]{1,0:T(8,128)(2,1)S(1)} %multiply_convert_fusion.x_ref, s32[]{:T(128)S(6)} %select_n.31), kind=kLoop, calls=%fused_computation.50 | loop fusion | bytes 98308 | tf_op jit(solution)/shard_map/dynamic_slice | solution.py:134
  51.7 6.9 %all-to-all-done.2 = bf16[32,2,768]{2,1,0:T(2,128)(2,1)S(1)} async-done(((bf16[32,2,768]{2,1,0:T(2,128)(2,1)}), bf16[32,2,768]{2,1,0:T(2,128)(2,1)S(1)}, u32[]{:S(2)}, u32[]{:S(2)}) %all-to-all-start.2) | async-done | bytes 98336 | tf_op jit(solution)/shard_map/all_to_all | solution.py:160
  58.6 0.1 convert_reduce_fusion.1
  58.7 0.7 %select_reduce_fusion.1 = bf16[4,768]{1,0:T(4,128)(2,1)} fusion(f32[4,2,768]{2,1,0:T(2,128)S(1)} %convert_reduce_fusion.1, pred[4,2,4]{2,1,0:T(4,128)(4,1)S(1)} %compare_and_fusion.1), kind=kLoop, calls=%fused_computation.22 | loop fusion | flops 46080 | bytes 30752 | tf_op jit(solution)/shard_map/reduce_sum | solution.py:166
  (19 shorter events, 0.3 us)
Async XLA Ops:
  0.6 1.9 %copy-start = (bf16[4,256,1024]{2,1,0:T(8,128)(2,1)S(1)}, bf16[4,256,1024]{2,1,0:T(8,128)(2,1)}, u32[]{:S(2)}) copy-start(bf16[4,256,1024]{2,1,0:T(8,128)(2,1)} %param.11) | copy-start | bytes 6291460
  1.7 1.9 %copy-start.1 = (bf16[4,256,1024]{2,1,0:T(8,128)(2,1)S(1)}, bf16[4,256,1024]{2,1,0:T(8,128)(2,1)}, u32[]{:S(2)}) copy-start(bf16[4,256,1024]{2,1,0:T(8,128)(2,1)} %param.12) | copy-start | bytes 6291460
  3.3 8.9 %copy-start.3 = (s32[16,2]{0,1:T(2,128)S(1)}, s32[16,2]{0,1:T(2,128)}, u32[]{:S(2)}) copy-start(s32[16,2]{0,1:T(2,128)} %param.16) | copy-start | bytes 388
  4.0 28.4 %copy-start.2 = (f32[6144]{0:T(1024)S(1)}, f32[6144]{0:T(1024)}, u32[]{:S(2)}) copy-start(f32[6144]{0:T(1024)} %param.14) | copy-start | bytes 73732
  4.8 27.7 %copy-start.4 = (bf16[6144,4]{0,1:T(4,128)(2,1)S(1)}, bf16[6144,4]{0,1:T(4,128)(2,1)}, u32[]{:S(2)}) copy-start(bf16[6144,4]{0,1:T(4,128)(2,1)} %param.15) | copy-start | bytes 147460
  4.8 14.6 %all-to-all-start = ((f32[8,4,7,128]{3,1,2,0:T(4,128)}), f32[8,4,7,128]{3,1,2,0:T(4,128)S(1)}, u32[]{:S(2)}, u32[]{:S(2)}) async-start(f32[8,4,7,128]{3,1,2,0:T(4,128)} %copy.75), calls=%async_computation | async-start | bytes 229376 | tf_op jit(solution)/shard_map/all_to_all | solution.py:116
  20.7 11.1 %all-to-all-start.1 = ((bf16[32,4,768]{2,1,0:T(4,128)(2,1)}), bf16[32,4,768]{2,1,0:T(4,128)(2,1)S(1)}, u32[]{:S(2)}, u32[]{:S(2)}) async-start(bf16[32,4,768]{2,1,0:T(4,128)(2,1)} %broadcast_in_dim.118), calls=%async_computation.1 | async-start | bytes 393216 | tf_op jit(solution)/shard_map/all_to_all | solution.py:128
  48.1 10.5 %all-to-all-start.2 = ((bf16[32,2,768]{2,1,0:T(2,128)(2,1)}), bf16[32,2,768]{2,1,0:T(2,128)(2,1)S(1)}, u32[]{:S(2)}, u32[]{:S(2)}) async-start(bf16[32,2,768]{2,1,0:T(2,128)(2,1)} %copy.84), calls=%async_computation.2 | async-start | bytes 196608 | tf_op jit(solution)/shard_map/all_to_all | solution.py:160

commit v7 on v6

--- a/solution.py
+++ b/solution.py
@@ -20,7 +20,7 @@
 FF_TILE = 256
 
 
-def expert_kernel(x_ref, gate_ref, up_ref, down_ref, coef_ref, out_ref, acc_ref):
+def expert_kernel(x_ref, gate_ref, up_ref, down_ref, sel_ref, out_ref, acc_ref):
     step = pl.program_id(0)
 
     @pl.when(step == 0)
@@ -35,11 +35,16 @@
 
     @pl.when(step == pl.num_programs(0) - 1)
     def _():
-        out_ref[...] = acc_ref[...] * coef_ref[...]
+        picked = jnp.dot(
+            sel_ref[...], acc_ref[...], precision=lax.Precision.HIGHEST,
+            preferred_element_type=jnp.float32,
+        )
+        out_ref[...] = picked.astype(out_ref.dtype)
 
 
-def expert_ffn(rows, w_gate, w_up, w_down, local, coefficient):
+def expert_ffn(rows, w_gate, w_up, w_down, local, select):
     n_rows, width = rows.shape
+    n_out = select.shape[0]
     hidden_units = w_gate.shape[2]
     tile = min(FF_TILE, hidden_units)
     return pl.pallas_call(
@@ -50,13 +55,13 @@
             pl.BlockSpec((None, width, tile), lambda f: (local, 0, f)),
             pl.BlockSpec((None, width, tile), lambda f: (local, 0, f)),
             pl.BlockSpec((None, tile, width), lambda f: (local, f, 0)),
-            pl.BlockSpec((n_rows, 1), lambda f: (0, 0)),
+            pl.BlockSpec((n_out, n_rows), lambda f: (0, 0)),
         ],
-        out_specs=pl.BlockSpec((n_rows, width), lambda f: (0, 0)),
-        out_shape=jax.ShapeDtypeStruct((n_rows, width), jnp.float32),
+        out_specs=pl.BlockSpec((n_out, width), lambda f: (0, 0)),
+        out_shape=jax.ShapeDtypeStruct((n_out, width), jnp.bfloat16),
         scratch_shapes=[pltpu.VMEM((n_rows, width), jnp.float32)],
         compiler_params=pltpu.CompilerParams(vmem_limit_bytes=48 * 1024 * 1024),
-    )(rows, w_gate, w_up, w_down, coefficient[:, None])
+    )(rows, w_gate, w_up, w_down, select)
 
 
 def slot_match(expert_ids, experts, rows_here, n_groups):
@@ -144,22 +149,25 @@
     local_experts = w_gate.shape[0]
     assert local_experts == 1
     width = normed_all.shape[1]
-    total = None
-    for local in range(local_experts):
-        expert_index = grp_id * local_experts + local
-        coefficient = jnp.sum(jnp.where(expert_ids == expert_index, route_weight, 0.0), axis=-1)
-        contribution = expert_ffn(normed_all, w_gate, w_up, w_down, local, coefficient)
-        total = contribution if total is None else total + contribution
-
     out_width = width // n_shard
-    sending = slot_match(expert_ids, (grp_id * local_experts)[None], rows_here, n_grp)[0]
-    grouped = total.reshape(n_grp, 1, rows_here, width)
-    picked = jnp.sum(jnp.where(sending[..., None], grouped, 0.0), axis=2)
-    blocks = picked.reshape(n_grp, CAP, n_shard, out_width)
-    blocks = jnp.transpose(blocks, (0, 2, 1, 3)).reshape(n_dev, CAP, out_width)
-    arrived = lax.all_to_all(blocks.astype(jnp.bfloat16), ("grp", "shard"), 0, 0, tiled=True)
-    arrived = arrived.astype(jnp.float32)
-    per_expert = jnp.sum(arrived.reshape(n_grp, n_shard, CAP, out_width), axis=1)
+    expert_index = grp_id
+    coefficient = jnp.sum(jnp.where(expert_ids == expert_index, route_weight, 0.0), axis=-1)
+    sending = slot_match(expert_ids, expert_index[None], rows_here, n_grp)[0]
+    row_of = jnp.arange(n_grp * rows_here, dtype=jnp.int32).reshape(n_grp, 1, rows_here)
+    select = jnp.sum(
+        jnp.where(
+            sending[..., None] & (row_of[..., None] == jnp.arange(n_grp * rows_here)[None, None, None, :]),
+            coefficient[None, None, None, :],
+            0.0,
+        ),
+        axis=2,
+    )
+    select = jnp.transpose(select, (1, 0, 2)).reshape(CAP * n_grp, n_grp * rows_here)
+    picked = expert_ffn(normed_all, w_gate, w_up, w_down, 0, select)
+    blocks = picked.reshape(CAP, n_dev, out_width)
+    arrived = lax.all_to_all(blocks, ("grp", "shard"), 1, 1, tiled=True)
+    arrived = arrived.astype(jnp.float32).reshape(CAP, n_grp, n_shard, out_width)
+    per_expert = jnp.transpose(jnp.sum(arrived, axis=2), (1, 0, 2))
     own_ids = lax.dynamic_slice_in_dim(expert_ids, grp_id * rows_here, rows_here, 0)
     homes = slot_match(own_ids, jnp.arange(n_grp, dtype=jnp.int32) * local_experts, rows_here, 1)[:, 0]
     spread_back = jnp.where(homes[..., None], per_expert[:, :, None, :], 0.0)

time: 59.8 us -> 59.5 us (level)
    convert_element_type x3 -> x0, local copies, waits for them, and re-layouts: 0.8 us -> none  [shards(): blocks.astype(jnp.bfloat16)]
    reshape x0 -> x2, local copies, waits for them, and re-layouts: none -> 0.79 us  [shards(): blocks = picked.reshape(CAP, n_dev, out_width)]
where the time goes in v7:
time: 59.5 us; the launch traced here: 59.1 us
  waiting for transfers between devices  22 us (37%)
  Pallas kernels  14 us (24%)
  starting transfers between devices  12.9 us (22%)
  local copies, waits for them, and re-layouts  4.67 us (8%)
  other arithmetic  3.3 us (6%)
  matrix products  1.32 us (2%)
  between operations  0.86 us (1%)
    pallas_call x1, Pallas kernels, expert_ffn(): pl.pallas_call(expert_kernel, grid=(hidden_units // tile,), in_specs=[pl....  14 us
    all_to_all x1, waiting for transfers between devices, shards(): lax.all_to_all(spread, ('grp', 'shard'), 0, 0, tiled=True)  8.46 us
    all_to_all x1, starting transfers between devices, shards(): stats = lax.all_to_all(packed, 'shard', 0, 0, tiled=True)  7.38 us
    all_to_all x1, waiting for transfers between devices, shards(): arrived = lax.all_to_all(blocks, ('grp', 'shard'), 1, 1, tiled=True)  6.9 us
    all_to_all x1, waiting for transfers between devices, shards(): stats = lax.all_to_all(packed, 'shard', 0, 0, tiled=True)  6.61 us
    all_to_all x1, starting transfers between devices, shards(): arrived = lax.all_to_all(blocks, ('grp', 'shard'), 1, 1, tiled=True)  2.95 us
    all_to_all x1, starting transfers between devices, shards(): lax.all_to_all(spread, ('grp', 'shard'), 0, 0, tiled=True)  2.58 us
  transfers between devices with their start and end apart: 3, of which 3 were waited for; matrix products, arithmetic and copies ran while one was open for 2% of the time, Pallas kernels for 0%

profile of v7, /device:TPU:0, one launch (start us, length us, event | category | flops | bytes accessed | tf_op | source)
XLA Modules:
  0.0 59.1 jit_solution(7160969630392439084)
XLA Ops:
  0.6 0.0 copy-start
  0.7 1.0 %reshape.264 = bf16[4,8,6,128]{3,2,1,0:T(8,128)(2,1)S(1)} reshape(bf16[4,6144]{1,0:T(4,128)(2,1)} %param.10) | data formatting | bytes 98304 | tf_op jit(solution)/shard_map/reshape | solution.py:87
  1.7 0.0 copy-start.1
  1.7 0.9 %broadcast_compare_fusion = pred[4,256]{1,0:T(4,128)(4,1)S(1)} fusion(s32[256]{0:T(256)S(1)} %iota_add_fusion, s32[4]{0:T(128)} %param.13), kind=kLoop, calls=%fused_computation.43 | loop fusion | flops 1024 | bytes 2064 | tf_op jit(solution)/shard_map/lt | solution.py:94
  2.6 0.0 copy-done
  2.6 0.7 %fusion.32 = (f32[4,8,6]{2,1,0:T(8,128)S(1)}, f32[4,8,6,256]{3,2,1,0:T(8,128)S(1)}) fusion(bf16[4,8,6,128]{3,2,1,0:T(8,128)(2,1)S(1)} %reshape.264, pred[4,256]{1,0:T(4,128)(4,1)S(1)} %broadcast_compare_fusion, bf16[4,256,1024]{2,1,0:T(8,128)(2,1)S(1)} %copy-done), kind=kOutput, calls=%fused_computation.57 | convolution fusion | flops 12730176 | bytes 2344704 | tf_op jit(solution)/shard_map/rgjd,rtgd->rgjt/dot_general | solution.py:90
  3.3 0.0 copy-start.3
  3.3 0.2 convert_reduce_fusion
  3.5 0.1 select_maximum_fusion
  3.6 0.0 copy-done.1
  3.6 0.4 fusion.18
  4.0 0.0 copy-start.2
  4.1 0.7 %copy.70 = f32[8,4,7,128]{3,1,2,0:T(4,128)} copy(f32[8,4,7,128]{3,2,0,1:T(8,128)S(1)} %maximum_bitcast_fusion) | data formatting | bytes 229376 | tf_op jit(solution)/shard_map/transpose | solution.py:120
  4.8 0.0 copy-start.4
  4.8 7.4 %all-to-all-start = ((f32[8,4,7,128]{3,1,2,0:T(4,128)}), f32[8,4,7,128]{3,1,2,0:T(4,128)S(1)}, u32[]{:S(2)}, u32[]{:S(2)}) async-start(f32[8,4,7,128]{3,1,2,0:T(4,128)} %copy.70), calls=%async_computation | async-start | bytes 229376 | tf_op jit(solution)/shard_map/all_to_all | solution.py:121
  12.2 0.0 copy-done.3
  12.2 0.1 and.47
  12.3 0.1 constant_dynamic-slice_fusion
  12.4 0.2 reduce_window_sum.22
  12.6 0.2 reduce_window_sum.23
  12.8 6.6 %all-to-all-done = f32[8,4,7,128]{3,1,2,0:T(4,128)S(1)} async-done(((f32[8,4,7,128]{3,1,2,0:T(4,128)}), f32[8,4,7,128]{3,1,2,0:T(4,128)S(1)}, u32[]{:S(2)}, u32[]{:S(2)}) %all-to-all-start) | async-done | bytes 114720 | tf_op jit(solution)/shard_map/all_to_all | solution.py:121
  19.5 0.1 fusion.23
  19.5 0.1 copy.73
  19.6 0.1 copy.72
  19.8 0.1 fusion.21
  19.9 0.1 fusion.25
  20.0 0.7 %broadcast_in_dim.107 = bf16[32,4,768]{2,1,0:T(4,128)(2,1)} broadcast(bf16[4,768]{1,0:T(4,128)(2,1)S(1)} %fusion.25), dimensions={1,2} | broadcast | bytes 202752 | tf_op jit(solution)/shard_map/broadcast_in_dim | solution.py:132
  20.7 2.6 %all-to-all-start.1 = ((bf16[32,4,768]{2,1,0:T(4,128)(2,1)}), bf16[32,4,768]{2,1,0:T(4,128)(2,1)S(1)}, u32[]{:S(2)}, u32[]{:S(2)}) async-start(bf16[32,4,768]{2,1,0:T(4,128)(2,1)} %broadcast_in_dim.107), calls=%async_computation.1 | async-start | bytes 393216 | tf_op jit(solution)/shard_map/all_to_all | solution.py:133
  23.3 0.1 iota_compare_fusion.1
  23.4 8.5 %all-to-all-done.1 = bf16[32,4,768]{2,1,0:T(4,128)(2,1)S(1)} async-done(((bf16[32,4,768]{2,1,0:T(4,128)(2,1)}), bf16[32,4,768]{2,1,0:T(4,128)(2,1)S(1)}, u32[]{:S(2)}, u32[]{:S(2)}) %all-to-all-start.1) | async-done | bytes 196640 | tf_op jit(solution)/shard_map/all_to_all | solution.py:133
  31.9 0.1 multiply_reduce_fusion
  32.0 0.1 copy.76
  32.1 0.1 rsqrt.12
  32.3 0.1 copy.85
  32.4 0.0 copy-done.2
  32.4 0.1 multiply_convert_fusion.x_ref
  32.5 0.0 copy-done.4
  32.5 0.2 fusion.33
  32.8 0.1 select_reduce_fusion.1
  32.9 14.0 %shard_map.113 = bf16[8,6144]{1,0:T(8,128)(2,1)S(1)} custom-call(bf16[16,6144]{1,0:T(8,128)(2,1)S(1)} %multiply_convert_fusion.x_ref, bf16[1,6144,1024]{2,1,0:T(8,128)(2,1)} %gate_ref.1, bf16[1,6144,1024]{2,1,0:T(8,128)(2,1)} %up_ref.1, bf16[1,1024,6144]{2,1,0:T(8,128)(2,1)} %down_ref.1, f32[8,16]{1,0:T(8,128)S(1)} %bitcast.80), custom_call_target="tpu_custom_call" | custom-call | tf_op jit(solution)/shard_map/pallas_call | solution.py:50
  46.9 0.1 reshape.270
  47.0 0.7 %copy.78 = bf16[2,32,768]{2,0,1:T(2,128)(2,1)} copy(bf16[2,32,768]{2,1,0:T(8,128)(2,1)S(1)} %reshape.270) | data formatting | bytes 196608 | tf_op jit(solution)/shard_map/reshape | solution.py:167
  47.7 2.9 %all-to-all-start.2 = ((bf16[2,32,768]{2,0,1:T(2,128)(2,1)}), bf16[2,32,768]{2,0,1:T(2,128)(2,1)S(1)}, u32[]{:S(2)}, u32[]{:S(2)}) async-start(bf16[2,32,768]{2,0,1:T(2,128)(2,1)} %copy.78), calls=%async_computation.2 | async-start | bytes 196608 | tf_op jit(solution)/shard_map/all_to_all | solution.py:168
  50.7 0.7 %constant_dynamic-slice_fusion.1 = bf16[4,6144]{1,0:T(4,128)(2,1)} fusion(bf16[16,6144]{1,0:T(8,128)(2,1)S(1)} %multiply_convert_fusion.x_ref, s32[]{:T(128)S(6)} %select_n.31), kind=kLoop, calls=%fused_computation.52 | loop fusion | bytes 98308 | tf_op jit(solution)/shard_map/dynamic_slice | solution.py:139
  51.4 6.9 %all-to-all-done.2 = bf16[2,32,768]{2,0,1:T(2,128)(2,1)S(1)} async-done(((bf16[2,32,768]{2,0,1:T(2,128)(2,1)}), bf16[2,32,768]{2,0,1:T(2,128)(2,1)S(1)}, u32[]{:S(2)}, u32[]{:S(2)}) %all-to-all-start.2) | async-done | bytes 98336 | tf_op jit(solution)/shard_map/all_to_all | solution.py:168
  58.3 0.1 convert_reduce_fusion.1
  58.4 0.7 %select_reduce_fusion = bf16[4,768]{1,0:T(4,128)(2,1)} fusion(f32[4,2,768]{2,1,0:T(2,128)S(1)} %copy.80, pred[4,2,4]{2,1,0:T(4,128)(4,1)S(1)} %compare_and_fusion.1), kind=kLoop, calls=%fused_computation.20 | loop fusion | flops 46080 | bytes 30752 | tf_op jit(solution)/shard_map/reduce_sum | solution.py:174
  (22 shorter events, 0.3 us)
Async XLA Ops:
  0.6 1.9 %copy-start = (bf16[4,256,1024]{2,1,0:T(8,128)(2,1)S(1)}, bf16[4,256,1024]{2,1,0:T(8,128)(2,1)}, u32[]{:S(2)}) copy-start(bf16[4,256,1024]{2,1,0:T(8,128)(2,1)} %param.11) | copy-start | bytes 6291460
  1.7 1.9 %copy-start.1 = (bf16[4,256,1024]{2,1,0:T(8,128)(2,1)S(1)}, bf16[4,256,1024]{2,1,0:T(8,128)(2,1)}, u32[]{:S(2)}) copy-start(bf16[4,256,1024]{2,1,0:T(8,128)(2,1)} %param.12) | copy-start | bytes 6291460
  3.3 8.9 %copy-start.3 = (s32[16,2]{0,1:T(2,128)S(1)}, s32[16,2]{0,1:T(2,128)}, u32[]{:S(2)}) copy-start(s32[16,2]{0,1:T(2,128)} %param.16) | copy-start | bytes 388
  4.0 28.4 %copy-start.2 = (f32[6144]{0:T(1024)S(1)}, f32[6144]{0:T(1024)}, u32[]{:S(2)}) copy-start(f32[6144]{0:T(1024)} %param.14) | copy-start | bytes 73732
  4.8 27.7 %copy-start.4 = (bf16[6144,4]{0,1:T(4,128)(2,1)S(1)}, bf16[6144,4]{0,1:T(4,128)(2,1)}, u32[]{:S(2)}) copy-start(bf16[6144,4]{0,1:T(4,128)(2,1)} %param.15) | copy-start | bytes 147460
  4.8 14.6 %all-to-all-start = ((f32[8,4,7,128]{3,1,2,0:T(4,128)}), f32[8,4,7,128]{3,1,2,0:T(4,128)S(1)}, u32[]{:S(2)}, u32[]{:S(2)}) async-start(f32[8,4,7,128]{3,1,2,0:T(4,128)} %copy.70), calls=%async_computation | async-start | bytes 229376 | tf_op jit(solution)/shard_map/all_to_all | solution.py:121
  20.7 11.1 %all-to-all-start.1 = ((bf16[32,4,768]{2,1,0:T(4,128)(2,1)}), bf16[32,4,768]{2,1,0:T(4,128)(2,1)S(1)}, u32[]{:S(2)}, u32[]{:S(2)}) async-start(bf16[32,4,768]{2,1,0:T(4,128)(2,1)} %broadcast_in_dim.107), calls=%async_computation.1 | async-start | bytes 393216 | tf_op jit(solution)/shard_map/all_to_all | solution.py:133
  47.7 10.5 %all-to-all-start.2 = ((bf16[2,32,768]{2,0,1:T(2,128)(2,1)}), bf16[2,32,768]{2,0,1:T(2,128)(2,1)S(1)}, u32[]{:S(2)}, u32[]{:S(2)}) async-start(bf16[2,32,768]{2,0,1:T(2,128)(2,1)} %copy.78), calls=%async_computation.2 | async-start | bytes 196608 | tf_op jit(solution)/shard_map/all_to_all | solution.py:168

commit v8 on v7

--- a/solution.py
+++ b/solution.py
@@ -38,13 +38,22 @@
         picked = jnp.dot(
             sel_ref[...], acc_ref[...], precision=lax.Precision.HIGHEST,
             preferred_element_type=jnp.float32,
-        )
-        out_ref[...] = picked.astype(out_ref.dtype)
-
-
-def expert_ffn(rows, w_gate, w_up, w_down, local, select):
+        ).astype(out_ref.dtype)
+        n_dev, slots, out_width = out_ref.shape
+        n_groups = sel_ref.shape[0] // slots
+        n_cols = n_dev // n_groups
+        for slot in range(slots):
+            for group in range(n_groups):
+                for col in range(n_cols):
+                    out_ref[group * n_cols + col, slot, :] = picked[
+                        slot * n_groups + group, col * out_width : (col + 1) * out_width
+                    ]
+
+
+def expert_ffn(rows, w_gate, w_up, w_down, local, select, n_dev):
     n_rows, width = rows.shape
-    n_out = select.shape[0]
+    slots = CAP
+    out_width = width * select.shape[0] // (slots * n_dev)
     hidden_units = w_gate.shape[2]
     tile = min(FF_TILE, hidden_units)
     return pl.pallas_call(
@@ -55,10 +64,10 @@
             pl.BlockSpec((None, width, tile), lambda f: (local, 0, f)),
             pl.BlockSpec((None, width, tile), lambda f: (local, 0, f)),
             pl.BlockSpec((None, tile, width), lambda f: (local, f, 0)),
-            pl.BlockSpec((n_out, n_rows), lambda f: (0, 0)),
+            pl.BlockSpec(select.shape, lambda f: (0, 0)),
         ],
-        out_specs=pl.BlockSpec((n_out, width), lambda f: (0, 0)),
-        out_shape=jax.ShapeDtypeStruct((n_out, width), jnp.bfloat16),
+        out_specs=pl.BlockSpec((n_dev, slots, out_width), lambda f: (0, 0, 0)),
+        out_shape=jax.ShapeDtypeStruct((n_dev, slots, out_width), jnp.bfloat16),
         scratch_shapes=[pltpu.VMEM((n_rows, width), jnp.float32)],
         compiler_params=pltpu.CompilerParams(vmem_limit_bytes=48 * 1024 * 1024),
     )(rows, w_gate, w_up, w_down, select)
@@ -163,11 +172,10 @@
         axis=2,
     )
     select = jnp.transpose(select, (1, 0, 2)).reshape(CAP * n_grp, n_grp * rows_here)
-    picked = expert_ffn(normed_all, w_gate, w_up, w_down, 0, select)
-    blocks = picked.reshape(CAP, n_dev, out_width)
-    arrived = lax.all_to_all(blocks, ("grp", "shard"), 1, 1, tiled=True)
-    arrived = arrived.astype(jnp.float32).reshape(CAP, n_grp, n_shard, out_width)
-    per_expert = jnp.transpose(jnp.sum(arrived, axis=2), (1, 0, 2))
+    blocks = expert_ffn(normed_all, w_gate, w_up, w_down, 0, select, n_dev)
+    arrived = lax.all_to_all(blocks, ("grp", "shard"), 0, 0, tiled=True)
+    arrived = arrived.astype(jnp.float32).reshape(n_grp, n_shard, CAP, out_width)
+    per_expert = jnp.sum(arrived, axis=1)
     own_ids = lax.dynamic_slice_in_dim(expert_ids, grp_id * rows_here, rows_here, 0)
     homes = slot_match(own_ids, jnp.arange(n_grp, dtype=jnp.int32) * local_experts, rows_here, 1)[:, 0]
     spread_back = jnp.where(homes[..., None], per_expert[:, :, None, :], 0.0)

time: 59.5 us -> 59.3 us (level)
  local copies, waits for them, and re-layouts: 4.67 us -> 3.86 us
  Pallas kernels: 14 us -> 14.7 us
    reshape x2 -> x0, local copies, waits for them, and re-layouts: 0.79 us -> none  [shards(): blocks = picked.reshape(CAP, n_dev, out_width)]
    pallas_call x1, Pallas kernels: 14 us -> 14.7 us  [expert_ffn(): pl.pallas_call(expert_kernel, grid=(hidden_units // tile,), in_specs=[pl....]
where the time goes in v8:
time: 59.3 us; the launch traced here: 58.9 us
  waiting for transfers between devices  22 us (37%)
  Pallas kernels  14.7 us (25%)
  starting transfers between devices  12.9 us (22%)
  local copies, waits for them, and re-layouts  3.86 us (7%)
  other arithmetic  3.3 us (6%)
  matrix products  1.31 us (2%)
  between operations  0.84 us (1%)
    pallas_call x1, Pallas kernels, expert_ffn(): pl.pallas_call(expert_kernel, grid=(hidden_units // tile,), in_specs=[pl....  14.7 us
    all_to_all x1, waiting for transfers between devices, shards(): lax.all_to_all(spread, ('grp', 'shard'), 0, 0, tiled=True)  8.46 us
    all_to_all x1, starting transfers between devices, shards(): stats = lax.all_to_all(packed, 'shard', 0, 0, tiled=True)  7.38 us
    all_to_all x1, waiting for transfers between devices, shards(): arrived = lax.all_to_all(blocks, ('grp', 'shard'), 0, 0, tiled=True)  6.9 us
    all_to_all x1, waiting for transfers between devices, shards(): stats = lax.all_to_all(packed, 'shard', 0, 0, tiled=True)  6.61 us
    all_to_all x1, starting transfers between devices, shards(): arrived = lax.all_to_all(blocks, ('grp', 'shard'), 0, 0, tiled=True)  2.95 us
    all_to_all x1, starting transfers between devices, shards(): lax.all_to_all(spread, ('grp', 'shard'), 0, 0, tiled=True)  2.58 us
  transfers between devices with their start and end apart: 3, of which 3 were waited for; matrix products, arithmetic and copies ran while one was open for 2% of the time, Pallas kernels for 0%

profile of v8, /device:TPU:0, one launch (start us, length us, event | category | flops | bytes accessed | tf_op | source)
XLA Modules:
  0.0 58.9 jit_solution(11241280275385530072)
XLA Ops:
  0.6 0.0 copy-start
  0.7 1.0 %reshape.261 = bf16[4,8,6,128]{3,2,1,0:T(8,128)(2,1)S(1)} reshape(bf16[4,6144]{1,0:T(4,128)(2,1)} %param.10) | data formatting | bytes 98304 | tf_op jit(solution)/shard_map/reshape | solution.py:96
  1.7 0.0 copy-start.1
  1.7 0.9 %broadcast_compare_fusion = pred[4,256]{1,0:T(4,128)(4,1)S(1)} fusion(s32[256]{0:T(256)S(1)} %iota_add_fusion, s32[4]{0:T(128)} %param.13), kind=kLoop, calls=%fused_computation.42 | loop fusion | flops 1024 | bytes 2064 | tf_op jit(solution)/shard_map/lt | solution.py:103
  2.6 0.0 copy-done
  2.6 0.7 %fusion.32 = (f32[4,8,6]{2,1,0:T(8,128)S(1)}, f32[4,8,6,256]{3,2,1,0:T(8,128)S(1)}) fusion(bf16[4,8,6,128]{3,2,1,0:T(8,128)(2,1)S(1)} %reshape.261, pred[4,256]{1,0:T(4,128)(4,1)S(1)} %broadcast_compare_fusion, bf16[4,256,1024]{2,1,0:T(8,128)(2,1)S(1)} %copy-done), kind=kOutput, calls=%fused_computation.56 | convolution fusion | flops 12730176 | bytes 2344704 | tf_op jit(solution)/shard_map/rgjd,rtgd->rgjt/dot_general | solution.py:99
  3.3 0.0 copy-start.3
  3.3 0.2 convert_reduce_fusion
  3.5 0.1 select_maximum_fusion
  3.6 0.0 copy-done.1
  3.6 0.4 fusion.18
  4.0 0.0 copy-start.2
  4.1 0.7 %copy.61 = f32[8,4,7,128]{3,1,2,0:T(4,128)} copy(f32[8,4,7,128]{3,2,0,1:T(8,128)S(1)} %maximum_bitcast_fusion) | data formatting | bytes 229376 | tf_op jit(solution)/shard_map/transpose | solution.py:129
  4.8 0.0 copy-start.4
  4.8 7.4 %all-to-all-start = ((f32[8,4,7,128]{3,1,2,0:T(4,128)}), f32[8,4,7,128]{3,1,2,0:T(4,128)S(1)}, u32[]{:S(2)}, u32[]{:S(2)}) async-start(f32[8,4,7,128]{3,1,2,0:T(4,128)} %copy.61), calls=%async_computation | async-start | bytes 229376 | tf_op jit(solution)/shard_map/all_to_all | solution.py:130
  12.2 0.0 copy-done.3
  12.2 0.1 and.47
  12.3 0.1 constant_dynamic-slice_fusion
  12.4 0.2 reduce_window_sum.22
  12.6 0.2 reduce_window_sum.23
  12.8 6.6 %all-to-all-done = f32[8,4,7,128]{3,1,2,0:T(4,128)S(1)} async-done(((f32[8,4,7,128]{3,1,2,0:T(4,128)}), f32[8,4,7,128]{3,1,2,0:T(4,128)S(1)}, u32[]{:S(2)}, u32[]{:S(2)}) %all-to-all-start) | async-done | bytes 114720 | tf_op jit(solution)/shard_map/all_to_all | solution.py:130
  19.5 0.1 fusion.23
  19.5 0.1 copy.64
  19.6 0.1 copy.63
  19.8 0.1 fusion.21
  19.9 0.1 fusion.25
  20.0 0.7 %broadcast_in_dim.107 = bf16[32,4,768]{2,1,0:T(4,128)(2,1)} broadcast(bf16[4,768]{1,0:T(4,128)(2,1)S(1)} %fusion.25), dimensions={1,2} | broadcast | bytes 202752 | tf_op jit(solution)/shard_map/broadcast_in_dim | solution.py:141
  20.7 2.6 %all-to-all-start.1 = ((bf16[32,4,768]{2,1,0:T(4,128)(2,1)}), bf16[32,4,768]{2,1,0:T(4,128)(2,1)S(1)}, u32[]{:S(2)}, u32[]{:S(2)}) async-start(bf16[32,4,768]{2,1,0:T(4,128)(2,1)} %broadcast_in_dim.107), calls=%async_computation.1 | async-start | bytes 393216 | tf_op jit(solution)/shard_map/all_to_all | solution.py:142
  23.3 0.1 iota_compare_fusion.1
  23.4 8.5 %all-to-all-done.1 = bf16[32,4,768]{2,1,0:T(4,128)(2,1)S(1)} async-done(((bf16[32,4,768]{2,1,0:T(4,128)(2,1)}), bf16[32,4,768]{2,1,0:T(4,128)(2,1)S(1)}, u32[]{:S(2)}, u32[]{:S(2)}) %all-to-all-start.1) | async-done | bytes 196640 | tf_op jit(solution)/shard_map/all_to_all | solution.py:142
  31.9 0.1 multiply_reduce_fusion
  32.0 0.1 copy.67
  32.1 0.1 rsqrt.12
  32.3 0.1 copy.72
  32.4 0.0 copy-done.2
  32.4 0.1 multiply_convert_fusion.x_ref
  32.5 0.0 copy-done.4
  32.5 0.2 fusion.33
  32.8 0.1 select_reduce_fusion.1
  32.9 14.7 %shard_map.113 = bf16[32,2,768]{2,1,0:T(2,128)(2,1)} custom-call(bf16[16,6144]{1,0:T(8,128)(2,1)S(1)} %multiply_convert_fusion.x_ref, bf16[1,6144,1024]{2,1,0:T(8,128)(2,1)} %gate_ref.1, bf16[1,6144,1024]{2,1,0:T(8,128)(2,1)} %up_ref.1, bf16[1,1024,6144]{2,1,0:T(8,128)(2,1)} %down_ref.1, f32[8,16]{1,0:T(8,128)S(1)} %bitcast.77), custom_call_target="tpu_custom_call" | custom-call | tf_op jit(solution)/shard_map/pallas_call | solution.py:59
  47.6 2.9 %all-to-all-start.2 = ((bf16[32,2,768]{2,1,0:T(2,128)(2,1)}), bf16[32,2,768]{2,1,0:T(2,128)(2,1)S(1)}, u32[]{:S(2)}, u32[]{:S(2)}) async-start(bf16[32,2,768]{2,1,0:T(2,128)(2,1)} %shard_map.113), calls=%async_computation.2 | async-start | bytes 196608 | tf_op jit(solution)/shard_map/all_to_all | solution.py:176
  50.6 0.7 %constant_dynamic-slice_fusion.1 = bf16[4,6144]{1,0:T(4,128)(2,1)} fusion(bf16[16,6144]{1,0:T(8,128)(2,1)S(1)} %multiply_convert_fusion.x_ref, s32[]{:T(128)S(6)} %select_n.31), kind=kLoop, calls=%fused_computation.51 | loop fusion | bytes 98308 | tf_op jit(solution)/shard_map/dynamic_slice | solution.py:148
  51.2 6.9 %all-to-all-done.2 = bf16[32,2,768]{2,1,0:T(2,128)(2,1)S(1)} async-done(((bf16[32,2,768]{2,1,0:T(2,128)(2,1)}), bf16[32,2,768]{2,1,0:T(2,128)(2,1)S(1)}, u32[]{:S(2)}, u32[]{:S(2)}) %all-to-all-start.2) | async-done | bytes 98336 | tf_op jit(solution)/shard_map/all_to_all | solution.py:176
  58.1 0.1 convert_reduce_fusion.1
  58.2 0.7 %select_reduce_fusion = bf16[4,768]{1,0:T(4,128)(2,1)} fusion(f32[4,2,768]{2,1,0:T(2,128)S(1)} %convert_reduce_fusion.1, pred[4,2,4]{2,1,0:T(4,128)(4,1)S(1)} %compare_and_fusion.1), kind=kLoop, calls=%fused_computation.20 | loop fusion | flops 46080 | bytes 30752 | tf_op jit(solution)/shard_map/reduce_sum | solution.py:182
  (20 shorter events, 0.3 us)
Async XLA Ops:
  0.6 1.9 %copy-start = (bf16[4,256,1024]{2,1,0:T(8,128)(2,1)S(1)}, bf16[4,256,1024]{2,1,0:T(8,128)(2,1)}, u32[]{:S(2)}) copy-start(bf16[4,256,1024]{2,1,0:T(8,128)(2,1)} %param.11) | copy-start | bytes 6291460
  1.7 1.9 %copy-start.1 = (bf16[4,256,1024]{2,1,0:T(8,128)(2,1)S(1)}, bf16[4,256,1024]{2,1,0:T(8,128)(2,1)}, u32[]{:S(2)}) copy-start(bf16[4,256,1024]{2,1,0:T(8,128)(2,1)} %param.12) | copy-start | bytes 6291460
  3.3 8.9 %copy-start.3 = (s32[16,2]{0,1:T(2,128)S(1)}, s32[16,2]{0,1:T(2,128)}, u32[]{:S(2)}) copy-start(s32[16,2]{0,1:T(2,128)} %param.16) | copy-start | bytes 388
  4.0 28.4 %copy-start.2 = (f32[6144]{0:T(1024)S(1)}, f32[6144]{0:T(1024)}, u32[]{:S(2)}) copy-start(f32[6144]{0:T(1024)} %param.14) | copy-start | bytes 73732
  4.8 27.7 %copy-start.4 = (bf16[6144,4]{0,1:T(4,128)(2,1)S(1)}, bf16[6144,4]{0,1:T(4,128)(2,1)}, u32[]{:S(2)}) copy-start(bf16[6144,4]{0,1:T(4,128)(2,1)} %param.15) | copy-start | bytes 147460
  4.8 14.6 %all-to-all-start = ((f32[8,4,7,128]{3,1,2,0:T(4,128)}), f32[8,4,7,128]{3,1,2,0:T(4,128)S(1)}, u32[]{:S(2)}, u32[]{:S(2)}) async-start(f32[8,4,7,128]{3,1,2,0:T(4,128)} %copy.61), calls=%async_computation | async-start | bytes 229376 | tf_op jit(solution)/shard_map/all_to_all | solution.py:130
  20.7 11.1 %all-to-all-start.1 = ((bf16[32,4,768]{2,1,0:T(4,128)(2,1)}), bf16[32,4,768]{2,1,0:T(4,128)(2,1)S(1)}, u32[]{:S(2)}, u32[]{:S(2)}) async-start(bf16[32,4,768]{2,1,0:T(4,128)(2,1)} %broadcast_in_dim.107), calls=%async_computation.1 | async-start | bytes 393216 | tf_op jit(solution)/shard_map/all_to_all | solution.py:142
  47.6 10.5 %all-to-all-start.2 = ((bf16[32,2,768]{2,1,0:T(2,128)(2,1)}), bf16[32,2,768]{2,1,0:T(2,128)(2,1)S(1)}, u32[]{:S(2)}, u32[]{:S(2)}) async-start(bf16[32,2,768]{2,1,0:T(2,128)(2,1)} %shard_map.113), calls=%async_computation.2 | async-start | bytes 196608 | tf_op jit(solution)/shard_map/all_to_all | solution.py:176

commit v9 on v7

--- a/solution.py
+++ b/solution.py
@@ -22,6 +22,8 @@
 
 def expert_kernel(x_ref, gate_ref, up_ref, down_ref, sel_ref, out_ref, acc_ref):
     step = pl.program_id(0)
+    n_cols, _, out_width = acc_ref.shape
+    n_sel = sel_ref.shape[0]
 
     @pl.when(step == 0)
     def _():
@@ -31,20 +33,26 @@
     gate_proj = jnp.dot(rows, gate_ref[...], preferred_element_type=jnp.float32)
     up_proj = jnp.dot(rows, up_ref[...], preferred_element_type=jnp.float32)
     hidden = (jax.nn.silu(gate_proj) * up_proj).astype(jnp.bfloat16)
-    acc_ref[...] += jnp.dot(hidden, down_ref[...], preferred_element_type=jnp.float32)
+    for col in range(n_cols):
+        acc_ref[col] += jnp.dot(
+            hidden, down_ref[:, col * out_width : (col + 1) * out_width],
+            preferred_element_type=jnp.float32,
+        )
 
     @pl.when(step == pl.num_programs(0) - 1)
     def _():
-        picked = jnp.dot(
-            sel_ref[...], acc_ref[...], precision=lax.Precision.HIGHEST,
-            preferred_element_type=jnp.float32,
-        )
-        out_ref[...] = picked.astype(out_ref.dtype)
+        for col in range(n_cols):
+            picked = jnp.dot(
+                sel_ref[...], acc_ref[col], precision=lax.Precision.HIGHEST,
+                preferred_element_type=jnp.float32,
+            )
+            out_ref[col * n_sel : (col + 1) * n_sel, :] = picked.astype(out_ref.dtype)
 
 
-def expert_ffn(rows, w_gate, w_up, w_down, local, select):
+def expert_ffn(rows, w_gate, w_up, w_down, local, select, n_cols):
     n_rows, width = rows.shape
-    n_out = select.shape[0]
+    n_sel = select.shape[0]
+    out_width = width // n_cols
     hidden_units = w_gate.shape[2]
     tile = min(FF_TILE, hidden_units)
     return pl.pallas_call(
@@ -55,11 +63,11 @@
             pl.BlockSpec((None, width, tile), lambda f: (local, 0, f)),
             pl.BlockSpec((None, width, tile), lambda f: (local, 0, f)),
             pl.BlockSpec((None, tile, width), lambda f: (local, f, 0)),
-            pl.BlockSpec((n_out, n_rows), lambda f: (0, 0)),
+            pl.BlockSpec(select.shape, lambda f: (0, 0)),
         ],
-        out_specs=pl.BlockSpec((n_out, width), lambda f: (0, 0)),
-        out_shape=jax.ShapeDtypeStruct((n_out, width), jnp.bfloat16),
-        scratch_shapes=[pltpu.VMEM((n_rows, width), jnp.float32)],
+        out_specs=pl.BlockSpec((n_cols * n_sel, out_width), lambda f: (0, 0)),
+        out_shape=jax.ShapeDtypeStruct((n_cols * n_sel, out_width), jnp.bfloat16),
+        scratch_shapes=[pltpu.VMEM((n_cols, n_rows, out_width), jnp.float32)],
         compiler_params=pltpu.CompilerParams(vmem_limit_bytes=48 * 1024 * 1024),
     )(rows, w_gate, w_up, w_down, select)
 
@@ -162,12 +170,11 @@
         ),
         axis=2,
     )
-    select = jnp.transpose(select, (1, 0, 2)).reshape(CAP * n_grp, n_grp * rows_here)
-    picked = expert_ffn(normed_all, w_gate, w_up, w_down, 0, select)
-    blocks = picked.reshape(CAP, n_dev, out_width)
-    arrived = lax.all_to_all(blocks, ("grp", "shard"), 1, 1, tiled=True)
-    arrived = arrived.astype(jnp.float32).reshape(CAP, n_grp, n_shard, out_width)
-    per_expert = jnp.transpose(jnp.sum(arrived, axis=2), (1, 0, 2))
+    select = select.reshape(n_grp * CAP, n_grp * rows_here)
+    blocks = expert_ffn(normed_all, w_gate, w_up, w_down, 0, select, n_shard)
+    arrived = lax.all_to_all(blocks, ("shard", "grp"), 0, 0, tiled=True)
+    arrived = arrived.astype(jnp.float32).reshape(n_shard, n_grp, CAP, out_width)
+    per_expert = jnp.sum(arrived, axis=0)
     own_ids = lax.dynamic_slice_in_dim(expert_ids, grp_id * rows_here, rows_here, 0)
     homes = slot_match(own_ids, jnp.arange(n_grp, dtype=jnp.int32) * local_experts, rows_here, 1)[:, 0]
     spread_back = jnp.where(homes[..., None], per_expert[:, :, None, :], 0.0)

time: 59.5 us -> 59.5 us (level)
    reshape x2 -> x0, local copies, waits for them, and re-layouts: 0.79 us -> none  [shards(): blocks = picked.reshape(CAP, n_dev, out_width)]
    all_to_all x0 -> x1, local copies, waits for them, and re-layouts: none -> 0.68 us  [shards(): arrived = lax.all_to_all(blocks, ('shard', 'grp'), 0, 0, tiled=True)]
where the time goes in v9:
time: 59.5 us; the launch traced here: 59.2 us
  waiting for transfers between devices  22.2 us (37%)
  Pallas kernels  14 us (24%)
  starting transfers between devices  12.9 us (22%)
  local copies, waits for them, and re-layouts  4.53 us (8%)
  other arithmetic  3.3 us (6%)
  matrix products  1.31 us (2%)
  between operations  0.83 us (1%)
    pallas_call x1, Pallas kernels, expert_ffn(): pl.pallas_call(expert_kernel, grid=(hidden_units // tile,), in_specs=[pl....  14 us
    all_to_all x1, waiting for transfers between devices, shards(): lax.all_to_all(spread, ('grp', 'shard'), 0, 0, tiled=True)  8.46 us
    all_to_all x1, starting transfers between devices, shards(): stats = lax.all_to_all(packed, 'shard', 0, 0, tiled=True)  7.38 us
    all_to_all x1, waiting for transfers between devices, shards(): arrived = lax.all_to_all(blocks, ('shard', 'grp'), 0, 0, tiled=True)  7.15 us
    all_to_all x1, waiting for transfers between devices, shards(): stats = lax.all_to_all(packed, 'shard', 0, 0, tiled=True)  6.61 us
    all_to_all x1, starting transfers between devices, shards(): arrived = lax.all_to_all(blocks, ('shard', 'grp'), 0, 0, tiled=True)  2.95 us
    all_to_all x1, starting transfers between devices, shards(): lax.all_to_all(spread, ('grp', 'shard'), 0, 0, tiled=True)  2.58 us
  transfers between devices with their start and end apart: 3, of which 3 were waited for; matrix products, arithmetic and copies ran while one was open for 2% of the time, Pallas kernels for 0%

profile of v9, /device:TPU:0, one launch (start us, length us, event | category | flops | bytes accessed | tf_op | source)
XLA Modules:
  0.0 59.2 jit_solution(7047237330306028985)
XLA Ops:
  0.6 0.0 copy-start
  0.7 1.0 %reshape.261 = bf16[4,8,6,128]{3,2,1,0:T(8,128)(2,1)S(1)} reshape(bf16[4,6144]{1,0:T(4,128)(2,1)} %param.10) | data formatting | bytes 98304 | tf_op jit(solution)/shard_map/reshape | solution.py:95
  1.7 0.0 copy-start.1
  1.7 0.9 %broadcast_compare_fusion = pred[4,256]{1,0:T(4,128)(4,1)S(1)} fusion(s32[256]{0:T(256)S(1)} %iota_add_fusion, s32[4]{0:T(128)} %param.13), kind=kLoop, calls=%fused_computation.42 | loop fusion | flops 1024 | bytes 2064 | tf_op jit(solution)/shard_map/lt | solution.py:102
  2.6 0.0 copy-done
  2.6 0.7 %fusion.32 = (f32[4,8,6]{2,1,0:T(8,128)S(1)}, f32[4,8,6,256]{3,2,1,0:T(8,128)S(1)}) fusion(bf16[4,8,6,128]{3,2,1,0:T(8,128)(2,1)S(1)} %reshape.261, pred[4,256]{1,0:T(4,128)(4,1)S(1)} %broadcast_compare_fusion, bf16[4,256,1024]{2,1,0:T(8,128)(2,1)S(1)} %copy-done), kind=kOutput, calls=%fused_computation.56 | convolution fusion | flops 12730176 | bytes 2344704 | tf_op jit(solution)/shard_map/rgjd,rtgd->rgjt/dot_general | solution.py:98
  3.3 0.0 copy-start.3
  3.3 0.2 convert_reduce_fusion
  3.5 0.1 select_maximum_fusion
  3.6 0.0 copy-done.1
  3.6 0.4 fusion.18
  4.0 0.0 copy-start.2
  4.1 0.7 %copy.61 = f32[8,4,7,128]{3,1,2,0:T(4,128)} copy(f32[8,4,7,128]{3,2,0,1:T(8,128)S(1)} %maximum_bitcast_fusion) | data formatting | bytes 229376 | tf_op jit(solution)/shard_map/transpose | solution.py:128
  4.8 0.0 copy-start.4
  4.8 7.4 %all-to-all-start = ((f32[8,4,7,128]{3,1,2,0:T(4,128)}), f32[8,4,7,128]{3,1,2,0:T(4,128)S(1)}, u32[]{:S(2)}, u32[]{:S(2)}) async-start(f32[8,4,7,128]{3,1,2,0:T(4,128)} %copy.61), calls=%async_computation | async-start | bytes 229376 | tf_op jit(solution)/shard_map/all_to_all | solution.py:129
  12.2 0.0 copy-done.3
  12.2 0.1 and.47
  12.3 0.1 constant_dynamic-slice_fusion
  12.4 0.2 reduce_window_sum.22
  12.6 0.2 reduce_window_sum.23
  12.8 6.6 %all-to-all-done = f32[8,4,7,128]{3,1,2,0:T(4,128)S(1)} async-done(((f32[8,4,7,128]{3,1,2,0:T(4,128)}), f32[8,4,7,128]{3,1,2,0:T(4,128)S(1)}, u32[]{:S(2)}, u32[]{:S(2)}) %all-to-all-start) | async-done | bytes 114720 | tf_op jit(solution)/shard_map/all_to_all | solution.py:129
  19.5 0.1 fusion.23
  19.5 0.1 copy.64
  19.6 0.1 copy.63
  19.8 0.1 fusion.21
  19.9 0.1 fusion.25
  20.0 0.7 %broadcast_in_dim.107 = bf16[32,4,768]{2,1,0:T(4,128)(2,1)} broadcast(bf16[4,768]{1,0:T(4,128)(2,1)S(1)} %fusion.25), dimensions={1,2} | broadcast | bytes 202752 | tf_op jit(solution)/shard_map/broadcast_in_dim | solution.py:140
  20.7 2.6 %all-to-all-start.1 = ((bf16[32,4,768]{2,1,0:T(4,128)(2,1)}), bf16[32,4,768]{2,1,0:T(4,128)(2,1)S(1)}, u32[]{:S(2)}, u32[]{:S(2)}) async-start(bf16[32,4,768]{2,1,0:T(4,128)(2,1)} %broadcast_in_dim.107), calls=%async_computation.1 | async-start | bytes 393216 | tf_op jit(solution)/shard_map/all_to_all | solution.py:141
  23.3 0.1 iota_compare_fusion.1
  23.4 8.5 %all-to-all-done.1 = bf16[32,4,768]{2,1,0:T(4,128)(2,1)S(1)} async-done(((bf16[32,4,768]{2,1,0:T(4,128)(2,1)}), bf16[32,4,768]{2,1,0:T(4,128)(2,1)S(1)}, u32[]{:S(2)}, u32[]{:S(2)}) %all-to-all-start.1) | async-done | bytes 196640 | tf_op jit(solution)/shard_map/all_to_all | solution.py:141
  31.9 0.1 multiply_reduce_fusion
  32.0 0.1 copy.67
  32.1 0.1 rsqrt.12
  32.3 0.1 copy.71
  32.4 0.0 copy-done.2
  32.4 0.1 multiply_convert_fusion.x_ref
  32.5 0.0 copy-done.4
  32.5 0.2 fusion.33
  32.8 0.1 select_reduce_fusion.1
  32.9 14.0 %shard_map.113 = bf16[64,768]{1,0:T(8,128)(2,1)S(1)} custom-call(bf16[16,6144]{1,0:T(8,128)(2,1)S(1)} %multiply_convert_fusion.x_ref, bf16[1,6144,1024]{2,1,0:T(8,128)(2,1)} %gate_ref.1, bf16[1,6144,1024]{2,1,0:T(8,128)(2,1)} %up_ref.1, bf16[1,1024,6144]{2,1,0:T(8,128)(2,1)} %down_ref.1, f32[8,16]{1,0:T(8,128)S(1)} %bitcast.75), custom_call_target="tpu_custom_call" | custom-call | tf_op jit(solution)/shard_map/pallas_call | solution.py:58
  46.9 0.7 %all_to_all.14 = bf16[32,2,768]{2,1,0:T(2,128)(2,1)} reshape(bf16[64,768]{1,0:T(8,128)(2,1)S(1)} %shard_map.113) | data formatting | bytes 196608 | tf_op jit(solution)/shard_map/all_to_all | solution.py:175
  47.6 2.9 %all-to-all-start.2 = ((bf16[32,2,768]{2,1,0:T(2,128)(2,1)}), bf16[32,2,768]{2,1,0:T(2,128)(2,1)S(1)}, u32[]{:S(2)}, u32[]{:S(2)}) async-start(bf16[32,2,768]{2,1,0:T(2,128)(2,1)} %all_to_all.14), calls=%async_computation.2 | async-start | bytes 196608 | tf_op jit(solution)/shard_map/all_to_all | solution.py:175
  50.6 0.7 %constant_dynamic-slice_fusion.1 = bf16[4,6144]{1,0:T(4,128)(2,1)} fusion(bf16[16,6144]{1,0:T(8,128)(2,1)S(1)} %multiply_convert_fusion.x_ref, s32[]{:T(128)S(6)} %select_n.31), kind=kLoop, calls=%fused_computation.51 | loop fusion | bytes 98308 | tf_op jit(solution)/shard_map/dynamic_slice | solution.py:147
  51.2 7.2 %all-to-all-done.2 = bf16[32,2,768]{2,1,0:T(2,128)(2,1)S(1)} async-done(((bf16[32,2,768]{2,1,0:T(2,128)(2,1)}), bf16[32,2,768]{2,1,0:T(2,128)(2,1)S(1)}, u32[]{:S(2)}, u32[]{:S(2)}) %all-to-all-start.2) | async-done | bytes 98336 | tf_op jit(solution)/shard_map/all_to_all | solution.py:175
  58.4 0.1 convert_reduce_fusion.1
  58.5 0.7 %select_reduce_fusion = bf16[4,768]{1,0:T(4,128)(2,1)} fusion(f32[4,2,768]{2,1,0:T(2,128)S(1)} %convert_reduce_fusion.1, pred[4,2,4]{2,1,0:T(4,128)(4,1)S(1)} %compare_and_fusion.1), kind=kLoop, calls=%fused_computation.20 | loop fusion | flops 46080 | bytes 30752 | tf_op jit(solution)/shard_map/reduce_sum | solution.py:181
  (19 shorter events, 0.3 us)
Async XLA Ops:
  0.6 1.9 %copy-start = (bf16[4,256,1024]{2,1,0:T(8,128)(2,1)S(1)}, bf16[4,256,1024]{2,1,0:T(8,128)(2,1)}, u32[]{:S(2)}) copy-start(bf16[4,256,1024]{2,1,0:T(8,128)(2,1)} %param.11) | copy-start | bytes 6291460
  1.7 1.9 %copy-start.1 = (bf16[4,256,1024]{2,1,0:T(8,128)(2,1)S(1)}, bf16[4,256,1024]{2,1,0:T(8,128)(2,1)}, u32[]{:S(2)}) copy-start(bf16[4,256,1024]{2,1,0:T(8,128)(2,1)} %param.12) | copy-start | bytes 6291460
  3.3 8.9 %copy-start.3 = (s32[16,2]{0,1:T(2,128)S(1)}, s32[16,2]{0,1:T(2,128)}, u32[]{:S(2)}) copy-start(s32[16,2]{0,1:T(2,128)} %param.16) | copy-start | bytes 388
  4.0 28.4 %copy-start.2 = (f32[6144]{0:T(1024)S(1)}, f32[6144]{0:T(1024)}, u32[]{:S(2)}) copy-start(f32[6144]{0:T(1024)} %param.14) | copy-start | bytes 73732
  4.8 27.7 %copy-start.4 = (bf16[6144,4]{0,1:T(4,128)(2,1)S(1)}, bf16[6144,4]{0,1:T(4,128)(2,1)}, u32[]{:S(2)}) copy-start(bf16[6144,4]{0,1:T(4,128)(2,1)} %param.15) | copy-start | bytes 147460
  4.8 14.6 %all-to-all-start = ((f32[8,4,7,128]{3,1,2,0:T(4,128)}), f32[8,4,7,128]{3,1,2,0:T(4,128)S(1)}, u32[]{:S(2)}, u32[]{:S(2)}) async-start(f32[8,4,7,128]{3,1,2,0:T(4,128)} %copy.61), calls=%async_computation | async-start | bytes 229376 | tf_op jit(solution)/shard_map/all_to_all | solution.py:129
  20.7 11.1 %all-to-all-start.1 = ((bf16[32,4,768]{2,1,0:T(4,128)(2,1)}), bf16[32,4,768]{2,1,0:T(4,128)(2,1)S(1)}, u32[]{:S(2)}, u32[]{:S(2)}) async-start(bf16[32,4,768]{2,1,0:T(4,128)(2,1)} %broadcast_in_dim.107), calls=%async_computation.1 | async-start | bytes 393216 | tf_op jit(solution)/shard_map/all_to_all | solution.py:141
  47.6 10.8 %all-to-all-start.2 = ((bf16[32,2,768]{2,1,0:T(2,128)(2,1)}), bf16[32,2,768]{2,1,0:T(2,128)(2,1)S(1)}, u32[]{:S(2)}, u32[]{:S(2)}) async-start(bf16[32,2,768]{2,1,0:T(2,128)(2,1)} %all_to_all.14), calls=%async_computation.2 | async-start | bytes 196608 | tf_op jit(solution)/shard_map/all_to_all | solution.py:175

commit v10 on v9

--- a/solution.py
+++ b/solution.py
@@ -41,12 +41,17 @@
 
     @pl.when(step == pl.num_programs(0) - 1)
     def _():
+        _, slots, _ = out_ref.shape
+        n_groups = n_sel // slots
         for col in range(n_cols):
             picked = jnp.dot(
                 sel_ref[...], acc_ref[col], precision=lax.Precision.HIGHEST,
                 preferred_element_type=jnp.float32,
-            )
-            out_ref[col * n_sel : (col + 1) * n_sel, :] = picked.astype(out_ref.dtype)
+            ).astype(out_ref.dtype)
+            for slot in range(slots):
+                out_ref[col * n_groups : (col + 1) * n_groups, slot, :] = picked[
+                    slot * n_groups : (slot + 1) * n_groups
+                ]
 
 
 def expert_ffn(rows, w_gate, w_up, w_down, local, select, n_cols):
@@ -65,8 +70,8 @@
             pl.BlockSpec((None, tile, width), lambda f: (local, f, 0)),
             pl.BlockSpec(select.shape, lambda f: (0, 0)),
         ],
-        out_specs=pl.BlockSpec((n_cols * n_sel, out_width), lambda f: (0, 0)),
-        out_shape=jax.ShapeDtypeStruct((n_cols * n_sel, out_width), jnp.bfloat16),
+        out_specs=pl.BlockSpec((n_cols * n_sel // CAP, CAP, out_width), lambda f: (0, 0, 0)),
+        out_shape=jax.ShapeDtypeStruct((n_cols * n_sel // CAP, CAP, out_width), jnp.bfloat16),
         scratch_shapes=[pltpu.VMEM((n_cols, n_rows, out_width), jnp.float32)],
         compiler_params=pltpu.CompilerParams(vmem_limit_bytes=48 * 1024 * 1024),
     )(rows, w_gate, w_up, w_down, select)
@@ -170,7 +175,7 @@
         ),
         axis=2,
     )
-    select = select.reshape(n_grp * CAP, n_grp * rows_here)
+    select = jnp.transpose(select, (1, 0, 2)).reshape(CAP * n_grp, n_grp * rows_here)
     blocks = expert_ffn(normed_all, w_gate, w_up, w_down, 0, select, n_shard)
     arrived = lax.all_to_all(blocks, ("shard", "grp"), 0, 0, tiled=True)
     arrived = arrived.astype(jnp.float32).reshape(n_shard, n_grp, CAP, out_width)

time: 59.5 us -> 59.5 us (level)
  Pallas kernels: 14 us -> 14.7 us
  local copies, waits for them, and re-layouts: 4.53 us -> 3.86 us
    all_to_all x1 -> x0, local copies, waits for them, and re-layouts: 0.68 us -> none  [shards(): arrived = lax.all_to_all(blocks, ('shard', 'grp'), 0, 0, tiled=True)]
    pallas_call x1, Pallas kernels: 14 us -> 14.7 us  [expert_ffn(): pl.pallas_call(expert_kernel, grid=(hidden_units // tile,), in_specs=[pl....]
where the time goes in v10:
time: 59.5 us; the launch traced here: 59.2 us
  waiting for transfers between devices  22.2 us (37%)
  Pallas kernels  14.7 us (25%)
  starting transfers between devices  12.9 us (22%)
  local copies, waits for them, and re-layouts  3.86 us (6%)
  other arithmetic  3.3 us (6%)
  matrix products  1.31 us (2%)
  between operations  0.84 us (1%)
    pallas_call x1, Pallas kernels, expert_ffn(): pl.pallas_call(expert_kernel, grid=(hidden_units // tile,), in_specs=[pl....  14.7 us
    all_to_all x1, waiting for transfers between devices, shards(): lax.all_to_all(spread, ('grp', 'shard'), 0, 0, tiled=True)  8.46 us
    all_to_all x1, starting transfers between devices, shards(): stats = lax.all_to_all(packed, 'shard', 0, 0, tiled=True)  7.38 us
    all_to_all x1, waiting for transfers between devices, shards(): arrived = lax.all_to_all(blocks, ('shard', 'grp'), 0, 0, tiled=True)  7.15 us
    all_to_all x1, waiting for transfers between devices, shards(): stats = lax.all_to_all(packed, 'shard', 0, 0, tiled=True)  6.61 us
    all_to_all x1, starting transfers between devices, shards(): arrived = lax.all_to_all(blocks, ('shard', 'grp'), 0, 0, tiled=True)  2.95 us
    all_to_all x1, starting transfers between devices, shards(): lax.all_to_all(spread, ('grp', 'shard'), 0, 0, tiled=True)  2.58 us
  transfers between devices with their start and end apart: 3, of which 3 were waited for; matrix products, arithmetic and copies ran while one was open for 2% of the time, Pallas kernels for 0%

profile of v10, /device:TPU:0, one launch (start us, length us, event | category | flops | bytes accessed | tf_op | source)
XLA Modules:
  0.0 59.2 jit_solution(3997096938420962968)
XLA Ops:
  0.6 0.0 copy-start
  0.7 1.0 %reshape.261 = bf16[4,8,6,128]{3,2,1,0:T(8,128)(2,1)S(1)} reshape(bf16[4,6144]{1,0:T(4,128)(2,1)} %param.10) | data formatting | bytes 98304 | tf_op jit(solution)/shard_map/reshape | solution.py:100
  1.7 0.0 copy-start.1
  1.7 0.9 %broadcast_compare_fusion = pred[4,256]{1,0:T(4,128)(4,1)S(1)} fusion(s32[256]{0:T(256)S(1)} %iota_add_fusion, s32[4]{0:T(128)} %param.13), kind=kLoop, calls=%fused_computation.42 | loop fusion | flops 1024 | bytes 2064 | tf_op jit(solution)/shard_map/lt | solution.py:107
  2.6 0.0 copy-done
  2.6 0.7 %fusion.32 = (f32[4,8,6]{2,1,0:T(8,128)S(1)}, f32[4,8,6,256]{3,2,1,0:T(8,128)S(1)}) fusion(bf16[4,8,6,128]{3,2,1,0:T(8,128)(2,1)S(1)} %reshape.261, pred[4,256]{1,0:T(4,128)(4,1)S(1)} %broadcast_compare_fusion, bf16[4,256,1024]{2,1,0:T(8,128)(2,1)S(1)} %copy-done), kind=kOutput, calls=%fused_computation.56 | convolution fusion | flops 12730176 | bytes 2344704 | tf_op jit(solution)/shard_map/rgjd,rtgd->rgjt/dot_general | solution.py:103
  3.3 0.0 copy-start.3
  3.3 0.2 convert_reduce_fusion
  3.5 0.1 select_maximum_fusion
  3.6 0.0 copy-done.1
  3.6 0.4 fusion.18
  4.0 0.0 copy-start.2
  4.1 0.7 %copy.61 = f32[8,4,7,128]{3,1,2,0:T(4,128)} copy(f32[8,4,7,128]{3,2,0,1:T(8,128)S(1)} %maximum_bitcast_fusion) | data formatting | bytes 229376 | tf_op jit(solution)/shard_map/transpose | solution.py:133
  4.8 0.0 copy-start.4
  4.8 7.4 %all-to-all-start = ((f32[8,4,7,128]{3,1,2,0:T(4,128)}), f32[8,4,7,128]{3,1,2,0:T(4,128)S(1)}, u32[]{:S(2)}, u32[]{:S(2)}) async-start(f32[8,4,7,128]{3,1,2,0:T(4,128)} %copy.61), calls=%async_computation | async-start | bytes 229376 | tf_op jit(solution)/shard_map/all_to_all | solution.py:134
  12.2 0.0 copy-done.3
  12.2 0.1 and.47
  12.3 0.1 constant_dynamic-slice_fusion
  12.4 0.2 reduce_window_sum.22
  12.6 0.2 reduce_window_sum.23
  12.8 6.6 %all-to-all-done = f32[8,4,7,128]{3,1,2,0:T(4,128)S(1)} async-done(((f32[8,4,7,128]{3,1,2,0:T(4,128)}), f32[8,4,7,128]{3,1,2,0:T(4,128)S(1)}, u32[]{:S(2)}, u32[]{:S(2)}) %all-to-all-start) | async-done | bytes 114720 | tf_op jit(solution)/shard_map/all_to_all | solution.py:134
  19.5 0.1 fusion.23
  19.5 0.1 copy.64
  19.6 0.1 copy.63
  19.8 0.1 fusion.21
  19.9 0.1 fusion.25
  20.0 0.7 %broadcast_in_dim.107 = bf16[32,4,768]{2,1,0:T(4,128)(2,1)} broadcast(bf16[4,768]{1,0:T(4,128)(2,1)S(1)} %fusion.25), dimensions={1,2} | broadcast | bytes 202752 | tf_op jit(solution)/shard_map/broadcast_in_dim | solution.py:145
  20.7 2.6 %all-to-all-start.1 = ((bf16[32,4,768]{2,1,0:T(4,128)(2,1)}), bf16[32,4,768]{2,1,0:T(4,128)(2,1)S(1)}, u32[]{:S(2)}, u32[]{:S(2)}) async-start(bf16[32,4,768]{2,1,0:T(4,128)(2,1)} %broadcast_in_dim.107), calls=%async_computation.1 | async-start | bytes 393216 | tf_op jit(solution)/shard_map/all_to_all | solution.py:146
  23.3 0.1 iota_compare_fusion.1
  23.4 8.5 %all-to-all-done.1 = bf16[32,4,768]{2,1,0:T(4,128)(2,1)S(1)} async-done(((bf16[32,4,768]{2,1,0:T(4,128)(2,1)}), bf16[32,4,768]{2,1,0:T(4,128)(2,1)S(1)}, u32[]{:S(2)}, u32[]{:S(2)}) %all-to-all-start.1) | async-done | bytes 196640 | tf_op jit(solution)/shard_map/all_to_all | solution.py:146
  31.9 0.1 multiply_reduce_fusion
  32.0 0.1 copy.67
  32.1 0.1 rsqrt.12
  32.3 0.1 copy.72
  32.4 0.0 copy-done.2
  32.4 0.1 multiply_convert_fusion.x_ref
  32.5 0.0 copy-done.4
  32.5 0.2 fusion.33
  32.8 0.1 select_reduce_fusion.1
  32.9 14.7 %shard_map.113 = bf16[32,2,768]{2,1,0:T(2,128)(2,1)} custom-call(bf16[16,6144]{1,0:T(8,128)(2,1)S(1)} %multiply_convert_fusion.x_ref, bf16[1,6144,1024]{2,1,0:T(8,128)(2,1)} %gate_ref.1, bf16[1,6144,1024]{2,1,0:T(8,128)(2,1)} %up_ref.1, bf16[1,1024,6144]{2,1,0:T(8,128)(2,1)} %down_ref.1, f32[8,16]{1,0:T(8,128)S(1)} %bitcast.76), custom_call_target="tpu_custom_call" | custom-call | tf_op jit(solution)/shard_map/pallas_call | solution.py:63
  47.6 2.9 %all-to-all-start.2 = ((bf16[32,2,768]{2,1,0:T(2,128)(2,1)}), bf16[32,2,768]{2,1,0:T(2,128)(2,1)S(1)}, u32[]{:S(2)}, u32[]{:S(2)}) async-start(bf16[32,2,768]{2,1,0:T(2,128)(2,1)} %shard_map.113), calls=%async_computation.2 | async-start | bytes 196608 | tf_op jit(solution)/shard_map/all_to_all | solution.py:180
  50.6 0.7 %constant_dynamic-slice_fusion.1 = bf16[4,6144]{1,0:T(4,128)(2,1)} fusion(bf16[16,6144]{1,0:T(8,128)(2,1)S(1)} %multiply_convert_fusion.x_ref, s32[]{:T(128)S(6)} %select_n.31), kind=kLoop, calls=%fused_computation.51 | loop fusion | bytes 98308 | tf_op jit(solution)/shard_map/dynamic_slice | solution.py:152
  51.2 7.2 %all-to-all-done.2 = bf16[32,2,768]{2,1,0:T(2,128)(2,1)S(1)} async-done(((bf16[32,2,768]{2,1,0:T(2,128)(2,1)}), bf16[32,2,768]{2,1,0:T(2,128)(2,1)S(1)}, u32[]{:S(2)}, u32[]{:S(2)}) %all-to-all-start.2) | async-done | bytes 98336 | tf_op jit(solution)/shard_map/all_to_all | solution.py:180
  58.4 0.1 convert_reduce_fusion.1
  58.5 0.7 %select_reduce_fusion = bf16[4,768]{1,0:T(4,128)(2,1)} fusion(f32[4,2,768]{2,1,0:T(2,128)S(1)} %convert_reduce_fusion.1, pred[4,2,4]{2,1,0:T(4,128)(4,1)S(1)} %compare_and_fusion.1), kind=kLoop, calls=%fused_computation.20 | loop fusion | flops 46080 | bytes 30752 | tf_op jit(solution)/shard_map/reduce_sum | solution.py:186
  (20 shorter events, 0.3 us)
Async XLA Ops:
  0.6 1.9 %copy-start = (bf16[4,256,1024]{2,1,0:T(8,128)(2,1)S(1)}, bf16[4,256,1024]{2,1,0:T(8,128)(2,1)}, u32[]{:S(2)}) copy-start(bf16[4,256,1024]{2,1,0:T(8,128)(2,1)} %param.11) | copy-start | bytes 6291460
  1.7 1.9 %copy-start.1 = (bf16[4,256,1024]{2,1,0:T(8,128)(2,1)S(1)}, bf16[4,256,1024]{2,1,0:T(8,128)(2,1)}, u32[]{:S(2)}) copy-start(bf16[4,256,1024]{2,1,0:T(8,128)(2,1)} %param.12) | copy-start | bytes 6291460
  3.3 8.9 %copy-start.3 = (s32[16,2]{0,1:T(2,128)S(1)}, s32[16,2]{0,1:T(2,128)}, u32[]{:S(2)}) copy-start(s32[16,2]{0,1:T(2,128)} %param.16) | copy-start | bytes 388
  4.0 28.4 %copy-start.2 = (f32[6144]{0:T(1024)S(1)}, f32[6144]{0:T(1024)}, u32[]{:S(2)}) copy-start(f32[6144]{0:T(1024)} %param.14) | copy-start | bytes 73732
  4.8 27.7 %copy-start.4 = (bf16[6144,4]{0,1:T(4,128)(2,1)S(1)}, bf16[6144,4]{0,1:T(4,128)(2,1)}, u32[]{:S(2)}) copy-start(bf16[6144,4]{0,1:T(4,128)(2,1)} %param.15) | copy-start | bytes 147460
  4.8 14.6 %all-to-all-start = ((f32[8,4,7,128]{3,1,2,0:T(4,128)}), f32[8,4,7,128]{3,1,2,0:T(4,128)S(1)}, u32[]{:S(2)}, u32[]{:S(2)}) async-start(f32[8,4,7,128]{3,1,2,0:T(4,128)} %copy.61), calls=%async_computation | async-start | bytes 229376 | tf_op jit(solution)/shard_map/all_to_all | solution.py:134
  20.7 11.1 %all-to-all-start.1 = ((bf16[32,4,768]{2,1,0:T(4,128)(2,1)}), bf16[32,4,768]{2,1,0:T(4,128)(2,1)S(1)}, u32[]{:S(2)}, u32[]{:S(2)}) async-start(bf16[32,4,768]{2,1,0:T(4,128)(2,1)} %broadcast_in_dim.107), calls=%async_computation.1 | async-start | bytes 393216 | tf_op jit(solution)/shard_map/all_to_all | solution.py:146
  47.6 10.8 %all-to-all-start.2 = ((bf16[32,2,768]{2,1,0:T(2,128)(2,1)}), bf16[32,2,768]{2,1,0:T(2,128)(2,1)S(1)}, u32[]{:S(2)}, u32[]{:S(2)}) async-start(bf16[32,2,768]{2,1,0:T(2,128)(2,1)} %shard_map.113), calls=%async_computation.2 | async-start | bytes 196608 | tf_op jit(solution)/shard_map/all_to_all | solution.py:180

commit v11 on v10

--- a/solution.py
+++ b/solution.py
@@ -17,7 +17,7 @@
 CAP = 2
 
 
-FF_TILE = 256
+FF_TILE = 512
 
 
 def expert_kernel(x_ref, gate_ref, up_ref, down_ref, sel_ref, out_ref, acc_ref):

time: 59.5 us -> 60.3 us (1.013)
  Pallas kernels: 14.7 us -> 15.5 us
    pallas_call x1, Pallas kernels: 14.7 us -> 15.5 us  [expert_ffn(): pl.pallas_call(expert_kernel, grid=(hidden_units // tile,), in_specs=[pl....]
where the time goes in v11:
time: 60.3 us; the launch traced here: 60 us
  waiting for transfers between devices  22.2 us (37%)
  Pallas kernels  15.5 us (26%)
  starting transfers between devices  12.9 us (21%)
  local copies, waits for them, and re-layouts  3.86 us (6%)
  other arithmetic  3.3 us (5%)
  matrix products  1.31 us (2%)
  between operations  0.84 us (1%)
    pallas_call x1, Pallas kernels, expert_ffn(): pl.pallas_call(expert_kernel, grid=(hidden_units // tile,), in_specs=[pl....  15.5 us
    all_to_all x1, waiting for transfers between devices, shards(): lax.all_to_all(spread, ('grp', 'shard'), 0, 0, tiled=True)  8.46 us
    all_to_all x1, starting transfers between devices, shards(): stats = lax.all_to_all(packed, 'shard', 0, 0, tiled=True)  7.38 us
    all_to_all x1, waiting for transfers between devices, shards(): arrived = lax.all_to_all(blocks, ('shard', 'grp'), 0, 0, tiled=True)  7.15 us
    all_to_all x1, waiting for transfers between devices, shards(): stats = lax.all_to_all(packed, 'shard', 0, 0, tiled=True)  6.61 us
    all_to_all x1, starting transfers between devices, shards(): arrived = lax.all_to_all(blocks, ('shard', 'grp'), 0, 0, tiled=True)  2.95 us
    all_to_all x1, starting transfers between devices, shards(): lax.all_to_all(spread, ('grp', 'shard'), 0, 0, tiled=True)  2.58 us
  transfers between devices with their start and end apart: 3, of which 3 were waited for; matrix products, arithmetic and copies ran while one was open for 2% of the time, Pallas kernels for 0%

profile of v11, /device:TPU:0, one launch (start us, length us, event | category | flops | bytes accessed | tf_op | source)
XLA Modules:
  0.0 60.0 jit_solution(6539527589316784358)
XLA Ops:
  0.6 0.0 copy-start
  0.7 1.0 %reshape.261 = bf16[4,8,6,128]{3,2,1,0:T(8,128)(2,1)S(1)} reshape(bf16[4,6144]{1,0:T(4,128)(2,1)} %param.10) | data formatting | bytes 98304 | tf_op jit(solution)/shard_map/reshape | solution.py:100
  1.7 0.0 copy-start.1
  1.7 0.9 %broadcast_compare_fusion = pred[4,256]{1,0:T(4,128)(4,1)S(1)} fusion(s32[256]{0:T(256)S(1)} %iota_add_fusion, s32[4]{0:T(128)} %param.13), kind=kLoop, calls=%fused_computation.42 | loop fusion | flops 1024 | bytes 2064 | tf_op jit(solution)/shard_map/lt | solution.py:107
  2.6 0.0 copy-done
  2.6 0.7 %fusion.32 = (f32[4,8,6]{2,1,0:T(8,128)S(1)}, f32[4,8,6,256]{3,2,1,0:T(8,128)S(1)}) fusion(bf16[4,8,6,128]{3,2,1,0:T(8,128)(2,1)S(1)} %reshape.261, pred[4,256]{1,0:T(4,128)(4,1)S(1)} %broadcast_compare_fusion, bf16[4,256,1024]{2,1,0:T(8,128)(2,1)S(1)} %copy-done), kind=kOutput, calls=%fused_computation.56 | convolution fusion | flops 12730176 | bytes 2344704 | tf_op jit(solution)/shard_map/rgjd,rtgd->rgjt/dot_general | solution.py:103
  3.3 0.0 copy-start.3
  3.3 0.2 convert_reduce_fusion
  3.5 0.1 select_maximum_fusion
  3.6 0.0 copy-done.1
  3.6 0.4 fusion.18
  4.0 0.0 copy-start.2
  4.1 0.7 %copy.61 = f32[8,4,7,128]{3,1,2,0:T(4,128)} copy(f32[8,4,7,128]{3,2,0,1:T(8,128)S(1)} %maximum_bitcast_fusion) | data formatting | bytes 229376 | tf_op jit(solution)/shard_map/transpose | solution.py:133
  4.8 0.0 copy-start.4
  4.8 7.4 %all-to-all-start = ((f32[8,4,7,128]{3,1,2,0:T(4,128)}), f32[8,4,7,128]{3,1,2,0:T(4,128)S(1)}, u32[]{:S(2)}, u32[]{:S(2)}) async-start(f32[8,4,7,128]{3,1,2,0:T(4,128)} %copy.61), calls=%async_computation | async-start | bytes 229376 | tf_op jit(solution)/shard_map/all_to_all | solution.py:134
  12.2 0.0 copy-done.3
  12.2 0.1 and.47
  12.3 0.1 constant_dynamic-slice_fusion
  12.4 0.2 reduce_window_sum.22
  12.6 0.2 reduce_window_sum.23
  12.8 6.6 %all-to-all-done = f32[8,4,7,128]{3,1,2,0:T(4,128)S(1)} async-done(((f32[8,4,7,128]{3,1,2,0:T(4,128)}), f32[8,4,7,128]{3,1,2,0:T(4,128)S(1)}, u32[]{:S(2)}, u32[]{:S(2)}) %all-to-all-start) | async-done | bytes 114720 | tf_op jit(solution)/shard_map/all_to_all | solution.py:134
  19.5 0.1 fusion.23
  19.5 0.1 copy.64
  19.6 0.1 copy.63
  19.8 0.1 fusion.21
  19.9 0.1 fusion.25
  20.0 0.7 %broadcast_in_dim.107 = bf16[32,4,768]{2,1,0:T(4,128)(2,1)} broadcast(bf16[4,768]{1,0:T(4,128)(2,1)S(1)} %fusion.25), dimensions={1,2} | broadcast | bytes 202752 | tf_op jit(solution)/shard_map/broadcast_in_dim | solution.py:145
  20.7 2.6 %all-to-all-start.1 = ((bf16[32,4,768]{2,1,0:T(4,128)(2,1)}), bf16[32,4,768]{2,1,0:T(4,128)(2,1)S(1)}, u32[]{:S(2)}, u32[]{:S(2)}) async-start(bf16[32,4,768]{2,1,0:T(4,128)(2,1)} %broadcast_in_dim.107), calls=%async_computation.1 | async-start | bytes 393216 | tf_op jit(solution)/shard_map/all_to_all | solution.py:146
  23.3 0.1 iota_compare_fusion.1
  23.4 8.5 %all-to-all-done.1 = bf16[32,4,768]{2,1,0:T(4,128)(2,1)S(1)} async-done(((bf16[32,4,768]{2,1,0:T(4,128)(2,1)}), bf16[32,4,768]{2,1,0:T(4,128)(2,1)S(1)}, u32[]{:S(2)}, u32[]{:S(2)}) %all-to-all-start.1) | async-done | bytes 196640 | tf_op jit(solution)/shard_map/all_to_all | solution.py:146
  31.9 0.1 multiply_reduce_fusion
  32.0 0.1 copy.67
  32.1 0.1 rsqrt.12
  32.3 0.1 copy.72
  32.4 0.0 copy-done.2
  32.4 0.1 multiply_convert_fusion.x_ref
  32.5 0.0 copy-done.4
  32.5 0.2 fusion.33
  32.8 0.1 select_reduce_fusion.1
  32.9 15.5 %shard_map.113 = bf16[32,2,768]{2,1,0:T(2,128)(2,1)} custom-call(bf16[16,6144]{1,0:T(8,128)(2,1)S(1)} %multiply_convert_fusion.x_ref, bf16[1,6144,1024]{2,1,0:T(8,128)(2,1)} %gate_ref.1, bf16[1,6144,1024]{2,1,0:T(8,128)(2,1)} %up_ref.1, bf16[1,1024,6144]{2,1,0:T(8,128)(2,1)} %down_ref.1, f32[8,16]{1,0:T(8,128)S(1)} %bitcast.76), custom_call_target="tpu_custom_call" | custom-call | tf_op jit(solution)/shard_map/pallas_call | solution.py:63
  48.4 2.9 %all-to-all-start.2 = ((bf16[32,2,768]{2,1,0:T(2,128)(2,1)}), bf16[32,2,768]{2,1,0:T(2,128)(2,1)S(1)}, u32[]{:S(2)}, u32[]{:S(2)}) async-start(bf16[32,2,768]{2,1,0:T(2,128)(2,1)} %shard_map.113), calls=%async_computation.2 | async-start | bytes 196608 | tf_op jit(solution)/shard_map/all_to_all | solution.py:180
  51.4 0.7 %constant_dynamic-slice_fusion.1 = bf16[4,6144]{1,0:T(4,128)(2,1)} fusion(bf16[16,6144]{1,0:T(8,128)(2,1)S(1)} %multiply_convert_fusion.x_ref, s32[]{:T(128)S(6)} %select_n.31), kind=kLoop, calls=%fused_computation.51 | loop fusion | bytes 98308 | tf_op jit(solution)/shard_map/dynamic_slice | solution.py:152
  52.0 7.2 %all-to-all-done.2 = bf16[32,2,768]{2,1,0:T(2,128)(2,1)S(1)} async-done(((bf16[32,2,768]{2,1,0:T(2,128)(2,1)}), bf16[32,2,768]{2,1,0:T(2,128)(2,1)S(1)}, u32[]{:S(2)}, u32[]{:S(2)}) %all-to-all-start.2) | async-done | bytes 98336 | tf_op jit(solution)/shard_map/all_to_all | solution.py:180
  59.2 0.1 convert_reduce_fusion.1
  59.3 0.7 %select_reduce_fusion = bf16[4,768]{1,0:T(4,128)(2,1)} fusion(f32[4,2,768]{2,1,0:T(2,128)S(1)} %convert_reduce_fusion.1, pred[4,2,4]{2,1,0:T(4,128)(4,1)S(1)} %compare_and_fusion.1), kind=kLoop, calls=%fused_computation.20 | loop fusion | flops 46080 | bytes 30752 | tf_op jit(solution)/shard_map/reduce_sum | solution.py:186
  (20 shorter events, 0.3 us)
Async XLA Ops:
  0.6 1.9 %copy-start = (bf16[4,256,1024]{2,1,0:T(8,128)(2,1)S(1)}, bf16[4,256,1024]{2,1,0:T(8,128)(2,1)}, u32[]{:S(2)}) copy-start(bf16[4,256,1024]{2,1,0:T(8,128)(2,1)} %param.11) | copy-start | bytes 6291460
  1.7 1.9 %copy-start.1 = (bf16[4,256,1024]{2,1,0:T(8,128)(2,1)S(1)}, bf16[4,256,1024]{2,1,0:T(8,128)(2,1)}, u32[]{:S(2)}) copy-start(bf16[4,256,1024]{2,1,0:T(8,128)(2,1)} %param.12) | copy-start | bytes 6291460
  3.3 8.9 %copy-start.3 = (s32[16,2]{0,1:T(2,128)S(1)}, s32[16,2]{0,1:T(2,128)}, u32[]{:S(2)}) copy-start(s32[16,2]{0,1:T(2,128)} %param.16) | copy-start | bytes 388
  4.0 28.4 %copy-start.2 = (f32[6144]{0:T(1024)S(1)}, f32[6144]{0:T(1024)}, u32[]{:S(2)}) copy-start(f32[6144]{0:T(1024)} %param.14) | copy-start | bytes 73732
  4.8 27.7 %copy-start.4 = (bf16[6144,4]{0,1:T(4,128)(2,1)S(1)}, bf16[6144,4]{0,1:T(4,128)(2,1)}, u32[]{:S(2)}) copy-start(bf16[6144,4]{0,1:T(4,128)(2,1)} %param.15) | copy-start | bytes 147460
  4.8 14.6 %all-to-all-start = ((f32[8,4,7,128]{3,1,2,0:T(4,128)}), f32[8,4,7,128]{3,1,2,0:T(4,128)S(1)}, u32[]{:S(2)}, u32[]{:S(2)}) async-start(f32[8,4,7,128]{3,1,2,0:T(4,128)} %copy.61), calls=%async_computation | async-start | bytes 229376 | tf_op jit(solution)/shard_map/all_to_all | solution.py:134
  20.7 11.1 %all-to-all-start.1 = ((bf16[32,4,768]{2,1,0:T(4,128)(2,1)}), bf16[32,4,768]{2,1,0:T(4,128)(2,1)S(1)}, u32[]{:S(2)}, u32[]{:S(2)}) async-start(bf16[32,4,768]{2,1,0:T(4,128)(2,1)} %broadcast_in_dim.107), calls=%async_computation.1 | async-start | bytes 393216 | tf_op jit(solution)/shard_map/all_to_all | solution.py:146
  48.4 10.8 %all-to-all-start.2 = ((bf16[32,2,768]{2,1,0:T(2,128)(2,1)}), bf16[32,2,768]{2,1,0:T(2,128)(2,1)S(1)}, u32[]{:S(2)}, u32[]{:S(2)}) async-start(bf16[32,2,768]{2,1,0:T(2,128)(2,1)} %shard_map.113), calls=%async_computation.2 | async-start | bytes 196608 | tf_op jit(solution)/shard_map/all_to_all | solution.py:180

commit v12 on v11

--- a/solution.py
+++ b/solution.py
@@ -17,7 +17,7 @@
 CAP = 2
 
 
-FF_TILE = 512
+FF_TILE = 128
 
 
 def expert_kernel(x_ref, gate_ref, up_ref, down_ref, sel_ref, out_ref, acc_ref):

time: 60.3 us -> 60.8 us (level)
  no operation moved by 1% of the time
where the time goes in v12:
time: 60.8 us; the launch traced here: 60.4 us
  waiting for transfers between devices  22.2 us (37%)
  Pallas kernels  16 us (26%)
  starting transfers between devices  12.9 us (21%)
  local copies, waits for them, and re-layouts  3.86 us (6%)
  other arithmetic  3.3 us (5%)
  matrix products  1.31 us (2%)
  between operations  0.84 us (1%)
    pallas_call x1, Pallas kernels, expert_ffn(): pl.pallas_call(expert_kernel, grid=(hidden_units // tile,), in_specs=[pl....  16 us
    all_to_all x1, waiting for transfers between devices, shards(): lax.all_to_all(spread, ('grp', 'shard'), 0, 0, tiled=True)  8.46 us
    all_to_all x1, starting transfers between devices, shards(): stats = lax.all_to_all(packed, 'shard', 0, 0, tiled=True)  7.38 us
    all_to_all x1, waiting for transfers between devices, shards(): arrived = lax.all_to_all(blocks, ('shard', 'grp'), 0, 0, tiled=True)  7.15 us
    all_to_all x1, waiting for transfers between devices, shards(): stats = lax.all_to_all(packed, 'shard', 0, 0, tiled=True)  6.61 us
    all_to_all x1, starting transfers between devices, shards(): arrived = lax.all_to_all(blocks, ('shard', 'grp'), 0, 0, tiled=True)  2.95 us
    all_to_all x1, starting transfers between devices, shards(): lax.all_to_all(spread, ('grp', 'shard'), 0, 0, tiled=True)  2.58 us
  transfers between devices with their start and end apart: 3, of which 3 were waited for; matrix products, arithmetic and copies ran while one was open for 2% of the time, Pallas kernels for 0%

profile of v12, /device:TPU:0, one launch (start us, length us, event | category | flops | bytes accessed | tf_op | source)
XLA Modules:
  0.0 60.4 jit_solution(7216933094679468116)
XLA Ops:
  0.6 0.0 copy-start
  0.7 1.0 %reshape.261 = bf16[4,8,6,128]{3,2,1,0:T(8,128)(2,1)S(1)} reshape(bf16[4,6144]{1,0:T(4,128)(2,1)} %param.10) | data formatting | bytes 98304 | tf_op jit(solution)/shard_map/reshape | solution.py:100
  1.7 0.0 copy-start.1
  1.7 0.9 %broadcast_compare_fusion = pred[4,256]{1,0:T(4,128)(4,1)S(1)} fusion(s32[256]{0:T(256)S(1)} %iota_add_fusion, s32[4]{0:T(128)} %param.13), kind=kLoop, calls=%fused_computation.42 | loop fusion | flops 1024 | bytes 2064 | tf_op jit(solution)/shard_map/lt | solution.py:107
  2.6 0.0 copy-done
  2.6 0.7 %fusion.32 = (f32[4,8,6]{2,1,0:T(8,128)S(1)}, f32[4,8,6,256]{3,2,1,0:T(8,128)S(1)}) fusion(bf16[4,8,6,128]{3,2,1,0:T(8,128)(2,1)S(1)} %reshape.261, pred[4,256]{1,0:T(4,128)(4,1)S(1)} %broadcast_compare_fusion, bf16[4,256,1024]{2,1,0:T(8,128)(2,1)S(1)} %copy-done), kind=kOutput, calls=%fused_computation.56 | convolution fusion | flops 12730176 | bytes 2344704 | tf_op jit(solution)/shard_map/rgjd,rtgd->rgjt/dot_general | solution.py:103
  3.3 0.0 copy-start.3
  3.3 0.2 convert_reduce_fusion
  3.5 0.1 select_maximum_fusion
  3.6 0.0 copy-done.1
  3.6 0.4 fusion.18
  4.0 0.0 copy-start.2
  4.1 0.7 %copy.61 = f32[8,4,7,128]{3,1,2,0:T(4,128)} copy(f32[8,4,7,128]{3,2,0,1:T(8,128)S(1)} %maximum_bitcast_fusion) | data formatting | bytes 229376 | tf_op jit(solution)/shard_map/transpose | solution.py:133
  4.8 0.0 copy-start.4
  4.8 7.4 %all-to-all-start = ((f32[8,4,7,128]{3,1,2,0:T(4,128)}), f32[8,4,7,128]{3,1,2,0:T(4,128)S(1)}, u32[]{:S(2)}, u32[]{:S(2)}) async-start(f32[8,4,7,128]{3,1,2,0:T(4,128)} %copy.61), calls=%async_computation | async-start | bytes 229376 | tf_op jit(solution)/shard_map/all_to_all | solution.py:134
  12.2 0.0 copy-done.3
  12.2 0.1 and.47
  12.3 0.1 constant_dynamic-slice_fusion
  12.4 0.2 reduce_window_sum.22
  12.6 0.2 reduce_window_sum.23
  12.8 6.6 %all-to-all-done = f32[8,4,7,128]{3,1,2,0:T(4,128)S(1)} async-done(((f32[8,4,7,128]{3,1,2,0:T(4,128)}), f32[8,4,7,128]{3,1,2,0:T(4,128)S(1)}, u32[]{:S(2)}, u32[]{:S(2)}) %all-to-all-start) | async-done | bytes 114720 | tf_op jit(solution)/shard_map/all_to_all | solution.py:134
  19.5 0.1 fusion.23
  19.5 0.1 copy.64
  19.6 0.1 copy.63
  19.8 0.1 fusion.21
  19.9 0.1 fusion.25
  20.0 0.7 %broadcast_in_dim.107 = bf16[32,4,768]{2,1,0:T(4,128)(2,1)} broadcast(bf16[4,768]{1,0:T(4,128)(2,1)S(1)} %fusion.25), dimensions={1,2} | broadcast | bytes 202752 | tf_op jit(solution)/shard_map/broadcast_in_dim | solution.py:145
  20.7 2.6 %all-to-all-start.1 = ((bf16[32,4,768]{2,1,0:T(4,128)(2,1)}), bf16[32,4,768]{2,1,0:T(4,128)(2,1)S(1)}, u32[]{:S(2)}, u32[]{:S(2)}) async-start(bf16[32,4,768]{2,1,0:T(4,128)(2,1)} %broadcast_in_dim.107), calls=%async_computation.1 | async-start | bytes 393216 | tf_op jit(solution)/shard_map/all_to_all | solution.py:146
  23.3 0.1 iota_compare_fusion.1
  23.4 8.5 %all-to-all-done.1 = bf16[32,4,768]{2,1,0:T(4,128)(2,1)S(1)} async-done(((bf16[32,4,768]{2,1,0:T(4,128)(2,1)}), bf16[32,4,768]{2,1,0:T(4,128)(2,1)S(1)}, u32[]{:S(2)}, u32[]{:S(2)}) %all-to-all-start.1) | async-done | bytes 196640 | tf_op jit(solution)/shard_map/all_to_all | solution.py:146
  31.9 0.1 multiply_reduce_fusion
  32.0 0.1 copy.67
  32.1 0.1 rsqrt.12
  32.3 0.1 copy.72
  32.4 0.0 copy-done.2
  32.4 0.1 multiply_convert_fusion.x_ref
  32.5 0.0 copy-done.4
  32.5 0.2 fusion.33
  32.8 0.1 select_reduce_fusion.1
  32.9 16.0 %shard_map.113 = bf16[32,2,768]{2,1,0:T(2,128)(2,1)} custom-call(bf16[16,6144]{1,0:T(8,128)(2,1)S(1)} %multiply_convert_fusion.x_ref, bf16[1,6144,1024]{2,1,0:T(8,128)(2,1)} %gate_ref.1, bf16[1,6144,1024]{2,1,0:T(8,128)(2,1)} %up_ref.1, bf16[1,1024,6144]{2,1,0:T(8,128)(2,1)} %down_ref.1, f32[8,16]{1,0:T(8,128)S(1)} %bitcast.76), custom_call_target="tpu_custom_call" | custom-call | tf_op jit(solution)/shard_map/pallas_call | solution.py:63
  48.9 2.9 %all-to-all-start.2 = ((bf16[32,2,768]{2,1,0:T(2,128)(2,1)}), bf16[32,2,768]{2,1,0:T(2,128)(2,1)S(1)}, u32[]{:S(2)}, u32[]{:S(2)}) async-start(bf16[32,2,768]{2,1,0:T(2,128)(2,1)} %shard_map.113), calls=%async_computation.2 | async-start | bytes 196608 | tf_op jit(solution)/shard_map/all_to_all | solution.py:180
  51.8 0.7 %constant_dynamic-slice_fusion.1 = bf16[4,6144]{1,0:T(4,128)(2,1)} fusion(bf16[16,6144]{1,0:T(8,128)(2,1)S(1)} %multiply_convert_fusion.x_ref, s32[]{:T(128)S(6)} %select_n.31), kind=kLoop, calls=%fused_computation.51 | loop fusion | bytes 98308 | tf_op jit(solution)/shard_map/dynamic_slice | solution.py:152
  52.5 7.2 %all-to-all-done.2 = bf16[32,2,768]{2,1,0:T(2,128)(2,1)S(1)} async-done(((bf16[32,2,768]{2,1,0:T(2,128)(2,1)}), bf16[32,2,768]{2,1,0:T(2,128)(2,1)S(1)}, u32[]{:S(2)}, u32[]{:S(2)}) %all-to-all-start.2) | async-done | bytes 98336 | tf_op jit(solution)/shard_map/all_to_all | solution.py:180
  59.6 0.1 convert_reduce_fusion.1
  59.7 0.7 %select_reduce_fusion = bf16[4,768]{1,0:T(4,128)(2,1)} fusion(f32[4,2,768]{2,1,0:T(2,128)S(1)} %convert_reduce_fusion.1, pred[4,2,4]{2,1,0:T(4,128)(4,1)S(1)} %compare_and_fusion.1), kind=kLoop, calls=%fused_computation.20 | loop fusion | flops 46080 | bytes 30752 | tf_op jit(solution)/shard_map/reduce_sum | solution.py:186
  (20 shorter events, 0.3 us)
Async XLA Ops:
  0.6 1.9 %copy-start = (bf16[4,256,1024]{2,1,0:T(8,128)(2,1)S(1)}, bf16[4,256,1024]{2,1,0:T(8,128)(2,1)}, u32[]{:S(2)}) copy-start(bf16[4,256,1024]{2,1,0:T(8,128)(2,1)} %param.11) | copy-start | bytes 6291460
  1.7 1.9 %copy-start.1 = (bf16[4,256,1024]{2,1,0:T(8,128)(2,1)S(1)}, bf16[4,256,1024]{2,1,0:T(8,128)(2,1)}, u32[]{:S(2)}) copy-start(bf16[4,256,1024]{2,1,0:T(8,128)(2,1)} %param.12) | copy-start | bytes 6291460
  3.3 8.9 %copy-start.3 = (s32[16,2]{0,1:T(2,128)S(1)}, s32[16,2]{0,1:T(2,128)}, u32[]{:S(2)}) copy-start(s32[16,2]{0,1:T(2,128)} %param.16) | copy-start | bytes 388
  4.0 28.4 %copy-start.2 = (f32[6144]{0:T(1024)S(1)}, f32[6144]{0:T(1024)}, u32[]{:S(2)}) copy-start(f32[6144]{0:T(1024)} %param.14) | copy-start | bytes 73732
  4.8 27.7 %copy-start.4 = (bf16[6144,4]{0,1:T(4,128)(2,1)S(1)}, bf16[6144,4]{0,1:T(4,128)(2,1)}, u32[]{:S(2)}) copy-start(bf16[6144,4]{0,1:T(4,128)(2,1)} %param.15) | copy-start | bytes 147460
  4.8 14.6 %all-to-all-start = ((f32[8,4,7,128]{3,1,2,0:T(4,128)}), f32[8,4,7,128]{3,1,2,0:T(4,128)S(1)}, u32[]{:S(2)}, u32[]{:S(2)}) async-start(f32[8,4,7,128]{3,1,2,0:T(4,128)} %copy.61), calls=%async_computation | async-start | bytes 229376 | tf_op jit(solution)/shard_map/all_to_all | solution.py:134
  20.7 11.1 %all-to-all-start.1 = ((bf16[32,4,768]{2,1,0:T(4,128)(2,1)}), bf16[32,4,768]{2,1,0:T(4,128)(2,1)S(1)}, u32[]{:S(2)}, u32[]{:S(2)}) async-start(bf16[32,4,768]{2,1,0:T(4,128)(2,1)} %broadcast_in_dim.107), calls=%async_computation.1 | async-start | bytes 393216 | tf_op jit(solution)/shard_map/all_to_all | solution.py:146
  48.9 10.8 %all-to-all-start.2 = ((bf16[32,2,768]{2,1,0:T(2,128)(2,1)}), bf16[32,2,768]{2,1,0:T(2,128)(2,1)S(1)}, u32[]{:S(2)}, u32[]{:S(2)}) async-start(bf16[32,2,768]{2,1,0:T(2,128)(2,1)} %shard_map.113), calls=%async_computation.2 | async-start | bytes 196608 | tf_op jit(solution)/shard_map/all_to_all | solution.py:180

commit v13 on v7

--- a/solution.py
+++ b/solution.py
@@ -58,7 +58,7 @@
             pl.BlockSpec((n_out, n_rows), lambda f: (0, 0)),
         ],
         out_specs=pl.BlockSpec((n_out, width), lambda f: (0, 0)),
-        out_shape=jax.ShapeDtypeStruct((n_out, width), jnp.bfloat16),
+        out_shape=jax.ShapeDtypeStruct((n_out, width), jnp.float32),
         scratch_shapes=[pltpu.VMEM((n_rows, width), jnp.float32)],
         compiler_params=pltpu.CompilerParams(vmem_limit_bytes=48 * 1024 * 1024),
     )(rows, w_gate, w_up, w_down, select)
@@ -166,7 +166,7 @@
     picked = expert_ffn(normed_all, w_gate, w_up, w_down, 0, select)
     blocks = picked.reshape(CAP, n_dev, out_width)
     arrived = lax.all_to_all(blocks, ("grp", "shard"), 1, 1, tiled=True)
-    arrived = arrived.astype(jnp.float32).reshape(CAP, n_grp, n_shard, out_width)
+    arrived = arrived.reshape(CAP, n_grp, n_shard, out_width)
     per_expert = jnp.transpose(jnp.sum(arrived, axis=2), (1, 0, 2))
     own_ids = lax.dynamic_slice_in_dim(expert_ids, grp_id * rows_here, rows_here, 0)
     homes = slot_match(own_ids, jnp.arange(n_grp, dtype=jnp.int32) * local_experts, rows_here, 1)[:, 0]

time: 59.5 us -> 60.5 us (1.017)
  waiting for transfers between devices: 22 us -> 23 us
    all_to_all x1, waiting for transfers between devices: 6.9 us -> 7.89 us  [shards(): arrived = lax.all_to_all(blocks, ('grp', 'shard'), 1, 1, tiled=True)]
where the time goes in v13:
time: 60.5 us; the launch traced here: 60.1 us
  waiting for transfers between devices  23 us (38%)
  Pallas kernels  14 us (23%)
  starting transfers between devices  12.9 us (21%)
  local copies, waits for them, and re-layouts  4.75 us (8%)
  other arithmetic  3.26 us (5%)
  matrix products  1.32 us (2%)
  between operations  0.86 us (1%)
    pallas_call x1, Pallas kernels, expert_ffn(): pl.pallas_call(expert_kernel, grid=(hidden_units // tile,), in_specs=[pl....  14 us
    all_to_all x1, waiting for transfers between devices, shards(): lax.all_to_all(spread, ('grp', 'shard'), 0, 0, tiled=True)  8.46 us
    all_to_all x1, waiting for transfers between devices, shards(): arrived = lax.all_to_all(blocks, ('grp', 'shard'), 1, 1, tiled=True)  7.89 us
    all_to_all x1, starting transfers between devices, shards(): stats = lax.all_to_all(packed, 'shard', 0, 0, tiled=True)  7.38 us
    all_to_all x1, waiting for transfers between devices, shards(): stats = lax.all_to_all(packed, 'shard', 0, 0, tiled=True)  6.61 us
    all_to_all x1, starting transfers between devices, shards(): arrived = lax.all_to_all(blocks, ('grp', 'shard'), 1, 1, tiled=True)  2.95 us
    all_to_all x1, starting transfers between devices, shards(): lax.all_to_all(spread, ('grp', 'shard'), 0, 0, tiled=True)  2.58 us
  transfers between devices with their start and end apart: 3, of which 3 were waited for; matrix products, arithmetic and copies ran while one was open for 2% of the time, Pallas kernels for 0%

profile of v13, /device:TPU:0, one launch (start us, length us, event | category | flops | bytes accessed | tf_op | source)
XLA Modules:
  0.0 60.1 jit_solution(12259283646608720359)
XLA Ops:
  0.6 0.0 copy-start
  0.7 1.0 %reshape.261 = bf16[4,8,6,128]{3,2,1,0:T(8,128)(2,1)S(1)} reshape(bf16[4,6144]{1,0:T(4,128)(2,1)} %param.10) | data formatting | bytes 98304 | tf_op jit(solution)/shard_map/reshape | solution.py:87
  1.7 0.0 copy-start.1
  1.7 0.9 %broadcast_compare_fusion = pred[4,256]{1,0:T(4,128)(4,1)S(1)} fusion(s32[256]{0:T(256)S(1)} %iota_add_fusion, s32[4]{0:T(128)} %param.13), kind=kLoop, calls=%fused_computation.43 | loop fusion | flops 1024 | bytes 2064 | tf_op jit(solution)/shard_map/lt | solution.py:94
  2.6 0.0 copy-done
  2.6 0.7 %fusion.32 = (f32[4,8,6]{2,1,0:T(8,128)S(1)}, f32[4,8,6,256]{3,2,1,0:T(8,128)S(1)}) fusion(bf16[4,8,6,128]{3,2,1,0:T(8,128)(2,1)S(1)} %reshape.261, pred[4,256]{1,0:T(4,128)(4,1)S(1)} %broadcast_compare_fusion, bf16[4,256,1024]{2,1,0:T(8,128)(2,1)S(1)} %copy-done), kind=kOutput, calls=%fused_computation.57 | convolution fusion | flops 12730176 | bytes 2344704 | tf_op jit(solution)/shard_map/rgjd,rtgd->rgjt/dot_general | solution.py:90
  3.3 0.0 copy-start.3
  3.3 0.2 convert_reduce_fusion
  3.5 0.1 select_maximum_fusion
  3.6 0.0 copy-done.1
  3.6 0.4 fusion.18
  4.0 0.0 copy-start.2
  4.1 0.7 %copy.70 = f32[8,4,7,128]{3,1,2,0:T(4,128)} copy(f32[8,4,7,128]{3,2,0,1:T(8,128)S(1)} %maximum_bitcast_fusion) | data formatting | bytes 229376 | tf_op jit(solution)/shard_map/transpose | solution.py:120
  4.8 0.0 copy-start.4
  4.8 7.4 %all-to-all-start = ((f32[8,4,7,128]{3,1,2,0:T(4,128)}), f32[8,4,7,128]{3,1,2,0:T(4,128)S(1)}, u32[]{:S(2)}, u32[]{:S(2)}) async-start(f32[8,4,7,128]{3,1,2,0:T(4,128)} %copy.70), calls=%async_computation | async-start | bytes 229376 | tf_op jit(solution)/shard_map/all_to_all | solution.py:121
  12.2 0.0 copy-done.3
  12.2 0.1 and.47
  12.3 0.1 constant_dynamic-slice_fusion
  12.4 0.2 reduce_window_sum.22
  12.6 0.2 reduce_window_sum.23
  12.8 6.6 %all-to-all-done = f32[8,4,7,128]{3,1,2,0:T(4,128)S(1)} async-done(((f32[8,4,7,128]{3,1,2,0:T(4,128)}), f32[8,4,7,128]{3,1,2,0:T(4,128)S(1)}, u32[]{:S(2)}, u32[]{:S(2)}) %all-to-all-start) | async-done | bytes 114720 | tf_op jit(solution)/shard_map/all_to_all | solution.py:121
  19.5 0.1 fusion.23
  19.5 0.1 copy.73
  19.6 0.1 copy.72
  19.8 0.1 fusion.21
  19.9 0.1 fusion.25
  20.0 0.7 %broadcast_in_dim.107 = bf16[32,4,768]{2,1,0:T(4,128)(2,1)} broadcast(bf16[4,768]{1,0:T(4,128)(2,1)S(1)} %fusion.25), dimensions={1,2} | broadcast | bytes 202752 | tf_op jit(solution)/shard_map/broadcast_in_dim | solution.py:132
  20.7 2.6 %all-to-all-start.1 = ((bf16[32,4,768]{2,1,0:T(4,128)(2,1)}), bf16[32,4,768]{2,1,0:T(4,128)(2,1)S(1)}, u32[]{:S(2)}, u32[]{:S(2)}) async-start(bf16[32,4,768]{2,1,0:T(4,128)(2,1)} %broadcast_in_dim.107), calls=%async_computation.1 | async-start | bytes 393216 | tf_op jit(solution)/shard_map/all_to_all | solution.py:133
  23.3 0.1 iota_compare_fusion.1
  23.4 8.5 %all-to-all-done.1 = bf16[32,4,768]{2,1,0:T(4,128)(2,1)S(1)} async-done(((bf16[32,4,768]{2,1,0:T(4,128)(2,1)}), bf16[32,4,768]{2,1,0:T(4,128)(2,1)S(1)}, u32[]{:S(2)}, u32[]{:S(2)}) %all-to-all-start.1) | async-done | bytes 196640 | tf_op jit(solution)/shard_map/all_to_all | solution.py:133
  31.9 0.1 multiply_reduce_fusion
  32.0 0.1 copy.76
  32.1 0.1 rsqrt.12
  32.3 0.1 copy.85
  32.4 0.0 copy-done.2
  32.4 0.1 multiply_convert_fusion.x_ref
  32.5 0.0 copy-done.4
  32.5 0.2 fusion.33
  32.8 0.1 select_reduce_fusion.1
  32.9 14.0 %shard_map.113 = f32[8,6144]{1,0:T(8,128)S(1)} custom-call(bf16[16,6144]{1,0:T(8,128)(2,1)S(1)} %multiply_convert_fusion.x_ref, bf16[1,6144,1024]{2,1,0:T(8,128)(2,1)} %gate_ref.1, bf16[1,6144,1024]{2,1,0:T(8,128)(2,1)} %up_ref.1, bf16[1,1024,6144]{2,1,0:T(8,128)(2,1)} %down_ref.1, f32[8,16]{1,0:T(8,128)S(1)} %bitcast.79), custom_call_target="tpu_custom_call" | custom-call | tf_op jit(solution)/shard_map/pallas_call | solution.py:50
  47.0 0.8 %copy.78 = f32[2,32,768]{2,0,1:T(2,128)} copy(f32[2,32,768]{2,1,0:T(8,128)S(1)} %reshape.267) | data formatting | bytes 393216 | tf_op jit(solution)/shard_map/reshape | solution.py:167
  47.8 2.9 %all-to-all-start.2 = ((f32[2,32,768]{2,0,1:T(2,128)}), f32[2,32,768]{2,0,1:T(2,128)S(1)}, u32[]{:S(2)}, u32[]{:S(2)}) async-start(f32[2,32,768]{2,0,1:T(2,128)} %copy.78), calls=%async_computation.2 | async-start | bytes 393216 | tf_op jit(solution)/shard_map/all_to_all | solution.py:168
  50.8 0.7 %constant_dynamic-slice_fusion.1 = bf16[4,6144]{1,0:T(4,128)(2,1)} fusion(bf16[16,6144]{1,0:T(8,128)(2,1)S(1)} %multiply_convert_fusion.x_ref, s32[]{:T(128)S(6)} %select_n.31), kind=kLoop, calls=%fused_computation.52 | loop fusion | bytes 98308 | tf_op jit(solution)/shard_map/dynamic_slice | solution.py:139
  51.4 7.9 %all-to-all-done.2 = f32[2,32,768]{2,0,1:T(2,128)S(1)} async-done(((f32[2,32,768]{2,0,1:T(2,128)}), f32[2,32,768]{2,0,1:T(2,128)S(1)}, u32[]{:S(2)}, u32[]{:S(2)}) %all-to-all-start.2) | async-done | bytes 196640 | tf_op jit(solution)/shard_map/all_to_all | solution.py:168
  59.3 0.1 bitcast_reduce_fusion
  59.4 0.7 %select_reduce_fusion = bf16[4,768]{1,0:T(4,128)(2,1)} fusion(f32[4,2,768]{2,1,0:T(2,128)S(1)} %copy.80, pred[4,2,4]{2,1,0:T(4,128)(4,1)S(1)} %compare_and_fusion.1), kind=kLoop, calls=%fused_computation.20 | loop fusion | flops 46080 | bytes 30752 | tf_op jit(solution)/shard_map/reduce_sum | solution.py:174
  (23 shorter events, 0.4 us)
Async XLA Ops:
  0.6 1.9 %copy-start = (bf16[4,256,1024]{2,1,0:T(8,128)(2,1)S(1)}, bf16[4,256,1024]{2,1,0:T(8,128)(2,1)}, u32[]{:S(2)}) copy-start(bf16[4,256,1024]{2,1,0:T(8,128)(2,1)} %param.11) | copy-start | bytes 6291460
  1.7 1.9 %copy-start.1 = (bf16[4,256,1024]{2,1,0:T(8,128)(2,1)S(1)}, bf16[4,256,1024]{2,1,0:T(8,128)(2,1)}, u32[]{:S(2)}) copy-start(bf16[4,256,1024]{2,1,0:T(8,128)(2,1)} %param.12) | copy-start | bytes 6291460
  3.3 8.9 %copy-start.3 = (s32[16,2]{0,1:T(2,128)S(1)}, s32[16,2]{0,1:T(2,128)}, u32[]{:S(2)}) copy-start(s32[16,2]{0,1:T(2,128)} %param.16) | copy-start | bytes 388
  4.0 28.4 %copy-start.2 = (f32[6144]{0:T(1024)S(1)}, f32[6144]{0:T(1024)}, u32[]{:S(2)}) copy-start(f32[6144]{0:T(1024)} %param.14) | copy-start | bytes 73732
  4.8 27.7 %copy-start.4 = (bf16[6144,4]{0,1:T(4,128)(2,1)S(1)}, bf16[6144,4]{0,1:T(4,128)(2,1)}, u32[]{:S(2)}) copy-start(bf16[6144,4]{0,1:T(4,128)(2,1)} %param.15) | copy-start | bytes 147460
  4.8 14.6 %all-to-all-start = ((f32[8,4,7,128]{3,1,2,0:T(4,128)}), f32[8,4,7,128]{3,1,2,0:T(4,128)S(1)}, u32[]{:S(2)}, u32[]{:S(2)}) async-start(f32[8,4,7,128]{3,1,2,0:T(4,128)} %copy.70), calls=%async_computation | async-start | bytes 229376 | tf_op jit(solution)/shard_map/all_to_all | solution.py:121
  20.7 11.1 %all-to-all-start.1 = ((bf16[32,4,768]{2,1,0:T(4,128)(2,1)}), bf16[32,4,768]{2,1,0:T(4,128)(2,1)S(1)}, u32[]{:S(2)}, u32[]{:S(2)}) async-start(bf16[32,4,768]{2,1,0:T(4,128)(2,1)} %broadcast_in_dim.107), calls=%async_computation.1 | async-start | bytes 393216 | tf_op jit(solution)/shard_map/all_to_all | solution.py:133
  47.8 11.5 %all-to-all-start.2 = ((f32[2,32,768]{2,0,1:T(2,128)}), f32[2,32,768]{2,0,1:T(2,128)S(1)}, u32[]{:S(2)}, u32[]{:S(2)}) async-start(f32[2,32,768]{2,0,1:T(2,128)} %copy.78), calls=%async_computation.2 | async-start | bytes 393216 | tf_op jit(solution)/shard_map/all_to_all | solution.py:168

commit v14 on v10

--- a/solution.py
+++ b/solution.py
@@ -71,7 +71,7 @@
             pl.BlockSpec(select.shape, lambda f: (0, 0)),
         ],
         out_specs=pl.BlockSpec((n_cols * n_sel // CAP, CAP, out_width), lambda f: (0, 0, 0)),
-        out_shape=jax.ShapeDtypeStruct((n_cols * n_sel // CAP, CAP, out_width), jnp.bfloat16),
+        out_shape=jax.ShapeDtypeStruct((n_cols * n_sel // CAP, CAP, out_width), jnp.float32),
         scratch_shapes=[pltpu.VMEM((n_cols, n_rows, out_width), jnp.float32)],
         compiler_params=pltpu.CompilerParams(vmem_limit_bytes=48 * 1024 * 1024),
     )(rows, w_gate, w_up, w_down, select)
@@ -178,7 +178,7 @@
     select = jnp.transpose(select, (1, 0, 2)).reshape(CAP * n_grp, n_grp * rows_here)
     blocks = expert_ffn(normed_all, w_gate, w_up, w_down, 0, select, n_shard)
     arrived = lax.all_to_all(blocks, ("shard", "grp"), 0, 0, tiled=True)
-    arrived = arrived.astype(jnp.float32).reshape(n_shard, n_grp, CAP, out_width)
+    arrived = arrived.reshape(n_shard, n_grp, CAP, out_width)
     per_expert = jnp.sum(arrived, axis=0)
     own_ids = lax.dynamic_slice_in_dim(expert_ids, grp_id * rows_here, rows_here, 0)
     homes = slot_match(own_ids, jnp.arange(n_grp, dtype=jnp.int32) * local_experts, rows_here, 1)[:, 0]

time: 59.5 us -> 60.8 us (1.022)
  waiting for transfers between devices: 22.2 us -> 23.3 us
    all_to_all x1, waiting for transfers between devices: 7.15 us -> 8.23 us  [shards(): arrived = lax.all_to_all(blocks, ('shard', 'grp'), 0, 0, tiled=True)]
where the time goes in v14:
time: 60.8 us; the launch traced here: 60.3 us
  waiting for transfers between devices  23.3 us (38%)
  Pallas kernels  14.8 us (24%)
  starting transfers between devices  12.9 us (21%)
  local copies, waits for them, and re-layouts  3.86 us (6%)
  other arithmetic  3.28 us (5%)
  matrix products  1.32 us (2%)
  between operations  0.84 us (1%)
    pallas_call x1, Pallas kernels, expert_ffn(): pl.pallas_call(expert_kernel, grid=(hidden_units // tile,), in_specs=[pl....  14.8 us
    all_to_all x1, waiting for transfers between devices, shards(): lax.all_to_all(spread, ('grp', 'shard'), 0, 0, tiled=True)  8.46 us
    all_to_all x1, waiting for transfers between devices, shards(): arrived = lax.all_to_all(blocks, ('shard', 'grp'), 0, 0, tiled=True)  8.23 us
    all_to_all x1, starting transfers between devices, shards(): stats = lax.all_to_all(packed, 'shard', 0, 0, tiled=True)  7.38 us
    all_to_all x1, waiting for transfers between devices, shards(): stats = lax.all_to_all(packed, 'shard', 0, 0, tiled=True)  6.61 us
    all_to_all x1, starting transfers between devices, shards(): arrived = lax.all_to_all(blocks, ('shard', 'grp'), 0, 0, tiled=True)  2.95 us
    all_to_all x1, starting transfers between devices, shards(): lax.all_to_all(spread, ('grp', 'shard'), 0, 0, tiled=True)  2.58 us
  transfers between devices with their start and end apart: 3, of which 3 were waited for; matrix products, arithmetic and copies ran while one was open for 2% of the time, Pallas kernels for 0%

profile of v14, /device:TPU:0, one launch (start us, length us, event | category | flops | bytes accessed | tf_op | source)
XLA Modules:
  0.0 60.3 jit_solution(2960159504025362981)
XLA Ops:
  0.6 0.0 copy-start
  0.7 1.0 %reshape.258 = bf16[4,8,6,128]{3,2,1,0:T(8,128)(2,1)S(1)} reshape(bf16[4,6144]{1,0:T(4,128)(2,1)} %param.10) | data formatting | bytes 98304 | tf_op jit(solution)/shard_map/reshape | solution.py:100
  1.7 0.0 copy-start.1
  1.7 0.9 %broadcast_compare_fusion = pred[4,256]{1,0:T(4,128)(4,1)S(1)} fusion(s32[256]{0:T(256)S(1)} %iota_add_fusion, s32[4]{0:T(128)} %param.13), kind=kLoop, calls=%fused_computation.41 | loop fusion | flops 1024 | bytes 2064 | tf_op jit(solution)/shard_map/lt | solution.py:107
  2.6 0.0 copy-done
  2.6 0.7 %fusion.32 = (f32[4,8,6]{2,1,0:T(8,128)S(1)}, f32[4,8,6,256]{3,2,1,0:T(8,128)S(1)}) fusion(bf16[4,8,6,128]{3,2,1,0:T(8,128)(2,1)S(1)} %reshape.258, pred[4,256]{1,0:T(4,128)(4,1)S(1)} %broadcast_compare_fusion, bf16[4,256,1024]{2,1,0:T(8,128)(2,1)S(1)} %copy-done), kind=kOutput, calls=%fused_computation.55 | convolution fusion | flops 12730176 | bytes 2344704 | tf_op jit(solution)/shard_map/rgjd,rtgd->rgjt/dot_general | solution.py:103
  3.3 0.0 copy-start.3
  3.3 0.2 convert_reduce_fusion
  3.5 0.1 select_maximum_fusion
  3.6 0.0 copy-done.1
  3.6 0.4 fusion.18
  4.0 0.0 copy-start.2
  4.1 0.7 %copy.61 = f32[8,4,7,128]{3,1,2,0:T(4,128)} copy(f32[8,4,7,128]{3,2,0,1:T(8,128)S(1)} %maximum_bitcast_fusion) | data formatting | bytes 229376 | tf_op jit(solution)/shard_map/transpose | solution.py:133
  4.8 0.0 copy-start.4
  4.8 7.4 %all-to-all-start = ((f32[8,4,7,128]{3,1,2,0:T(4,128)}), f32[8,4,7,128]{3,1,2,0:T(4,128)S(1)}, u32[]{:S(2)}, u32[]{:S(2)}) async-start(f32[8,4,7,128]{3,1,2,0:T(4,128)} %copy.61), calls=%async_computation | async-start | bytes 229376 | tf_op jit(solution)/shard_map/all_to_all | solution.py:134
  12.2 0.0 copy-done.3
  12.2 0.1 and.47
  12.3 0.1 constant_dynamic-slice_fusion
  12.4 0.2 reduce_window_sum.22
  12.6 0.2 reduce_window_sum.23
  12.8 6.6 %all-to-all-done = f32[8,4,7,128]{3,1,2,0:T(4,128)S(1)} async-done(((f32[8,4,7,128]{3,1,2,0:T(4,128)}), f32[8,4,7,128]{3,1,2,0:T(4,128)S(1)}, u32[]{:S(2)}, u32[]{:S(2)}) %all-to-all-start) | async-done | bytes 114720 | tf_op jit(solution)/shard_map/all_to_all | solution.py:134
  19.5 0.1 fusion.23
  19.5 0.1 copy.64
  19.6 0.1 copy.63
  19.8 0.1 fusion.21
  19.9 0.1 fusion.25
  20.0 0.7 %broadcast_in_dim.107 = bf16[32,4,768]{2,1,0:T(4,128)(2,1)} broadcast(bf16[4,768]{1,0:T(4,128)(2,1)S(1)} %fusion.25), dimensions={1,2} | broadcast | bytes 202752 | tf_op jit(solution)/shard_map/broadcast_in_dim | solution.py:145
  20.7 2.6 %all-to-all-start.1 = ((bf16[32,4,768]{2,1,0:T(4,128)(2,1)}), bf16[32,4,768]{2,1,0:T(4,128)(2,1)S(1)}, u32[]{:S(2)}, u32[]{:S(2)}) async-start(bf16[32,4,768]{2,1,0:T(4,128)(2,1)} %broadcast_in_dim.107), calls=%async_computation.1 | async-start | bytes 393216 | tf_op jit(solution)/shard_map/all_to_all | solution.py:146
  23.3 0.1 iota_compare_fusion.1
  23.4 8.5 %all-to-all-done.1 = bf16[32,4,768]{2,1,0:T(4,128)(2,1)S(1)} async-done(((bf16[32,4,768]{2,1,0:T(4,128)(2,1)}), bf16[32,4,768]{2,1,0:T(4,128)(2,1)S(1)}, u32[]{:S(2)}, u32[]{:S(2)}) %all-to-all-start.1) | async-done | bytes 196640 | tf_op jit(solution)/shard_map/all_to_all | solution.py:146
  31.9 0.1 multiply_reduce_fusion
  32.0 0.1 copy.67
  32.1 0.1 rsqrt.12
  32.3 0.1 copy.72
  32.4 0.0 copy-done.2
  32.4 0.1 multiply_convert_fusion.x_ref
  32.5 0.0 copy-done.4
  32.5 0.2 fusion.33
  32.8 0.1 select_reduce_fusion.1
  32.9 14.8 %shard_map.113 = f32[32,2,768]{2,1,0:T(2,128)} custom-call(bf16[16,6144]{1,0:T(8,128)(2,1)S(1)} %multiply_convert_fusion.x_ref, bf16[1,6144,1024]{2,1,0:T(8,128)(2,1)} %gate_ref.1, bf16[1,6144,1024]{2,1,0:T(8,128)(2,1)} %up_ref.1, bf16[1,1024,6144]{2,1,0:T(8,128)(2,1)} %down_ref.1, f32[8,16]{1,0:T(8,128)S(1)} %bitcast.75), custom_call_target="tpu_custom_call" | custom-call | tf_op jit(solution)/shard_map/pallas_call | solution.py:63
  47.7 2.9 %all-to-all-start.2 = ((f32[32,2,768]{2,1,0:T(2,128)}), f32[32,2,768]{2,1,0:T(2,128)S(1)}, u32[]{:S(2)}, u32[]{:S(2)}) async-start(f32[32,2,768]{2,1,0:T(2,128)} %shard_map.113), calls=%async_computation.2 | async-start | bytes 393216 | tf_op jit(solution)/shard_map/all_to_all | solution.py:180
  50.6 0.7 %constant_dynamic-slice_fusion.1 = bf16[4,6144]{1,0:T(4,128)(2,1)} fusion(bf16[16,6144]{1,0:T(8,128)(2,1)S(1)} %multiply_convert_fusion.x_ref, s32[]{:T(128)S(6)} %select_n.31), kind=kLoop, calls=%fused_computation.50 | loop fusion | bytes 98308 | tf_op jit(solution)/shard_map/dynamic_slice | solution.py:152
  51.3 8.2 %all-to-all-done.2 = f32[32,2,768]{2,1,0:T(2,128)S(1)} async-done(((f32[32,2,768]{2,1,0:T(2,128)}), f32[32,2,768]{2,1,0:T(2,128)S(1)}, u32[]{:S(2)}, u32[]{:S(2)}) %all-to-all-start.2) | async-done | bytes 196640 | tf_op jit(solution)/shard_map/all_to_all | solution.py:180
  59.5 0.1 reduce_sum.99
  59.6 0.7 %select_reduce_fusion = bf16[4,768]{1,0:T(4,128)(2,1)} fusion(f32[4,2,768]{2,1,0:T(2,128)S(1)} %reduce_sum.99, pred[4,2,4]{2,1,0:T(4,128)(4,1)S(1)} %compare_and_fusion.1), kind=kLoop, calls=%fused_computation.19 | loop fusion | flops 46080 | bytes 30752 | tf_op jit(solution)/shard_map/reduce_sum | solution.py:186
  (20 shorter events, 0.3 us)
Async XLA Ops:
  0.6 1.9 %copy-start = (bf16[4,256,1024]{2,1,0:T(8,128)(2,1)S(1)}, bf16[4,256,1024]{2,1,0:T(8,128)(2,1)}, u32[]{:S(2)}) copy-start(bf16[4,256,1024]{2,1,0:T(8,128)(2,1)} %param.11) | copy-start | bytes 6291460
  1.7 1.9 %copy-start.1 = (bf16[4,256,1024]{2,1,0:T(8,128)(2,1)S(1)}, bf16[4,256,1024]{2,1,0:T(8,128)(2,1)}, u32[]{:S(2)}) copy-start(bf16[4,256,1024]{2,1,0:T(8,128)(2,1)} %param.12) | copy-start | bytes 6291460
  3.3 8.9 %copy-start.3 = (s32[16,2]{0,1:T(2,128)S(1)}, s32[16,2]{0,1:T(2,128)}, u32[]{:S(2)}) copy-start(s32[16,2]{0,1:T(2,128)} %param.16) | copy-start | bytes 388
  4.0 28.4 %copy-start.2 = (f32[6144]{0:T(1024)S(1)}, f32[6144]{0:T(1024)}, u32[]{:S(2)}) copy-start(f32[6144]{0:T(1024)} %param.14) | copy-start | bytes 73732
  4.8 27.7 %copy-start.4 = (bf16[6144,4]{0,1:T(4,128)(2,1)S(1)}, bf16[6144,4]{0,1:T(4,128)(2,1)}, u32[]{:S(2)}) copy-start(bf16[6144,4]{0,1:T(4,128)(2,1)} %param.15) | copy-start | bytes 147460
  4.8 14.6 %all-to-all-start = ((f32[8,4,7,128]{3,1,2,0:T(4,128)}), f32[8,4,7,128]{3,1,2,0:T(4,128)S(1)}, u32[]{:S(2)}, u32[]{:S(2)}) async-start(f32[8,4,7,128]{3,1,2,0:T(4,128)} %copy.61), calls=%async_computation | async-start | bytes 229376 | tf_op jit(solution)/shard_map/all_to_all | solution.py:134
  20.7 11.1 %all-to-all-start.1 = ((bf16[32,4,768]{2,1,0:T(4,128)(2,1)}), bf16[32,4,768]{2,1,0:T(4,128)(2,1)S(1)}, u32[]{:S(2)}, u32[]{:S(2)}) async-start(bf16[32,4,768]{2,1,0:T(4,128)(2,1)} %broadcast_in_dim.107), calls=%async_computation.1 | async-start | bytes 393216 | tf_op jit(solution)/shard_map/all_to_all | solution.py:146
  47.7 11.8 %all-to-all-start.2 = ((f32[32,2,768]{2,1,0:T(2,128)}), f32[32,2,768]{2,1,0:T(2,128)S(1)}, u32[]{:S(2)}, u32[]{:S(2)}) async-start(f32[32,2,768]{2,1,0:T(2,128)} %shard_map.113), calls=%async_computation.2 | async-start | bytes 393216 | tf_op jit(solution)/shard_map/all_to_all | solution.py:180

commit v15 on v7

--- a/solution.py
+++ b/solution.py
@@ -94,11 +94,10 @@
     live_mask = (position[None, :] < lengths[:, None])[:, None, None, :]
     scores = jnp.where(live_mask, scores, NEG_FILL)
     scores = scores.reshape(rows_here, KV_HEADS, kv_share, n_blocks, BLOCK)
-    live_blocks = live_mask.reshape(rows_here, 1, 1, n_blocks, BLOCK)
     block_max = jnp.max(scores, axis=-1)
-    block_probs = jnp.where(live_blocks, jnp.exp(scores - block_max[..., None]), 0.0).astype(
-        jnp.bfloat16
-    )
+    block_probs = jnp.where(
+        scores > 0.5 * NEG_FILL, jnp.exp(scores - block_max[..., None]), 0.0
+    ).astype(jnp.bfloat16)
     block_sum = jnp.sum(block_probs.astype(jnp.float32), axis=-1)
     block_mix = jnp.einsum(
         "rgjbt,rbtgd->rgjbd", block_probs, value_heads, preferred_element_type=jnp.float32

time: 59.5 us -> 59.5 us (level)
  no operation moved by 1% of the time
where the time goes in v15:
time: 59.5 us; the launch traced here: 59.1 us
  waiting for transfers between devices  22 us (37%)
  Pallas kernels  14 us (24%)
  starting transfers between devices  12.9 us (22%)
  local copies, waits for them, and re-layouts  4.67 us (8%)
  other arithmetic  3.36 us (6%)
  matrix products  1.33 us (2%)
  between operations  0.86 us (1%)
    pallas_call x1, Pallas kernels, expert_ffn(): pl.pallas_call(expert_kernel, grid=(hidden_units // tile,), in_specs=[pl....  14 us
    all_to_all x1, waiting for transfers between devices, shards(): lax.all_to_all(spread, ('grp', 'shard'), 0, 0, tiled=True)  8.46 us
    all_to_all x1, starting transfers between devices, shards(): stats = lax.all_to_all(packed, 'shard', 0, 0, tiled=True)  7.38 us
    all_to_all x1, waiting for transfers between devices, shards(): arrived = lax.all_to_all(blocks, ('grp', 'shard'), 1, 1, tiled=True)  6.9 us
    all_to_all x1, waiting for transfers between devices, shards(): stats = lax.all_to_all(packed, 'shard', 0, 0, tiled=True)  6.61 us
    all_to_all x1, starting transfers between devices, shards(): arrived = lax.all_to_all(blocks, ('grp', 'shard'), 1, 1, tiled=True)  2.95 us
    all_to_all x1, starting transfers between devices, shards(): lax.all_to_all(spread, ('grp', 'shard'), 0, 0, tiled=True)  2.58 us
  transfers between devices with their start and end apart: 3, of which 3 were waited for; matrix products, arithmetic and copies ran while one was open for 2% of the time, Pallas kernels for 0%

profile of v15, /device:TPU:0, one launch (start us, length us, event | category | flops | bytes accessed | tf_op | source)
XLA Modules:
  0.0 59.1 jit_solution(2466828438213076676)
XLA Ops:
  0.6 0.0 copy-start
  0.7 1.0 %reshape.242 = bf16[4,8,6,128]{3,2,1,0:T(8,128)(2,1)S(1)} reshape(bf16[4,6144]{1,0:T(4,128)(2,1)} %param.10) | data formatting | bytes 98304 | tf_op jit(solution)/shard_map/reshape | solution.py:87
  1.7 0.0 copy-start.3
  1.7 0.9 %broadcast_compare_fusion = pred[4,256]{1,0:T(4,128)(4,1)S(1)} fusion(s32[256]{0:T(256)S(1)} %iota_add_fusion, s32[4]{0:T(128)} %param.13), kind=kLoop, calls=%fused_computation.46 | loop fusion | flops 1024 | bytes 2064 | tf_op jit(solution)/shard_map/lt | solution.py:94
  2.6 0.0 copy-done
  2.6 0.7 %fusion.32 = (f32[4,8,6]{2,1,0:T(8,128)S(1)}, f32[4,8,6,256]{3,2,1,0:T(8,128)S(1)}) fusion(bf16[4,8,6,128]{3,2,1,0:T(8,128)(2,1)S(1)} %reshape.242, pred[4,256]{1,0:T(4,128)(4,1)S(1)} %broadcast_compare_fusion, bf16[4,256,1024]{2,1,0:T(8,128)(2,1)S(1)} %copy-done), kind=kOutput, calls=%fused_computation.59 | convolution fusion | flops 12730176 | bytes 2344704 | tf_op jit(solution)/shard_map/rgjd,rtgd->rgjt/dot_general | solution.py:90
  3.3 0.0 copy-start.2
  3.3 0.1 fusion.22
  3.4 0.2 convert_reduce_fusion
  3.6 0.1 select_maximum_fusion
  3.7 0.0 copy-done.3
  3.7 0.4 fusion.18
  4.1 0.0 copy-start.1
  4.2 0.7 %copy.70 = f32[8,4,7,128]{3,1,2,0:T(4,128)} copy(f32[8,4,7,128]{3,2,0,1:T(8,128)S(1)} %maximum_bitcast_fusion) | data formatting | bytes 229376 | tf_op jit(solution)/shard_map/transpose | solution.py:119
  4.9 0.0 copy-start.4
  4.9 7.4 %all-to-all-start = ((f32[8,4,7,128]{3,1,2,0:T(4,128)}), f32[8,4,7,128]{3,1,2,0:T(4,128)S(1)}, u32[]{:S(2)}, u32[]{:S(2)}) async-start(f32[8,4,7,128]{3,1,2,0:T(4,128)} %copy.70), calls=%async_computation | async-start | bytes 229376 | tf_op jit(solution)/shard_map/all_to_all | solution.py:120
  12.3 0.0 copy-done.2
  12.3 0.1 and.47
  12.4 0.1 constant_dynamic-slice_fusion
  12.5 0.2 reduce_window_sum.22
  12.7 0.2 reduce_window_sum.23
  12.9 6.6 %all-to-all-done = f32[8,4,7,128]{3,1,2,0:T(4,128)S(1)} async-done(((f32[8,4,7,128]{3,1,2,0:T(4,128)}), f32[8,4,7,128]{3,1,2,0:T(4,128)S(1)}, u32[]{:S(2)}, u32[]{:S(2)}) %all-to-all-start) | async-done | bytes 114720 | tf_op jit(solution)/shard_map/all_to_all | solution.py:120
  19.5 0.1 fusion.24
  19.6 0.1 copy.73
  19.7 0.1 copy.72
  19.9 0.1 fusion.21
  20.0 0.1 fusion.26
  20.1 0.7 %broadcast_in_dim.101 = bf16[32,4,768]{2,1,0:T(4,128)(2,1)} broadcast(bf16[4,768]{1,0:T(4,128)(2,1)S(1)} %fusion.26), dimensions={1,2} | broadcast | bytes 202752 | tf_op jit(solution)/shard_map/broadcast_in_dim | solution.py:131
  20.8 2.6 %all-to-all-start.1 = ((bf16[32,4,768]{2,1,0:T(4,128)(2,1)}), bf16[32,4,768]{2,1,0:T(4,128)(2,1)S(1)}, u32[]{:S(2)}, u32[]{:S(2)}) async-start(bf16[32,4,768]{2,1,0:T(4,128)(2,1)} %broadcast_in_dim.101), calls=%async_computation.1 | async-start | bytes 393216 | tf_op jit(solution)/shard_map/all_to_all | solution.py:132
  23.4 0.1 iota_compare_fusion.1
  23.5 8.5 %all-to-all-done.1 = bf16[32,4,768]{2,1,0:T(4,128)(2,1)S(1)} async-done(((bf16[32,4,768]{2,1,0:T(4,128)(2,1)}), bf16[32,4,768]{2,1,0:T(4,128)(2,1)S(1)}, u32[]{:S(2)}, u32[]{:S(2)}) %all-to-all-start.1) | async-done | bytes 196640 | tf_op jit(solution)/shard_map/all_to_all | solution.py:132
  31.9 0.1 multiply_reduce_fusion
  32.1 0.1 copy.76
  32.2 0.1 rsqrt.12
  32.3 0.1 copy.85
  32.5 0.0 copy-done.1
  32.5 0.1 multiply_convert_fusion.x_ref
  32.6 0.0 copy-done.4
  32.6 0.2 fusion.33
  32.9 0.1 select_reduce_fusion.1
  33.0 14.0 %shard_map.113 = bf16[8,6144]{1,0:T(8,128)(2,1)S(1)} custom-call(bf16[16,6144]{1,0:T(8,128)(2,1)S(1)} %multiply_convert_fusion.x_ref, bf16[1,6144,1024]{2,1,0:T(8,128)(2,1)} %gate_ref.1, bf16[1,6144,1024]{2,1,0:T(8,128)(2,1)} %up_ref.1, bf16[1,1024,6144]{2,1,0:T(8,128)(2,1)} %down_ref.1, f32[8,16]{1,0:T(8,128)S(1)} %bitcast.80), custom_call_target="tpu_custom_call" | custom-call | tf_op jit(solution)/shard_map/pallas_call | solution.py:50
  47.0 0.1 reshape.248
  47.1 0.7 %copy.78 = bf16[2,32,768]{2,0,1:T(2,128)(2,1)} copy(bf16[2,32,768]{2,1,0:T(8,128)(2,1)S(1)} %reshape.248) | data formatting | bytes 196608 | tf_op jit(solution)/shard_map/reshape | solution.py:166
  47.8 2.9 %all-to-all-start.2 = ((bf16[2,32,768]{2,0,1:T(2,128)(2,1)}), bf16[2,32,768]{2,0,1:T(2,128)(2,1)S(1)}, u32[]{:S(2)}, u32[]{:S(2)}) async-start(bf16[2,32,768]{2,0,1:T(2,128)(2,1)} %copy.78), calls=%async_computation.2 | async-start | bytes 196608 | tf_op jit(solution)/shard_map/all_to_all | solution.py:167
  50.8 0.7 %constant_dynamic-slice_fusion.1 = bf16[4,6144]{1,0:T(4,128)(2,1)} fusion(bf16[16,6144]{1,0:T(8,128)(2,1)S(1)} %multiply_convert_fusion.x_ref, s32[]{:T(128)S(6)} %select_n.31), kind=kLoop, calls=%fused_computation.55 | loop fusion | bytes 98308 | tf_op jit(solution)/shard_map/dynamic_slice | solution.py:138
  51.4 6.9 %all-to-all-done.2 = bf16[2,32,768]{2,0,1:T(2,128)(2,1)S(1)} async-done(((bf16[2,32,768]{2,0,1:T(2,128)(2,1)}), bf16[2,32,768]{2,0,1:T(2,128)(2,1)S(1)}, u32[]{:S(2)}, u32[]{:S(2)}) %all-to-all-start.2) | async-done | bytes 98336 | tf_op jit(solution)/shard_map/all_to_all | solution.py:167
  58.3 0.1 convert_reduce_fusion.1
  58.4 0.7 %select_reduce_fusion = bf16[4,768]{1,0:T(4,128)(2,1)} fusion(f32[4,2,768]{2,1,0:T(2,128)S(1)} %copy.80, pred[4,2,4]{2,1,0:T(4,128)(4,1)S(1)} %compare_and_fusion.1), kind=kLoop, calls=%fused_computation.22 | loop fusion | flops 46080 | bytes 30752 | tf_op jit(solution)/shard_map/reduce_sum | solution.py:173
  (22 shorter events, 0.3 us)
Async XLA Ops:
  0.6 1.9 %copy-start = (bf16[4,256,1024]{2,1,0:T(8,128)(2,1)S(1)}, bf16[4,256,1024]{2,1,0:T(8,128)(2,1)}, u32[]{:S(2)}) copy-start(bf16[4,256,1024]{2,1,0:T(8,128)(2,1)} %param.11) | copy-start | bytes 6291460
  1.7 2.0 %copy-start.3 = (bf16[4,256,1024]{2,1,0:T(8,128)(2,1)S(1)}, bf16[4,256,1024]{2,1,0:T(8,128)(2,1)}, u32[]{:S(2)}) copy-start(bf16[4,256,1024]{2,1,0:T(8,128)(2,1)} %param.12) | copy-start | bytes 6291460
  3.3 9.0 %copy-start.2 = (s32[16,2]{0,1:T(2,128)S(1)}, s32[16,2]{0,1:T(2,128)}, u32[]{:S(2)}) copy-start(s32[16,2]{0,1:T(2,128)} %param.16) | copy-start | bytes 388
  4.1 28.4 %copy-start.1 = (f32[6144]{0:T(1024)S(1)}, f32[6144]{0:T(1024)}, u32[]{:S(2)}) copy-start(f32[6144]{0:T(1024)} %param.14) | copy-start | bytes 73732
  4.9 27.7 %copy-start.4 = (bf16[6144,4]{0,1:T(4,128)(2,1)S(1)}, bf16[6144,4]{0,1:T(4,128)(2,1)}, u32[]{:S(2)}) copy-start(bf16[6144,4]{0,1:T(4,128)(2,1)} %param.15) | copy-start | bytes 147460
  4.9 14.6 %all-to-all-start = ((f32[8,4,7,128]{3,1,2,0:T(4,128)}), f32[8,4,7,128]{3,1,2,0:T(4,128)S(1)}, u32[]{:S(2)}, u32[]{:S(2)}) async-start(f32[8,4,7,128]{3,1,2,0:T(4,128)} %copy.70), calls=%async_computation | async-start | bytes 229376 | tf_op jit(solution)/shard_map/all_to_all | solution.py:120
  20.8 11.1 %all-to-all-start.1 = ((bf16[32,4,768]{2,1,0:T(4,128)(2,1)}), bf16[32,4,768]{2,1,0:T(4,128)(2,1)S(1)}, u32[]{:S(2)}, u32[]{:S(2)}) async-start(bf16[32,4,768]{2,1,0:T(4,128)(2,1)} %broadcast_in_dim.101), calls=%async_computation.1 | async-start | bytes 393216 | tf_op jit(solution)/shard_map/all_to_all | solution.py:132
  47.8 10.5 %all-to-all-start.2 = ((bf16[2,32,768]{2,0,1:T(2,128)(2,1)}), bf16[2,32,768]{2,0,1:T(2,128)(2,1)S(1)}, u32[]{:S(2)}, u32[]{:S(2)}) async-start(bf16[2,32,768]{2,0,1:T(2,128)(2,1)} %copy.78), calls=%async_computation.2 | async-start | bytes 196608 | tf_op jit(solution)/shard_map/all_to_all | solution.py:167

commit v16 on v7

--- a/solution.py
+++ b/solution.py
@@ -103,10 +103,15 @@
     block_mix = jnp.einsum(
         "rgjbt,rbtgd->rgjbd", block_probs, value_heads, preferred_element_type=jnp.float32
     )
-    dev_max = jnp.max(block_max, axis=-1)
-    dev_factor = jnp.exp(block_max - dev_max[..., None])
-    dev_sum = jnp.sum(block_sum * dev_factor, axis=-1).reshape(rows_here, HEADS)
-    dev_mix = jnp.sum(block_mix * dev_factor[..., None], axis=-2).reshape(rows_here, HEADS, HEAD_DIM)
+    if n_blocks == 1:
+        dev_max = block_max[..., 0]
+        dev_sum = block_sum[..., 0].reshape(rows_here, HEADS)
+        dev_mix = block_mix[..., 0, :].reshape(rows_here, HEADS, HEAD_DIM)
+    else:
+        dev_max = jnp.max(block_max, axis=-1)
+        dev_factor = jnp.exp(block_max - dev_max[..., None])
+        dev_sum = jnp.sum(block_sum * dev_factor, axis=-1).reshape(rows_here, HEADS)
+        dev_mix = jnp.sum(block_mix * dev_factor[..., None], axis=-2).reshape(rows_here, HEADS, HEAD_DIM)
     dev_max = dev_max.reshape(rows_here, HEADS)
 
     per_chunk = HEADS // n_shard

time: 59.5 us -> 59.4 us (level)
  no operation moved by 1% of the time
where the time goes in v16:
time: 59.4 us; the launch traced here: 59.1 us
  waiting for transfers between devices  22 us (37%)
  Pallas kernels  14 us (24%)
  starting transfers between devices  12.9 us (22%)
  local copies, waits for them, and re-layouts  4.66 us (8%)
  other arithmetic  3.3 us (6%)
  matrix products  1.33 us (2%)
  between operations  0.85 us (1%)
    pallas_call x1, Pallas kernels, expert_ffn(): pl.pallas_call(expert_kernel, grid=(hidden_units // tile,), in_specs=[pl....  14 us
    all_to_all x1, waiting for transfers between devices, shards(): lax.all_to_all(spread, ('grp', 'shard'), 0, 0, tiled=True)  8.46 us
    all_to_all x1, starting transfers between devices, shards(): stats = lax.all_to_all(packed, 'shard', 0, 0, tiled=True)  7.38 us
    all_to_all x1, waiting for transfers between devices, shards(): arrived = lax.all_to_all(blocks, ('grp', 'shard'), 1, 1, tiled=True)  6.9 us
    all_to_all x1, waiting for transfers between devices, shards(): stats = lax.all_to_all(packed, 'shard', 0, 0, tiled=True)  6.61 us
    all_to_all x1, starting transfers between devices, shards(): arrived = lax.all_to_all(blocks, ('grp', 'shard'), 1, 1, tiled=True)  2.95 us
    all_to_all x1, starting transfers between devices, shards(): lax.all_to_all(spread, ('grp', 'shard'), 0, 0, tiled=True)  2.58 us
  transfers between devices with their start and end apart: 3, of which 3 were waited for; matrix products, arithmetic and copies ran while one was open for 2% of the time, Pallas kernels for 0%

profile of v16, /device:TPU:0, one launch (start us, length us, event | category | flops | bytes accessed | tf_op | source)
XLA Modules:
  0.0 59.1 jit_solution(11824708682797822508)
XLA Ops:
  0.6 0.0 copy-start
  0.7 1.0 %reshape.244 = bf16[4,8,6,128]{3,2,1,0:T(8,128)(2,1)S(1)} reshape(bf16[4,6144]{1,0:T(4,128)(2,1)} %param.10) | data formatting | bytes 98304 | tf_op jit(solution)/shard_map/reshape | solution.py:87
  1.7 0.0 copy-start.1
  1.7 0.9 %broadcast_compare_fusion = pred[4,256]{1,0:T(4,128)(4,1)S(1)} fusion(s32[256]{0:T(256)S(1)} %iota_add_fusion, s32[4]{0:T(128)} %param.13), kind=kLoop, calls=%fused_computation.39 | loop fusion | flops 1024 | bytes 2064 | tf_op jit(solution)/shard_map/lt | solution.py:94
  2.6 0.0 copy-done
  2.6 0.7 %fusion.22 = (f32[4,8,6]{2,1,0:T(8,128)S(1)}, f32[4,8,6,256]{3,2,1,0:T(8,128)S(1)}) fusion(bf16[4,8,6,128]{3,2,1,0:T(8,128)(2,1)S(1)} %reshape.244, pred[4,256]{1,0:T(4,128)(4,1)S(1)} %broadcast_compare_fusion, bf16[4,256,1024]{2,1,0:T(8,128)(2,1)S(1)} %copy-done), kind=kOutput, calls=%fused_computation.52 | convolution fusion | flops 12730176 | bytes 2344704 | tf_op jit(solution)/shard_map/rgjd,rtgd->rgjt/dot_general | solution.py:90
  3.3 0.0 copy-start.3
  3.3 0.2 convert_reduce_fusion
  3.5 0.0 copy-done.1
  3.5 0.4 fusion
  4.0 0.0 copy-start.2
  4.0 0.1 select_maximum_fusion
  4.1 0.7 %copy.70 = f32[8,4,7,128]{3,1,2,0:T(4,128)} copy(f32[8,4,7,128]{3,2,0,1:T(8,128)S(1)} %maximum_bitcast_fusion) | data formatting | bytes 229376 | tf_op jit(solution)/shard_map/transpose | solution.py:125
  4.8 0.0 copy-start.4
  4.8 7.4 %all-to-all-start = ((f32[8,4,7,128]{3,1,2,0:T(4,128)}), f32[8,4,7,128]{3,1,2,0:T(4,128)S(1)}, u32[]{:S(2)}, u32[]{:S(2)}) async-start(f32[8,4,7,128]{3,1,2,0:T(4,128)} %copy.70), calls=%async_computation | async-start | bytes 229376 | tf_op jit(solution)/shard_map/all_to_all | solution.py:126
  12.2 0.0 copy-done.3
  12.2 0.1 and.47
  12.3 0.1 constant_dynamic-slice_fusion
  12.4 0.2 reduce_window_sum.22
  12.6 0.2 reduce_window_sum.23
  12.8 6.6 %all-to-all-done = f32[8,4,7,128]{3,1,2,0:T(4,128)S(1)} async-done(((f32[8,4,7,128]{3,1,2,0:T(4,128)}), f32[8,4,7,128]{3,1,2,0:T(4,128)S(1)}, u32[]{:S(2)}, u32[]{:S(2)}) %all-to-all-start) | async-done | bytes 114720 | tf_op jit(solution)/shard_map/all_to_all | solution.py:126
  19.4 0.1 fusion.14
  19.5 0.1 copy.73
  19.6 0.1 copy.72
  19.8 0.1 fusion.12
  19.9 0.1 fusion.16
  20.0 0.7 %broadcast_in_dim.105 = bf16[32,4,768]{2,1,0:T(4,128)(2,1)} broadcast(bf16[4,768]{1,0:T(4,128)(2,1)S(1)} %fusion.16), dimensions={1,2} | broadcast | bytes 202752 | tf_op jit(solution)/shard_map/broadcast_in_dim | solution.py:137
  20.7 2.6 %all-to-all-start.1 = ((bf16[32,4,768]{2,1,0:T(4,128)(2,1)}), bf16[32,4,768]{2,1,0:T(4,128)(2,1)S(1)}, u32[]{:S(2)}, u32[]{:S(2)}) async-start(bf16[32,4,768]{2,1,0:T(4,128)(2,1)} %broadcast_in_dim.105), calls=%async_computation.1 | async-start | bytes 393216 | tf_op jit(solution)/shard_map/all_to_all | solution.py:138
  23.3 0.1 iota_compare_fusion.1
  23.4 8.5 %all-to-all-done.1 = bf16[32,4,768]{2,1,0:T(4,128)(2,1)S(1)} async-done(((bf16[32,4,768]{2,1,0:T(4,128)(2,1)}), bf16[32,4,768]{2,1,0:T(4,128)(2,1)S(1)}, u32[]{:S(2)}, u32[]{:S(2)}) %all-to-all-start.1) | async-done | bytes 196640 | tf_op jit(solution)/shard_map/all_to_all | solution.py:138
  31.8 0.1 multiply_reduce_fusion
  32.0 0.1 copy.76
  32.1 0.1 rsqrt.12
  32.3 0.1 copy.85
  32.4 0.0 copy-done.2
  32.4 0.1 multiply_convert_fusion.x_ref
  32.5 0.0 copy-done.4
  32.5 0.2 fusion.23
  32.8 0.1 select_reduce_fusion.1
  32.9 14.0 %shard_map.113 = bf16[8,6144]{1,0:T(8,128)(2,1)S(1)} custom-call(bf16[16,6144]{1,0:T(8,128)(2,1)S(1)} %multiply_convert_fusion.x_ref, bf16[1,6144,1024]{2,1,0:T(8,128)(2,1)} %gate_ref.1, bf16[1,6144,1024]{2,1,0:T(8,128)(2,1)} %up_ref.1, bf16[1,1024,6144]{2,1,0:T(8,128)(2,1)} %down_ref.1, f32[8,16]{1,0:T(8,128)S(1)} %bitcast.62), custom_call_target="tpu_custom_call" | custom-call | tf_op jit(solution)/shard_map/pallas_call | solution.py:50
  46.9 0.1 reshape.250
  47.0 0.7 %copy.78 = bf16[2,32,768]{2,0,1:T(2,128)(2,1)} copy(bf16[2,32,768]{2,1,0:T(8,128)(2,1)S(1)} %reshape.250) | data formatting | bytes 196608 | tf_op jit(solution)/shard_map/reshape | solution.py:172
  47.7 2.9 %all-to-all-start.2 = ((bf16[2,32,768]{2,0,1:T(2,128)(2,1)}), bf16[2,32,768]{2,0,1:T(2,128)(2,1)S(1)}, u32[]{:S(2)}, u32[]{:S(2)}) async-start(bf16[2,32,768]{2,0,1:T(2,128)(2,1)} %copy.78), calls=%async_computation.2 | async-start | bytes 196608 | tf_op jit(solution)/shard_map/all_to_all | solution.py:173
  50.7 0.7 %constant_dynamic-slice_fusion.1 = bf16[4,6144]{1,0:T(4,128)(2,1)} fusion(bf16[16,6144]{1,0:T(8,128)(2,1)S(1)} %multiply_convert_fusion.x_ref, s32[]{:T(128)S(6)} %select_n.31), kind=kLoop, calls=%fused_computation.48 | loop fusion | bytes 98308 | tf_op jit(solution)/shard_map/dynamic_slice | solution.py:144
  51.3 6.9 %all-to-all-done.2 = bf16[2,32,768]{2,0,1:T(2,128)(2,1)S(1)} async-done(((bf16[2,32,768]{2,0,1:T(2,128)(2,1)}), bf16[2,32,768]{2,0,1:T(2,128)(2,1)S(1)}, u32[]{:S(2)}, u32[]{:S(2)}) %all-to-all-start.2) | async-done | bytes 98336 | tf_op jit(solution)/shard_map/all_to_all | solution.py:173
  58.2 0.1 convert_reduce_fusion.1
  58.4 0.7 %select_reduce_fusion = bf16[4,768]{1,0:T(4,128)(2,1)} fusion(f32[4,2,768]{2,1,0:T(2,128)S(1)} %copy.80, pred[4,2,4]{2,1,0:T(4,128)(4,1)S(1)} %compare_and_fusion.1), kind=kLoop, calls=%fused_computation.17 | loop fusion | flops 46080 | bytes 30752 | tf_op jit(solution)/shard_map/reduce_sum | solution.py:179
  (21 shorter events, 0.3 us)
Async XLA Ops:
  0.6 1.9 %copy-start = (bf16[4,256,1024]{2,1,0:T(8,128)(2,1)S(1)}, bf16[4,256,1024]{2,1,0:T(8,128)(2,1)}, u32[]{:S(2)}) copy-start(bf16[4,256,1024]{2,1,0:T(8,128)(2,1)} %param.11) | copy-start | bytes 6291460
  1.7 1.8 %copy-start.1 = (bf16[4,256,1024]{2,1,0:T(8,128)(2,1)S(1)}, bf16[4,256,1024]{2,1,0:T(8,128)(2,1)}, u32[]{:S(2)}) copy-start(bf16[4,256,1024]{2,1,0:T(8,128)(2,1)} %param.12) | copy-start | bytes 6291460
  3.3 8.9 %copy-start.3 = (s32[16,2]{0,1:T(2,128)S(1)}, s32[16,2]{0,1:T(2,128)}, u32[]{:S(2)}) copy-start(s32[16,2]{0,1:T(2,128)} %param.16) | copy-start | bytes 388
  4.0 28.4 %copy-start.2 = (f32[6144]{0:T(1024)S(1)}, f32[6144]{0:T(1024)}, u32[]{:S(2)}) copy-start(f32[6144]{0:T(1024)} %param.14) | copy-start | bytes 73732
  4.8 27.7 %copy-start.4 = (bf16[6144,4]{0,1:T(4,128)(2,1)S(1)}, bf16[6144,4]{0,1:T(4,128)(2,1)}, u32[]{:S(2)}) copy-start(bf16[6144,4]{0,1:T(4,128)(2,1)} %param.15) | copy-start | bytes 147460
  4.8 14.6 %all-to-all-start = ((f32[8,4,7,128]{3,1,2,0:T(4,128)}), f32[8,4,7,128]{3,1,2,0:T(4,128)S(1)}, u32[]{:S(2)}, u32[]{:S(2)}) async-start(f32[8,4,7,128]{3,1,2,0:T(4,128)} %copy.70), calls=%async_computation | async-start | bytes 229376 | tf_op jit(solution)/shard_map/all_to_all | solution.py:126
  20.7 11.1 %all-to-all-start.1 = ((bf16[32,4,768]{2,1,0:T(4,128)(2,1)}), bf16[32,4,768]{2,1,0:T(4,128)(2,1)S(1)}, u32[]{:S(2)}, u32[]{:S(2)}) async-start(bf16[32,4,768]{2,1,0:T(4,128)(2,1)} %broadcast_in_dim.105), calls=%async_computation.1 | async-start | bytes 393216 | tf_op jit(solution)/shard_map/all_to_all | solution.py:138
  47.7 10.5 %all-to-all-start.2 = ((bf16[2,32,768]{2,0,1:T(2,128)(2,1)}), bf16[2,32,768]{2,0,1:T(2,128)(2,1)S(1)}, u32[]{:S(2)}, u32[]{:S(2)}) async-start(bf16[2,32,768]{2,0,1:T(2,128)(2,1)} %copy.78), calls=%async_computation.2 | async-start | bytes 196608 | tf_op jit(solution)/shard_map/all_to_all | solution.py:173

commit v17 on v7

--- a/solution.py
+++ b/solution.py
@@ -151,13 +151,12 @@
     width = normed_all.shape[1]
     out_width = width // n_shard
     expert_index = grp_id
-    coefficient = jnp.sum(jnp.where(expert_ids == expert_index, route_weight, 0.0), axis=-1)
     sending = slot_match(expert_ids, expert_index[None], rows_here, n_grp)[0]
     row_of = jnp.arange(n_grp * rows_here, dtype=jnp.int32).reshape(n_grp, 1, rows_here)
     select = jnp.sum(
         jnp.where(
             sending[..., None] & (row_of[..., None] == jnp.arange(n_grp * rows_here)[None, None, None, :]),
-            coefficient[None, None, None, :],
+            1.0,
             0.0,
         ),
         axis=2,
@@ -170,7 +169,18 @@
     per_expert = jnp.transpose(jnp.sum(arrived, axis=2), (1, 0, 2))
     own_ids = lax.dynamic_slice_in_dim(expert_ids, grp_id * rows_here, rows_here, 0)
     homes = slot_match(own_ids, jnp.arange(n_grp, dtype=jnp.int32) * local_experts, rows_here, 1)[:, 0]
-    spread_back = jnp.where(homes[..., None], per_expert[:, :, None, :], 0.0)
+    own_weight = lax.dynamic_slice_in_dim(route_weight, grp_id * rows_here, rows_here, 0)
+    expert_weight = jnp.sum(
+        jnp.where(
+            own_ids[None, :, :] == (jnp.arange(n_grp, dtype=jnp.int32) * local_experts)[:, None, None],
+            own_weight[None, :, :],
+            0.0,
+        ),
+        axis=-1,
+    )
+    spread_back = jnp.where(
+        homes[..., None], per_expert[:, :, None, :] * expert_weight[:, None, :, None], 0.0
+    )
     result = jnp.sum(spread_back, axis=(0, 1))
     return (normed, result.astype(jnp.bfloat16))
 

time: 59.5 us -> 60 us (level)
  transfers between devices with their start and end apart: 3 -> 3, of which waited for: 3 -> 3; matrix products, arithmetic and copies ran while one was open for 2% -> 1% of each run, Pallas kernels for 0% -> 0%
where the time goes in v17:
time: 60 us; the launch traced here: 59.6 us
  waiting for transfers between devices  22.4 us (37%)
  Pallas kernels  14 us (23%)
  starting transfers between devices  12.9 us (22%)
  local copies, waits for them, and re-layouts  4.75 us (8%)
  other arithmetic  3.29 us (5%)
  matrix products  1.32 us (2%)
  between operations  0.86 us (1%)
    pallas_call x1, Pallas kernels, expert_ffn(): pl.pallas_call(expert_kernel, grid=(hidden_units // tile,), in_specs=[pl....  14 us
    all_to_all x1, waiting for transfers between devices, shards(): lax.all_to_all(spread, ('grp', 'shard'), 0, 0, tiled=True)  8.52 us
    all_to_all x1, waiting for transfers between devices, shards(): arrived = lax.all_to_all(blocks, ('grp', 'shard'), 1, 1, tiled=True)  7.45 us
    all_to_all x1, starting transfers between devices, shards(): stats = lax.all_to_all(packed, 'shard', 0, 0, tiled=True)  7.38 us
    all_to_all x1, waiting for transfers between devices, shards(): stats = lax.all_to_all(packed, 'shard', 0, 0, tiled=True)  6.45 us
    all_to_all x1, starting transfers between devices, shards(): arrived = lax.all_to_all(blocks, ('grp', 'shard'), 1, 1, tiled=True)  2.95 us
    all_to_all x1, starting transfers between devices, shards(): lax.all_to_all(spread, ('grp', 'shard'), 0, 0, tiled=True)  2.58 us
  transfers between devices with their start and end apart: 3, of which 3 were waited for; matrix products, arithmetic and copies ran while one was open for 1% of the time, Pallas kernels for 0%

profile of v17, /device:TPU:0, one launch (start us, length us, event | category | flops | bytes accessed | tf_op | source)
XLA Modules:
  0.0 59.6 jit_solution(386369845640004077)
XLA Ops:
  0.6 0.0 copy-start
  0.7 1.0 %reshape.266 = bf16[4,8,6,128]{3,2,1,0:T(8,128)(2,1)S(1)} reshape(bf16[4,6144]{1,0:T(4,128)(2,1)} %param.10) | data formatting | bytes 98304 | tf_op jit(solution)/shard_map/reshape | solution.py:87
  1.7 0.0 copy-start.1
  1.7 0.9 %broadcast_compare_fusion = pred[4,256]{1,0:T(4,128)(4,1)S(1)} fusion(s32[256]{0:T(256)S(1)} %iota_add_fusion, s32[4]{0:T(128)} %param.13), kind=kLoop, calls=%fused_computation.45 | loop fusion | flops 1024 | bytes 2064 | tf_op jit(solution)/shard_map/lt | solution.py:94
  2.6 0.0 copy-done
  2.6 0.7 %fusion.30 = (f32[4,8,6]{2,1,0:T(8,128)S(1)}, f32[4,8,6,256]{3,2,1,0:T(8,128)S(1)}) fusion(bf16[4,8,6,128]{3,2,1,0:T(8,128)(2,1)S(1)} %reshape.266, pred[4,256]{1,0:T(4,128)(4,1)S(1)} %broadcast_compare_fusion, bf16[4,256,1024]{2,1,0:T(8,128)(2,1)S(1)} %copy-done), kind=kOutput, calls=%fused_computation.58 | convolution fusion | flops 12730176 | bytes 2344704 | tf_op jit(solution)/shard_map/rgjd,rtgd->rgjt/dot_general | solution.py:90
  3.3 0.0 copy-start.3
  3.3 0.2 convert_reduce_fusion
  3.5 0.1 select_maximum_fusion
  3.6 0.0 copy-done.1
  3.6 0.4 fusion.18
  4.0 0.0 copy-start.2
  4.1 0.7 %copy.78 = f32[8,4,7,128]{3,1,2,0:T(4,128)} copy(f32[8,4,7,128]{3,2,0,1:T(8,128)S(1)} %maximum_bitcast_fusion) | data formatting | bytes 229376 | tf_op jit(solution)/shard_map/transpose | solution.py:120
  4.8 0.0 copy-start.4
  4.8 7.4 %all-to-all-start = ((f32[8,4,7,128]{3,1,2,0:T(4,128)}), f32[8,4,7,128]{3,1,2,0:T(4,128)S(1)}, u32[]{:S(2)}, u32[]{:S(2)}) async-start(f32[8,4,7,128]{3,1,2,0:T(4,128)} %copy.78), calls=%async_computation | async-start | bytes 229376 | tf_op jit(solution)/shard_map/all_to_all | solution.py:121
  12.2 0.0 copy-done.3
  12.2 0.1 and.47
  12.3 0.1 constant_dynamic-slice_fusion.1
  12.4 0.2 reduce_window_sum.23
  12.6 0.1 iota_compare_fusion.1
  12.7 0.2 reduce_window_sum.22
  12.9 0.1 select_reduce_fusion.1
  13.0 6.4 %all-to-all-done = f32[8,4,7,128]{3,1,2,0:T(4,128)S(1)} async-done(((f32[8,4,7,128]{3,1,2,0:T(4,128)}), f32[8,4,7,128]{3,1,2,0:T(4,128)S(1)}, u32[]{:S(2)}, u32[]{:S(2)}) %all-to-all-start) | async-done | bytes 114720 | tf_op jit(solution)/shard_map/all_to_all | solution.py:121
  19.5 0.1 fusion.23
  19.5 0.1 copy.81
  19.6 0.1 copy.80
  19.8 0.1 fusion.21
  19.9 0.1 fusion.25
  20.0 0.7 %broadcast_in_dim.70 = bf16[32,4,768]{2,1,0:T(4,128)(2,1)} broadcast(bf16[4,768]{1,0:T(4,128)(2,1)S(1)} %fusion.25), dimensions={1,2} | broadcast | bytes 202752 | tf_op jit(solution)/shard_map/broadcast_in_dim | solution.py:132
  20.7 2.6 %all-to-all-start.1 = ((bf16[32,4,768]{2,1,0:T(4,128)(2,1)}), bf16[32,4,768]{2,1,0:T(4,128)(2,1)S(1)}, u32[]{:S(2)}, u32[]{:S(2)}) async-start(bf16[32,4,768]{2,1,0:T(4,128)(2,1)} %broadcast_in_dim.70), calls=%async_computation.1 | async-start | bytes 393216 | tf_op jit(solution)/shard_map/all_to_all | solution.py:133
  23.3 8.5 %all-to-all-done.1 = bf16[32,4,768]{2,1,0:T(4,128)(2,1)S(1)} async-done(((bf16[32,4,768]{2,1,0:T(4,128)(2,1)}), bf16[32,4,768]{2,1,0:T(4,128)(2,1)S(1)}, u32[]{:S(2)}, u32[]{:S(2)}) %all-to-all-start.1) | async-done | bytes 196640 | tf_op jit(solution)/shard_map/all_to_all | solution.py:133
  31.9 0.1 multiply_reduce_fusion
  32.0 0.1 copy.84
  32.1 0.1 rsqrt.12
  32.3 0.1 copy.93
  32.4 0.0 copy-done.2
  32.4 0.1 multiply_convert_fusion.x_ref
  32.5 0.7 %constant_dynamic-slice_fusion.2 = bf16[4,6144]{1,0:T(4,128)(2,1)} fusion(bf16[16,6144]{1,0:T(8,128)(2,1)S(1)} %multiply_convert_fusion.x_ref, s32[]{:T(128)S(6)} %select_n.32), kind=kLoop, calls=%fused_computation.53 | loop fusion | bytes 98308 | tf_op jit(solution)/shard_map/dynamic_slice | solution.py:139
  33.2 0.0 copy-done.4
  33.2 0.2 fusion.31
  33.4 14.0 %shard_map.113 = bf16[8,6144]{1,0:T(8,128)(2,1)S(1)} custom-call(bf16[16,6144]{1,0:T(8,128)(2,1)S(1)} %multiply_convert_fusion.x_ref, bf16[1,6144,1024]{2,1,0:T(8,128)(2,1)} %gate_ref.1, bf16[1,6144,1024]{2,1,0:T(8,128)(2,1)} %up_ref.1, bf16[1,1024,6144]{2,1,0:T(8,128)(2,1)} %down_ref.1, f32[8,16]{1,0:T(8,128)S(1)} %bitcast.80), custom_call_target="tpu_custom_call" | custom-call | tf_op jit(solution)/shard_map/pallas_call | solution.py:50
  47.4 0.1 reshape.272
  47.5 0.7 %copy.86 = bf16[2,32,768]{2,0,1:T(2,128)(2,1)} copy(bf16[2,32,768]{2,1,0:T(8,128)(2,1)S(1)} %reshape.272) | data formatting | bytes 196608 | tf_op jit(solution)/shard_map/reshape | solution.py:166
  48.2 2.9 %all-to-all-start.2 = ((bf16[2,32,768]{2,0,1:T(2,128)(2,1)}), bf16[2,32,768]{2,0,1:T(2,128)(2,1)S(1)}, u32[]{:S(2)}, u32[]{:S(2)}) async-start(bf16[2,32,768]{2,0,1:T(2,128)(2,1)} %copy.86), calls=%async_computation.2 | async-start | bytes 196608 | tf_op jit(solution)/shard_map/all_to_all | solution.py:167
  51.2 0.1 constant_dynamic-slice_fusion
  51.3 7.5 %all-to-all-done.2 = bf16[2,32,768]{2,0,1:T(2,128)(2,1)S(1)} async-done(((bf16[2,32,768]{2,0,1:T(2,128)(2,1)}), bf16[2,32,768]{2,0,1:T(2,128)(2,1)S(1)}, u32[]{:S(2)}, u32[]{:S(2)}) %all-to-all-start.2) | async-done | bytes 98336 | tf_op jit(solution)/shard_map/all_to_all | solution.py:167
  58.8 0.1 convert_reduce_fusion.1
  58.9 0.7 %select_reduce_fusion = bf16[4,768]{1,0:T(4,128)(2,1)} fusion(f32[4,4]{1,0:T(4,128)S(1)} %select_reduce_fusion.2, f32[4,2,768]{2,1,0:T(2,128)S(1)} %copy.88, pred[4,2,4]{2,1,0:T(4,128)(4,1)S(1)} %compare_and_fusion.1), kind=kLoop, calls=%fused_computation.20 | loop fusion | flops 70656 | bytes 30816 | tf_op jit(solution)/shard_map/reduce_sum | solution.py:184
  (23 shorter events, 0.3 us)
Async XLA Ops:
  0.6 1.9 %copy-start = (bf16[4,256,1024]{2,1,0:T(8,128)(2,1)S(1)}, bf16[4,256,1024]{2,1,0:T(8,128)(2,1)}, u32[]{:S(2)}) copy-start(bf16[4,256,1024]{2,1,0:T(8,128)(2,1)} %param.11) | copy-start | bytes 6291460
  1.7 1.9 %copy-start.1 = (bf16[4,256,1024]{2,1,0:T(8,128)(2,1)S(1)}, bf16[4,256,1024]{2,1,0:T(8,128)(2,1)}, u32[]{:S(2)}) copy-start(bf16[4,256,1024]{2,1,0:T(8,128)(2,1)} %param.12) | copy-start | bytes 6291460
  3.3 8.9 %copy-start.3 = (s32[16,2]{0,1:T(2,128)S(1)}, s32[16,2]{0,1:T(2,128)}, u32[]{:S(2)}) copy-start(s32[16,2]{0,1:T(2,128)} %param.16) | copy-start | bytes 388
  4.0 28.4 %copy-start.2 = (f32[6144]{0:T(1024)S(1)}, f32[6144]{0:T(1024)}, u32[]{:S(2)}) copy-start(f32[6144]{0:T(1024)} %param.14) | copy-start | bytes 73732
  4.8 28.4 %copy-start.4 = (bf16[6144,4]{0,1:T(4,128)(2,1)S(1)}, bf16[6144,4]{0,1:T(4,128)(2,1)}, u32[]{:S(2)}) copy-start(bf16[6144,4]{0,1:T(4,128)(2,1)} %param.15) | copy-start | bytes 147460
  4.8 14.6 %all-to-all-start = ((f32[8,4,7,128]{3,1,2,0:T(4,128)}), f32[8,4,7,128]{3,1,2,0:T(4,128)S(1)}, u32[]{:S(2)}, u32[]{:S(2)}) async-start(f32[8,4,7,128]{3,1,2,0:T(4,128)} %copy.78), calls=%async_computation | async-start | bytes 229376 | tf_op jit(solution)/shard_map/all_to_all | solution.py:121
  20.7 11.1 %all-to-all-start.1 = ((bf16[32,4,768]{2,1,0:T(4,128)(2,1)}), bf16[32,4,768]{2,1,0:T(4,128)(2,1)S(1)}, u32[]{:S(2)}, u32[]{:S(2)}) async-start(bf16[32,4,768]{2,1,0:T(4,128)(2,1)} %broadcast_in_dim.70), calls=%async_computation.1 | async-start | bytes 393216 | tf_op jit(solution)/shard_map/all_to_all | solution.py:133
  48.2 10.5 %all-to-all-start.2 = ((bf16[2,32,768]{2,0,1:T(2,128)(2,1)}), bf16[2,32,768]{2,0,1:T(2,128)(2,1)S(1)}, u32[]{:S(2)}, u32[]{:S(2)}) async-start(bf16[2,32,768]{2,0,1:T(2,128)(2,1)} %copy.86), calls=%async_computation.2 | async-start | bytes 196608 | tf_op jit(solution)/shard_map/all_to_all | solution.py:167
